TPU v7x, 256 devices: a whole 4x4x8 slice. The times are simulated.
256 devices in a mesh: sec: 2 (over y_lo), dp: 8 (over x, y_hi), seq: 16 (over z, core).
Axes of the slice: x: 4, y: 4 (y_hi: 2, y_lo: 2; y = y_hi * 2 + y_lo), z: 8, core: 2. Of those that a mesh axis runs over, the one named last changes fastest.
Arguments:
- hidden: bfloat16 [256, 128, 2560], P(('sec', 'dp', 'seq')), may hold values from -24 to 24
- cond_shift: bfloat16 [256, 2560], P(('sec', 'dp', 'seq')), may hold values from -0.3125 to 0.3125
- cond_scale: bfloat16 [256, 2560], P(('sec', 'dp', 'seq')), may hold values from -1.75 to 1.75
- noisy: bfloat16 [256, 128, 256], P(('sec', 'dp', 'seq')), may hold values from -6 to 6
- noise_level: float32 [256], P(('sec', 'dp', 'seq')), may hold values from 0.2 to 1
- w_out: bfloat16 [2560, 256], replicated, may hold values from -0.125 to 0.125
- w_embed: bfloat16 [256, 2048], replicated, may hold values from -0.375 to 0.375
- w_root: bfloat16 [2, 2048], replicated, may hold values from -0.03125 to 0.03125
- w_qkv: bfloat16 [3, 2048, 2048], P(None, None, 'seq'), may hold values from -0.125 to 0.125
- w_proj: bfloat16 [2048, 512], P('seq'), may hold values from -0.125 to 0.125
- text_table: bfloat16 [49408, 512], P('seq'), may hold values from -6 to 6
- text_ids: int32 [32, 32], replicated, may hold values from 0 to 49407
- prompt_index: int32 [256], P(('sec', 'dp')), may hold values from 0 to 31
- reward_weight: float32 [256], P(('sec', 'dp')), may hold values from 1000 to 4000
Outputs:
- rewards: float32 [256], P(('sec', 'dp'))
- grad_w_out: float32 [2560, 256], P('seq')
- grad_hidden: bfloat16 [256, 128, 2560], P(('sec', 'dp', 'seq'))
All inputs are finite; a program needn't handle non-finite values.
Results may differ from a plain program's by a relative error of at most 0.017.
The roundings to bfloat16 on the way count: a program that leaves them out, or rounds other values in their place, can miss the bound.
Values may be sent and summed in bfloat16 or wider, within the bound.
No kernel may reach another device: no remote copies, remote signals or barrier semaphores. Data moves between devices by JAX's collectives and lax.ppermute only.
A program may use at most 128 MiB of HBM per device.

v0:
```python
import jax
import jax.numpy as jnp
from jax import lax
from jax.sharding import PartitionSpec as P

D_REW = 2048
HEADS = 16
PROMPTS = 32


normalizing_sharpness = 10.0
epsilon = 1e-06
highest = lax.Precision.HIGHEST


def rotate(angle, first, second):
    cosine = jnp.cos(angle)
    sine_term = jnp.sin(angle)
    return (cosine * first + sine_term * second, cosine * second - sine_term * first)


def suffix(values):
    return jnp.sum(values, axis=1, keepdims=True) - jnp.cumsum(values, axis=1)


def local_path(motion):
    spin = motion[..., 0]
    theta = jnp.cumsum(spin, axis=1) - spin
    step_east, step_north = rotate(theta, motion[..., 1], motion[..., 2])
    path_east = jnp.cumsum(step_east, axis=1) - step_east
    path_north = jnp.cumsum(step_north, axis=1) - step_north
    return (theta, path_east, path_north)


def embed(motion, root_east, root_north, w_embed, root_rows):
    emb = jnp.einsum(
        "cfe,ed->cfd", motion.astype(jnp.bfloat16), w_embed, preferred_element_type=jnp.float32
    )
    emb = emb + root_east[..., None] * root_rows[0] + root_north[..., None] * root_rows[1]
    scale_rms = jnp.sqrt(jnp.mean(emb * emb, axis=-1, keepdims=True) + epsilon)
    return (emb / scale_rms, scale_rms)


def unit_rows(vectors):
    length = jnp.sqrt(jnp.sum(vectors * vectors, axis=-1, keepdims=True) + epsilon)
    return (vectors / length, length)


def norm_grad(grad, normed, scale_rms):
    return (grad - normed * jnp.mean(grad * normed, axis=-1, keepdims=True)) / scale_rms


def motion_grad(d_emb, normed_e, scale_rms, motion, theta, embed_rows, root_rows):
    d_unemb = norm_grad(d_emb, normed_e, scale_rms)
    d_embedded = jnp.einsum("cfd,ed->cfe", d_unemb, embed_rows, precision=highest)
    grad_east = suffix(jnp.sum(d_unemb * root_rows[0], axis=-1))
    grad_north = suffix(jnp.sum(d_unemb * root_rows[1], axis=-1))
    vel_east = motion[..., 1]
    vel_north = motion[..., 2]
    d_east, d_north = rotate(-theta, grad_east, grad_north)
    cosine = jnp.cos(theta)
    sine_term = jnp.sin(theta)
    d_theta = grad_east * (cosine * vel_north - sine_term * vel_east) - grad_north * (
        cosine * vel_east + sine_term * vel_north
    )
    d_spin = suffix(d_theta)
    return d_embedded.at[..., 0].add(d_spin).at[..., 1].add(d_east).at[..., 2].add(d_north)


def local(
    hidden,
    cond_shift,
    cond_scale,
    noisy,
    noise_level,
    w_out,
    w_embed,
    w_root,
    w_qkv,
    w_proj,
    text_table,
    text_ids,
    prompt_index,
    reward_weight,
):
    clips_dev = hidden.shape[0]
    ways = lax.axis_size("seq")
    group = clips_dev * ways
    frames = hidden.shape[1]
    width_cols = w_qkv.shape[2]
    head_size = D_REW // HEADS
    heads_dev = width_cols // head_size
    root_rows = w_root.astype(jnp.float32)
    embed_rows = w_embed.astype(jnp.float32)
    vocab_rows = text_table.shape[0]
    local_ids = text_ids - lax.axis_index("seq") * vocab_rows
    inside = (local_ids >= 0) & (local_ids < vocab_rows)
    picked = jnp.take(text_table, jnp.clip(local_ids, 0, vocab_rows - 1), axis=0).astype(
        jnp.float32
    )
    text_part = jnp.sum(jnp.where(inside[..., None], picked, 0.0), axis=1)
    text_raw = lax.psum(text_part, "seq")
    text_unit, text_len = unit_rows(text_raw)
    hidden_f = hidden.astype(jnp.float32)
    centred = hidden_f - jnp.mean(hidden_f, axis=-1, keepdims=True)
    inv_std = lax.rsqrt(jnp.mean(centred * centred, axis=-1, keepdims=True) + epsilon)
    normed_h = centred * inv_std
    gain = 1.0 + cond_scale.astype(jnp.float32)[:, None, :]
    modulated = (normed_h * gain + cond_shift.astype(jnp.float32)[:, None, :]).astype(jnp.bfloat16)
    eps_pred = jnp.einsum("cfd,de->cfe", modulated, w_out, preferred_element_type=jnp.float32)
    level = noise_level[:, None, None]
    x_clean = noisy.astype(jnp.float32) - level * eps_pred
    theta, path_east, path_north = local_path(x_clean)
    normed_e, scale_rms = embed(x_clean, path_east, path_north, w_embed, root_rows)
    projected = jnp.einsum(
        "cfd,jdk->cfjk",
        lax.all_gather(normed_e.astype(jnp.bfloat16), "seq", axis=0, tiled=True),
        w_qkv,
        preferred_element_type=jnp.float32,
    )
    projected = projected.reshape(group, frames, 3, heads_dev, head_size)
    query_unit, query_len = unit_rows(projected[:, :, 0])
    key_unit, key_len = unit_rows(projected[:, :, 1])
    asking_vectors_group = query_unit.astype(jnp.bfloat16)
    lookup_vectors_group = key_unit.astype(jnp.bfloat16)
    value_b = projected[:, :, 2].astype(jnp.bfloat16)
    similarity_table = normalizing_sharpness * jnp.einsum(
        "cfhd,cghd->chfg",
        asking_vectors_group,
        lookup_vectors_group,
        preferred_element_type=jnp.float32,
    )
    expo = jnp.exp(similarity_table)
    focus_probabilities = expo / jnp.sum(expo, axis=-1, keepdims=True)
    attention_b = focus_probabilities.astype(jnp.bfloat16)
    column_mass = jnp.sum(attention_b, axis=2, dtype=jnp.float32)
    value_f = value_b.astype(jnp.float32)
    pooled = jnp.einsum("chg,cghd->chd", column_mass, value_f, precision=highest)
    pooled_b = pooled.astype(jnp.bfloat16).reshape(group, width_cols)
    motion_part = jnp.dot(pooled_b, w_proj, preferred_element_type=jnp.float32)
    motion_emb = lax.psum(motion_part, "seq")
    choose = (prompt_index[:, None] == jnp.arange(PROMPTS)[None, :]).astype(jnp.float32)
    target = jnp.dot(choose, text_unit, precision=highest)
    emb_len = jnp.sqrt(jnp.sum(motion_emb * motion_emb, axis=-1) + epsilon)
    rewards = jnp.sum(motion_emb * target, axis=-1) / emb_len
    d_memb = (
        (-reward_weight)[:, None]
        * (target - rewards[:, None] * motion_emb / emb_len[:, None])
        / emb_len[:, None]
    )
    d_pooled = jnp.dot(d_memb, w_proj.astype(jnp.float32).T, precision=highest).reshape(
        group, heads_dev, head_size
    )
    reduction_dimension = jnp.einsum("chd,cghd->chg", d_pooled, value_f, precision=highest)
    d_value = jnp.transpose(column_mass, (0, 2, 1))[..., None] * d_pooled[:, None]
    pairwise_dot_similarity = jnp.sum(
        focus_probabilities * reduction_dimension[:, :, None, :], axis=-1, keepdims=True
    )
    similarity_derivative = (
        normalizing_sharpness
        * focus_probabilities
        * (reduction_dimension[:, :, None, :] - pairwise_dot_similarity)
    ).astype(jnp.bfloat16)
    d_qu = jnp.einsum(
        "chfg,cghd->cfhd",
        similarity_derivative,
        lookup_vectors_group,
        preferred_element_type=jnp.float32,
    )
    d_ku = jnp.einsum(
        "chfg,cfhd->cghd",
        similarity_derivative,
        asking_vectors_group,
        preferred_element_type=jnp.float32,
    )
    d_query = (d_qu - query_unit * jnp.sum(query_unit * d_qu, axis=-1, keepdims=True)) / query_len
    d_key = (d_ku - key_unit * jnp.sum(key_unit * d_ku, axis=-1, keepdims=True)) / key_len
    d_proj = (
        jnp.stack([d_query, d_key, d_value], axis=2)
        .astype(jnp.bfloat16)
        .reshape(group, frames, 3, width_cols)
    )
    d_emb = lax.psum_scatter(
        jnp.einsum("cfjk,jdk->cfd", d_proj, w_qkv, preferred_element_type=jnp.float32),
        "seq",
        scatter_dimension=0,
        tiled=True,
    )
    d_motion = motion_grad(d_emb, normed_e, scale_rms, x_clean, theta, embed_rows, root_rows)
    d_eps_b = (-level * d_motion).astype(jnp.bfloat16)
    d_mod = jnp.einsum("cfe,de->cfd", d_eps_b, w_out, preferred_element_type=jnp.float32)
    d_norm = d_mod * gain
    grad_hidden = (
        inv_std
        * (
            d_norm
            - jnp.mean(d_norm, axis=-1, keepdims=True)
            - normed_h * jnp.mean(d_norm * normed_h, axis=-1, keepdims=True)
        )
    ).astype(jnp.bfloat16)
    rows_dev = w_out.shape[0] // ways
    grad_term = jnp.einsum("cfd,cfe->de", modulated, d_eps_b, preferred_element_type=jnp.float32)
    grad_total = lax.psum(grad_term, ("sec", "dp", "seq"))
    grad_w_out = lax.dynamic_slice_in_dim(grad_total, lax.axis_index("seq") * rows_dev, rows_dev, 0)
    return (rewards, grad_w_out, grad_hidden)


def solution(mesh):
    placed = (
        P(("sec", "dp", "seq"), None, None),
        P(("sec", "dp", "seq"), None),
        P(("sec", "dp", "seq"), None),
        P(("sec", "dp", "seq"), None, None),
        P(("sec", "dp", "seq")),
        P(),
        P(),
        P(),
        P(None, None, "seq"),
        P("seq", None),
        P("seq", None),
        P(),
        P(("sec", "dp")),
        P(("sec", "dp")),
    )
    return jax.shard_map(
        local,
        mesh=mesh,
        in_specs=placed,
        out_specs=(P(("sec", "dp")), P("seq", None), P(("sec", "dp", "seq"), None, None)),
        check_vma=False,
    )
```

profile of v0, /device:TPU:6, one launch (start us, length us, event | category | flops | bytes accessed | tf_op | source)
XLA Modules:
  0.0 640.2 jit_solution(5430359469314224564)
XLA Ops:
  9.1 5.1 gather_fusion
  14.2 2.3 select_reduce_fusion
  17.3 1.3 convert_reduce_fusion
  18.5 1.4 fusion.22
  20.7 1.8 fusion.24
  26.0 1.7 multiply_reduce_fusion.3
  30.3 88.0 %all-reduce.3.cloned.1.call-done = f32[32,512]{1,0:T(8,128)} async-done(((f32[32,512]{1,0:T(8,128)}), f32[32,512]{1,0:T(8,128)}) %all-reduce.3.cloned.1.call-update) | async-done | bytes 65552 | tf_op jit(solution)/shard_map/psum | solution.py:102
  118.3 1.0 multiply_reduce_fusion.8
  119.8 55.7 %all-gather.3.cloned.1.call-done = bf16[2048,2048]{1,0:T(8,128)(2,1)} async-done(((bf16[128,2048]{1,0:T(8,128)(2,1)}), bf16[2048,2048]{1,0:T(8,128)(2,1)}) %all-gather.3.cloned.1.call-update) | async-done | bytes 8388624 | tf_op jit(solution)/shard_map/all_gather | solution.py:117
  175.5 6.4 convolution_bitcast_fusion.1
  182.1 1.6 fusion.32
  183.8 2.7 convert_reduce_fusion.1
  186.5 2.1 fusion.37
  188.8 47.4 %psum.21 = f32[16,512]{1,0:T(8,128)} all-reduce(f32[16,512]{1,0:T(8,128)S(1)} %fusion.59), channel_id=1, replica_groups=mesh['sec'=2,'dp'=8,'seq'=16] {'seq'}, use_global_device_ids=true, to_apply=%region_10.11 | all-reduce | flops 8192 | bytes 65536 | tf_op jit(solution)/shard_map/psum | solution.py:141
  236.2 1.2 multiply_reduce_fusion.9
  237.4 1.0 fusion.45
  238.8 1.7 fusion.35
  241.5 1.0 copy-done.2
  244.8 8.1 %convolution_bitcast_fusion = f32[16,128,2048]{2,1,0:T(8,128)} fusion(bf16[16,128,1,128]{1,3,0,2:T(8,128)(2,1)S(1)} %multiply_convert_fusion, bf16[16,128,1,128]{1,3,0,2:T(8,128)(2,1)S(1)} %get-tuple-element.60, bf16[16,128,1,128]{1,3,0,2:T(8,128)(2,1)S(1)} %get-tuple-element.59, bf16[3,2048,128]{2,1,0:T(8,128)(2,1)S(1)} %copy-done.9), kind=kOutput, calls=%fused_computation.2 | convolution fusion | flops 3222798336 | bytes 19922944 | tf_op jit(solution)/shard_map/cfjk,jdk->cfd/dot_general | solution.py:184
  253.2 100.2 %reduce-scatter.2.cloned.1.call-done = f32[1,128,2048]{2,1,0:T(8,128)} async-done(((f32[16,128,2048]{2,1,0:T(8,128)}), f32[1,128,2048]{2,1,0:T(8,128)}) %reduce-scatter.2.cloned.1.call-update) | async-done | bytes 1048592 | tf_op jit(solution)/shard_map/reduce_scatter | solution.py:183
  353.4 1.9 fusion.30
  355.6 2.1 multiply_reduce_fusion.7
  358.4 2.0 fusion.66
  360.8 2.7 fusion.27
  363.5 1.3 fusion.40
  364.9 1.0 scatter-add.10
  367.2 3.3 fusion.53
  371.1 3.2 fusion.18
  374.3 1.5 reduce_sum.224
  375.8 2.8 fusion.21
  378.6 253.5 %all-reduce.5.cloned.1.call-done = f32[2560,256]{1,0:T(8,128)} async-done(((f32[2560,256]{1,0:T(8,128)}), f32[2560,256]{1,0:T(8,128)}) %all-reduce.5.cloned.1.call-update) | async-done | bytes 2621456 | tf_op jit(solution)/shard_map/psum | solution.py:203
  632.1 1.6 constant_dynamic-slice_fusion
  (126 shorter events, 16.8 us)
Async XLA Ops:
  7.2 1.9 copy-start
  7.2 111.1 %all-reduce.3.cloned.1.call-start = ((), (), s32[]{:S(2)}) async-start(), calls=%async_computation.1 | async-start | bytes 131072 | tf_op jit(solution)/shard_map/psum | solution.py:102
  14.1 5.8 copy-start.20
  14.1 6.4 %copy-start.21 = (bf16[1,2560]{1,0:T(2,128)(2,1)S(1)}, bf16[1,2560]{1,0:T(2,128)(2,1)}, u32[]{:S(2)}) copy-start(bf16[1,2560]{1,0:T(2,128)(2,1)} %param.21) | copy-start | bytes 15364
  14.1 6.4 %copy-start.22 = (bf16[1,2560]{1,0:T(2,128)(2,1)S(1)}, bf16[1,2560]{1,0:T(2,128)(2,1)}, u32[]{:S(2)}) copy-start(bf16[1,2560]{1,0:T(2,128)(2,1)} %param.22) | copy-start | bytes 15364
  14.2 6.5 %copy-start.36 = (bf16[1,128,256]{2,1,0:T(8,128)(2,1)S(1)}, bf16[1,128,256]{2,1,0:T(8,128)(2,1)}, u32[]{:S(2)}) copy-start(bf16[1,128,256]{2,1,0:T(8,128)(2,1)} %param.23) | copy-start | bytes 196612
  16.5 159.0 %all-gather.3.cloned.1.call-start = ((), (), s32[]{:S(2)}) async-start(), calls=%async_computation.4 | async-start | bytes 8912896 | tf_op jit(solution)/shard_map/all_gather | solution.py:117
  16.5 4.1 copy-start.3
  18.5 3.9 copy-start.23
  20.0 2.5 copy-start.27
  20.7 1.8 copy-start.14
  24.9 2.8 copy-start.10
  27.8 2.0 copy-start.37
  29.7 323.7 %reduce-scatter.2.cloned.1.call-start = ((), (), s32[]{:S(2)}) async-start(), calls=%async_computation.2 | async-start | bytes 17825792 | tf_op jit(solution)/shard_map/reduce_scatter | solution.py:183
  181.8 2.0 copy-start.1
  183.8 4.8 copy-start.13
  183.8 52.3 %copy-start.16 = (f32[32,512]{1,0:T(8,128)S(1)}, f32[32,512]{1,0:T(8,128)}, u32[]{:S(2)}) copy-start(f32[32,512]{1,0:T(8,128)} %all-reduce.3.cloned.1.call-done) | copy-start | bytes 196612
  236.2 4.4 copy-start.6
  237.4 3.5 copy-start.35
  238.4 2.5 copy-start.8
  240.5 1.9 copy-start.2
  252.9 100.5 %copy-start.26 = (f32[128]{0:T(128)S(1)}, f32[128]{0:T(128)}, u32[]{:S(2)}) copy-start(f32[128]{0:T(128)} %copy-done.25) | copy-start | bytes 1540
  252.9 102.5 %copy-start.19 = (f32[1,2048]{1,0:T(1,128)S(1)}, f32[1,2048]{1,0:T(1,128)}, u32[]{:S(2)}) copy-start(f32[1,2048]{1,0:T(1,128)} %get-tuple-element.67) | copy-start | bytes 24580
  252.9 102.5 %copy-start.18 = (f32[1,2048]{1,0:T(1,128)S(1)}, f32[1,2048]{1,0:T(1,128)}, u32[]{:S(2)}) copy-start(f32[1,2048]{1,0:T(1,128)} %get-tuple-element.66) | copy-start | bytes 24580
  253.0 379.2 %all-reduce.5.cloned.1.call-start = ((), (), s32[]{:S(2)}) async-start(), calls=%async_computation.3 | async-start | bytes 5242880 | tf_op jit(solution)/shard_map/psum | solution.py:203
  353.4 2.0 copy-start.5
  353.4 2.2 copy-start.7
  355.6 2.7 copy-start.29
  355.6 2.7 copy-start.30
  355.6 2.7 copy-start.32
  355.6 2.7 copy-start.34
  355.6 5.0 copy-start.11
  (10 other events, 10.1 us)
Sparse Core Ops, SparseCore 0:
  16.6 101.6 all-reduce.2
  120.8 54.6 all-gather.2
  253.1 100.3 reduce-scatter.1
  370.6 261.4 all-reduce.4
where the time goes:
time: 641 us; the launch traced here: 640 us
  waiting for transfers between devices  497 us (78%)
  blocking collectives  47.4 us (7%)
  matrix products  37.3 us (6%)
  other arithmetic  26.9 us (4%)
  local copies, waits for them, and re-layouts  15.9 us (2%)
  between operations  14.9 us (2%)
    psum x1, waiting for transfers between devices, local(): grad_total = lax.psum(grad_term, ('sec', 'dp', 'seq'))  253 us
    reduce_scatter x1, waiting for transfers between devices, local(): lax.psum_scatter(jnp.einsum('cfjk,jdk->cfd', d_proj, w_qkv, preferred_ele...  100 us
    psum x1, waiting for transfers between devices, local(): text_raw = lax.psum(text_part, 'seq')  88 us
    all_gather x1, waiting for transfers between devices, local(): lax.all_gather(normed_e.astype(jnp.bfloat16), 'seq', axis=0, tiled=True)  55.7 us
    psum x1, blocking collectives, local(): motion_emb = lax.psum(motion_part, 'seq')  47.4 us
  transfers between devices with their start and end apart: 4, of which 4 were waited for; matrix products, arithmetic and copies ran while one was open for 3% of the time, Pallas kernels for 0%

commit v1 on v0

--- a/solution.py
+++ b/solution.py
@@ -85,22 +85,28 @@
 ):
     clips_dev = hidden.shape[0]
     ways = lax.axis_size("seq")
-    group = clips_dev * ways
-    frames = hidden.shape[1]
-    width_cols = w_qkv.shape[2]
+    me = lax.axis_index("seq")
     head_size = D_REW // HEADS
-    heads_dev = width_cols // head_size
     root_rows = w_root.astype(jnp.float32)
     embed_rows = w_embed.astype(jnp.float32)
+
     vocab_rows = text_table.shape[0]
-    local_ids = text_ids - lax.axis_index("seq") * vocab_rows
+    local_ids = text_ids - me * vocab_rows
     inside = (local_ids >= 0) & (local_ids < vocab_rows)
     picked = jnp.take(text_table, jnp.clip(local_ids, 0, vocab_rows - 1), axis=0).astype(
         jnp.float32
     )
     text_part = jnp.sum(jnp.where(inside[..., None], picked, 0.0), axis=1)
-    text_raw = lax.psum(text_part, "seq")
+    proj_dev = w_proj.shape[0]
+    proj_text = lax.all_gather(
+        jnp.concatenate([w_proj.astype(jnp.float32), text_part], axis=0), "seq", axis=0
+    )
+    proj_rows = proj_text[:, :proj_dev].reshape(ways * proj_dev, w_proj.shape[1])
+    text_raw = jnp.sum(proj_text[:, proj_dev:], axis=0)
     text_unit, text_len = unit_rows(text_raw)
+
+    w_all = lax.all_gather(w_qkv, "seq", axis=0)
+
     hidden_f = hidden.astype(jnp.float32)
     centred = hidden_f - jnp.mean(hidden_f, axis=-1, keepdims=True)
     inv_std = lax.rsqrt(jnp.mean(centred * centred, axis=-1, keepdims=True) + epsilon)
@@ -113,17 +119,16 @@
     theta, path_east, path_north = local_path(x_clean)
     normed_e, scale_rms = embed(x_clean, path_east, path_north, w_embed, root_rows)
     projected = jnp.einsum(
-        "cfd,jdk->cfjk",
-        lax.all_gather(normed_e.astype(jnp.bfloat16), "seq", axis=0, tiled=True),
-        w_qkv,
-        preferred_element_type=jnp.float32,
-    )
-    projected = projected.reshape(group, frames, 3, heads_dev, head_size)
-    query_unit, query_len = unit_rows(projected[:, :, 0])
-    key_unit, key_len = unit_rows(projected[:, :, 1])
+        "cfd,hjdk->cfhjk",
+        normed_e.astype(jnp.bfloat16),
+        w_all,
+        preferred_element_type=jnp.float32,
+    )
+    query_unit, query_len = unit_rows(projected[:, :, :, 0])
+    key_unit, key_len = unit_rows(projected[:, :, :, 1])
     asking_vectors_group = query_unit.astype(jnp.bfloat16)
     lookup_vectors_group = key_unit.astype(jnp.bfloat16)
-    value_b = projected[:, :, 2].astype(jnp.bfloat16)
+    value_b = projected[:, :, :, 2].astype(jnp.bfloat16)
     similarity_table = normalizing_sharpness * jnp.einsum(
         "cfhd,cghd->chfg",
         asking_vectors_group,
@@ -136,20 +141,23 @@
     column_mass = jnp.sum(attention_b, axis=2, dtype=jnp.float32)
     value_f = value_b.astype(jnp.float32)
     pooled = jnp.einsum("chg,cghd->chd", column_mass, value_f, precision=highest)
-    pooled_b = pooled.astype(jnp.bfloat16).reshape(group, width_cols)
-    motion_part = jnp.dot(pooled_b, w_proj, preferred_element_type=jnp.float32)
-    motion_emb = lax.psum(motion_part, "seq")
-    choose = (prompt_index[:, None] == jnp.arange(PROMPTS)[None, :]).astype(jnp.float32)
+    pooled_b = pooled.astype(jnp.bfloat16).reshape(clips_dev, D_REW)
+    motion_emb = jnp.dot(
+        pooled_b, proj_rows.astype(jnp.bfloat16), preferred_element_type=jnp.float32
+    )
+    prompts = lax.dynamic_slice_in_dim(prompt_index, me * clips_dev, clips_dev)
+    weights = lax.dynamic_slice_in_dim(reward_weight, me * clips_dev, clips_dev)
+    choose = (prompts[:, None] == jnp.arange(PROMPTS)[None, :]).astype(jnp.float32)
     target = jnp.dot(choose, text_unit, precision=highest)
     emb_len = jnp.sqrt(jnp.sum(motion_emb * motion_emb, axis=-1) + epsilon)
     rewards = jnp.sum(motion_emb * target, axis=-1) / emb_len
     d_memb = (
-        (-reward_weight)[:, None]
+        (-weights)[:, None]
         * (target - rewards[:, None] * motion_emb / emb_len[:, None])
         / emb_len[:, None]
     )
-    d_pooled = jnp.dot(d_memb, w_proj.astype(jnp.float32).T, precision=highest).reshape(
-        group, heads_dev, head_size
+    d_pooled = jnp.dot(d_memb, proj_rows.T, precision=highest).reshape(
+        clips_dev, HEADS, head_size
     )
     reduction_dimension = jnp.einsum("chd,cghd->chg", d_pooled, value_f, precision=highest)
     d_value = jnp.transpose(column_mass, (0, 2, 1))[..., None] * d_pooled[:, None]
@@ -175,17 +183,8 @@
     )
     d_query = (d_qu - query_unit * jnp.sum(query_unit * d_qu, axis=-1, keepdims=True)) / query_len
     d_key = (d_ku - key_unit * jnp.sum(key_unit * d_ku, axis=-1, keepdims=True)) / key_len
-    d_proj = (
-        jnp.stack([d_query, d_key, d_value], axis=2)
-        .astype(jnp.bfloat16)
-        .reshape(group, frames, 3, width_cols)
-    )
-    d_emb = lax.psum_scatter(
-        jnp.einsum("cfjk,jdk->cfd", d_proj, w_qkv, preferred_element_type=jnp.float32),
-        "seq",
-        scatter_dimension=0,
-        tiled=True,
-    )
+    d_proj = jnp.stack([d_query, d_key, d_value], axis=3).astype(jnp.bfloat16)
+    d_emb = jnp.einsum("cfhjk,hjdk->cfd", d_proj, w_all, preferred_element_type=jnp.float32)
     d_motion = motion_grad(d_emb, normed_e, scale_rms, x_clean, theta, embed_rows, root_rows)
     d_eps_b = (-level * d_motion).astype(jnp.bfloat16)
     d_mod = jnp.einsum("cfe,de->cfd", d_eps_b, w_out, preferred_element_type=jnp.float32)
@@ -198,11 +197,34 @@
             - normed_h * jnp.mean(d_norm * normed_h, axis=-1, keepdims=True)
         )
     ).astype(jnp.bfloat16)
+    grad_term = jnp.einsum("cfd,cfe->de", modulated, d_eps_b, preferred_element_type=jnp.float32)
+
     rows_dev = w_out.shape[0] // ways
-    grad_term = jnp.einsum("cfd,cfe->de", modulated, d_eps_b, preferred_element_type=jnp.float32)
-    grad_total = lax.psum(grad_term, ("sec", "dp", "seq"))
-    grad_w_out = lax.dynamic_slice_in_dim(grad_total, lax.axis_index("seq") * rows_dev, rows_dev, 0)
-    return (rewards, grad_w_out, grad_hidden)
+    cols = grad_term.shape[1]
+    n_dp = lax.axis_size("dp")
+    total_clips = clips_dev * ways * n_dp * lax.axis_size("sec")
+    extra = -(-total_clips // cols)
+    extra = -(-extra // 8) * 8
+    first_clip = (
+        (lax.axis_index("sec") * n_dp + lax.axis_index("dp")) * ways + me
+    ) * clips_dev
+    columns = jnp.arange(extra * cols)
+    slots = columns[None, :] == (first_clip + jnp.arange(clips_dev))[:, None]
+    reward_rows = jnp.sum(jnp.where(slots, rewards[:, None], 0.0), axis=0).reshape(extra, cols)
+    stacked = jnp.concatenate(
+        [
+            grad_term.reshape(ways, rows_dev, cols),
+            jnp.broadcast_to(reward_rows[None], (ways, extra, cols)),
+        ],
+        axis=1,
+    ).reshape(ways * (rows_dev + extra), cols)
+    block = lax.psum_scatter(stacked, "seq", scatter_dimension=0, tiled=True)
+    block = lax.psum(block, ("sec", "dp"))
+    grad_w_out = block[:rows_dev]
+    group_first = (lax.axis_index("sec") * n_dp + lax.axis_index("dp")) * ways * clips_dev
+    all_rewards = block[rows_dev:].reshape(extra * cols)
+    rewards_out = lax.dynamic_slice_in_dim(all_rewards, group_first, ways * clips_dev)
+    return (rewards_out, grad_w_out, grad_hidden)
 
 
 def solution(mesh):

time: 641 us -> 446 us (0.70)
  waiting for transfers between devices: 497 us -> 317 us
  blocking collectives: 47.4 us -> 0 us
  matrix products: 37.3 us -> 58.2 us
  other arithmetic: 26.9 us -> 34.6 us
    psum x2 -> x1, waiting for transfers between devices: 341 us -> 93.9 us  [local(): block = lax.psum(block, ('sec', 'dp'))]
    all_gather x1 -> x2, waiting for transfers between devices: 55.7 us -> 163 us  [the longest x1 133 us: local(): w_all = lax.all_gather(w_qkv, 'seq', axis=0)]
    psum x1 -> x0, blocking collectives: 47.4 us -> none  [local(): motion_emb = lax.psum(motion_part, 'seq')]
    reduce_scatter x1, waiting for transfers between devices: 100 us -> 59 us  [local(): block = lax.psum_scatter(stacked, 'seq', scatter_dimension=0, tiled=True)]
    dot_general x4, matrix products: 15.6 us -> 38.5 us  [the longest x1 16 us: local(): jnp.einsum('cfd,hjdk->cfhjk', normed_e.astype(jnp.bfloat16), w_all, prefe...]
where the time goes in v1:
time: 446 us; the launch traced here: 443 us
  waiting for transfers between devices  317 us (71%)
  matrix products  58.2 us (13%)
  other arithmetic  34.6 us (8%)
  between operations  16.9 us (4%)
  local copies, waits for them, and re-layouts  16.6 us (4%)
    all_gather x1, waiting for transfers between devices, local(): w_all = lax.all_gather(w_qkv, 'seq', axis=0)  133 us
    psum x1, waiting for transfers between devices, local(): block = lax.psum(block, ('sec', 'dp'))  93.9 us
    reduce_scatter x1, waiting for transfers between devices, local(): block = lax.psum_scatter(stacked, 'seq', scatter_dimension=0, tiled=True)  59 us
    all_gather x1, waiting for transfers between devices, local(): lax.all_gather(jnp.concatenate([w_proj.astype(jnp.float32), text_part], a...  30.1 us
    dot_general x1, matrix products, local(): jnp.einsum('cfd,hjdk->cfhjk', normed_e.astype(jnp.bfloat16), w_all, prefe...  16 us
    dot_general x1, matrix products, local(): jnp.einsum('cfhjk,hjdk->cfd', d_proj, w_all, preferred_element_type=jnp.f...  14.5 us
  transfers between devices with their start and end apart: 4, of which 4 were waited for; matrix products, arithmetic and copies ran while one was open for 3% of the time, Pallas kernels for 0%

profile of v1, /device:TPU:6, one launch (start us, length us, event | category | flops | bytes accessed | tf_op | source)
XLA Modules:
  0.0 443.4 jit_solution(8635623600535376236)
XLA Ops:
  9.1 5.1 %gather_fusion = bf16[1024,512]{1,0:T(8,128)(2,1)} fusion(bf16[3088,512]{1,0:T(8,128)(2,1)S(1)} %copy-done, s32[1024]{0:T(1024)S(1)} %broadcast_clamp_fusion), kind=kCustom, calls=%fused_computation | custom fusion | bytes 2101248 | tf_op jit(solution)/shard_map/jit(_take)/gather | solution.py:96
  14.2 1.6 select_reduce_fusion
  20.1 1.3 convert_reduce_fusion
  21.4 1.4 fusion.19
  22.8 2.0 fusion.21
  30.1 2.8 multiply_reduce_fusion.4
  33.0 30.1 %all-gather.7.cloned.1.call-done = f32[2560,512]{1,0:T(8,128)} async-done(((f32[160,512]{1,0:T(8,128)}), f32[2560,512]{1,0:T(8,128)}) %all-gather.7.cloned.1.call-update) | async-done | bytes 5242896 | tf_op jit(solution)/shard_map/all_gather | solution.py:101
  63.0 1.3 slice_reduce_fusion
  65.3 133.1 %all-gather.5.cloned.1.call-done = bf16[48,2048,128]{2,1,0:T(8,128)(2,1)} async-done(((bf16[3,2048,128]{2,1,0:T(8,128)(2,1)}), bf16[48,2048,128]{2,1,0:T(8,128)(2,1)}) %all-gather.5.cloned.1.call-update) | async-done | bytes 25165840 | tf_op jit(solution)/shard_map/all_gather | solution.py:108
  198.4 16.0 %convolution_bitcast_fusion.1 = f32[1,128,16,3,128]{1,4,3,2,0:T(8,128)} fusion(bf16[16,3,2048,128]{3,2,1,0:T(8,128)(2,1)} %bitcast.182, f32[128,2048]{1,0:T(8,128)} %get-tuple-element.74, f32[128]{0:T(128)S(1)} %add_sqrt_fusion.3), kind=kOutput, calls=%fused_computation.12 | convolution fusion | flops 3221749760 | bytes 29360640 | tf_op jit(solution)/shard_map/cfd,hjdk->cfhjk/dot_general | solution.py:121
  214.5 1.7 fusion.22
  216.2 2.8 fusion.23
  219.0 2.7 convert_reduce_fusion.1
  221.7 2.1 fusion.34
  223.8 2.6 fusion.4
  228.4 5.4 %fusion.1 = f32[1,16,128]{2,0,1:T(1,128)S(1)} fusion(f32[512,1,1]{0,1,2:T(1,128)S(1)} %bitcast.203, f32[16,160,512]{2,1,0:T(8,128)} %bitcast.186), kind=kOutput, calls=%fused_computation.2 | convolution fusion | flops 12582912 | bytes 4204544 | tf_op jit(solution)/shard_map/dot_general | solution.py:159
  237.3 1.1 multiply_convert_fusion
  238.4 1.6 fusion.30
  240.0 14.5 %multiply_reduce_fusion = (f32[128]{0:T(128)S(1)}, f32[128,2048]{1,0:T(8,128)}) fusion(f32[128,2048]{1,0:T(8,128)} %get-tuple-element.74, f32[128]{0:T(128)S(1)} %add_sqrt_fusion.3, bf16[16,3,2048,128]{3,2,1,0:T(8,128)(2,1)} %bitcast.183, bf16[128,16,1,128]{0,3,1,2:T(8,128)(2,1)} %multiply_convert_fusion, bf16[128,16,1,128]{0,3,1,2:T(8,128)(2,1)} %get-tuple-element.60, ...), kind=kOutput, calls=%fused_computation.50 | convolution fusion | flops 3223584768 | bytes 28836864 | tf_op jit(solution)/shard_map/cfhjk,hjdk->cfd/dot_general | solution.py:187
  254.5 3.7 multiply_reduce_fusion.8
  258.8 1.9 fusion.56
  261.2 2.7 fusion.66
  263.9 1.3 fusion.36
  267.5 3.2 fusion.15
  270.7 1.5 reduce_sum.241
  272.2 3.1 fusion.18
  275.3 2.2 copy.68
  277.5 1.6 fusion.37
  279.1 1.8 pad_maximum_fusion
  281.0 59.0 %reduce-scatter.2.cloned.1.call-done = f32[168,256]{1,0:T(8,128)} async-done(((f32[2688,256]{1,0:T(8,128)}), f32[168,256]{1,0:T(8,128)}) %reduce-scatter.2.cloned.1.call-update) | async-done | bytes 172048 | tf_op jit(solution)/shard_map/reduce_scatter | solution.py:221
  340.1 93.9 %all-reduce.2.cloned.1.call-done = f32[168,256]{1,0:T(8,128)} async-done(((f32[168,256]{1,0:T(8,128)}), f32[168,256]{1,0:T(8,128)}) %all-reduce.2.cloned.1.call-update) | async-done | bytes 172048 | tf_op jit(solution)/shard_map/psum | solution.py:222
  435.3 1.6 slice.138
  (122 shorter events, 19.9 us)
Async XLA Ops:
  7.2 2.0 copy-start
  7.2 55.8 %all-gather.7.cloned.1.call-start = ((), (), s32[]{:S(2)}) async-start(), calls=%async_computation.4 | async-start | bytes 5570560 | tf_op jit(solution)/shard_map/all_gather | solution.py:101
  15.8 2.3 copy-start.29
  15.9 3.5 copy-start.30
  15.9 4.1 copy-start.16
  15.9 4.1 copy-start.17
  16.6 6.2 %copy-start.28 = (bf16[1,128,256]{2,1,0:T(8,128)(2,1)S(1)}, bf16[1,128,256]{2,1,0:T(8,128)(2,1)}, u32[]{:S(2)}) copy-start(bf16[1,128,256]{2,1,0:T(8,128)(2,1)} %param.23) | copy-start | bytes 196612
  16.7 181.8 %all-gather.5.cloned.1.call-start = ((), (), s32[]{:S(2)}) async-start(), calls=%async_computation.3 | async-start | bytes 26738688 | tf_op jit(solution)/shard_map/all_gather | solution.py:108
  17.4 322.6 %reduce-scatter.2.cloned.1.call-start = ((), (), s32[]{:S(2)}) async-start(), calls=%async_computation.1 | async-start | bytes 2924544 | tf_op jit(solution)/shard_map/reduce_scatter | solution.py:221
  20.1 4.7 %copy-start.7 = (f32[2560]{0:T(1024)}, f32[2560]{0:T(1024)S(1)}, u32[]{:S(2)}) copy-start(f32[2560]{0:T(1024)S(1)} %get-tuple-element.83) | copy-start | bytes 30724
  20.1 4.7 %copy-start.9 = (f32[2560]{0:T(1024)}, f32[2560]{0:T(1024)S(1)}, u32[]{:S(2)}) copy-start(f32[2560]{0:T(1024)S(1)} %get-tuple-element.82) | copy-start | bytes 30724
  21.4 3.4 copy-start.18
  22.8 2.8 copy-start.26
  27.3 37.0 %copy-start.4 = (f32[1,128,1]{2,1,0:T(8,128)}, f32[1,128,1]{2,1,0:T(8,128)S(1)}, u32[]{:S(2)}) copy-start(f32[1,128,1]{2,1,0:T(8,128)S(1)} %get-tuple-element.66) | copy-start | bytes 1540
  30.1 32.9 %copy-start.11 = (f32[1,2048]{1,0:T(1,128)}, f32[1,2048]{1,0:T(1,128)S(1)}, u32[]{:S(2)}) copy-start(f32[1,2048]{1,0:T(1,128)S(1)} %get-tuple-element.68) | copy-start | bytes 24580
  30.1 32.9 %copy-start.13 = (f32[1,2048]{1,0:T(1,128)}, f32[1,2048]{1,0:T(1,128)S(1)}, u32[]{:S(2)}) copy-start(f32[1,2048]{1,0:T(1,128)S(1)} %get-tuple-element.69) | copy-start | bytes 24580
  228.4 6.1 %copy-start.1 = (f32[1,128,16,3,128]{1,4,3,2,0:T(8,128)S(1)}, f32[1,128,16,3,128]{1,4,3,2,0:T(8,128)}, u32[]{:S(2)}) copy-start(f32[1,128,16,3,128]{1,4,3,2,0:T(8,128)} %convolution_bitcast_fusion.1) | copy-start | bytes 9437188
  233.8 1.2 copy-start.2
  233.8 1.6 copy-start.3
  239.9 14.5 %copy-start.12 = (f32[1,2048]{1,0:T(1,128)S(1)}, f32[1,2048]{1,0:T(1,128)}, u32[]{:S(2)}) copy-start(f32[1,2048]{1,0:T(1,128)} %copy-done.11) | copy-start | bytes 24580
  239.9 14.5 %copy-start.14 = (f32[1,2048]{1,0:T(1,128)S(1)}, f32[1,2048]{1,0:T(1,128)}, u32[]{:S(2)}) copy-start(f32[1,2048]{1,0:T(1,128)} %copy-done.13) | copy-start | bytes 24580
  254.4 4.3 copy-start.20
  254.4 4.3 copy-start.21
  254.4 4.3 copy-start.23
  254.5 4.3 copy-start.25
  254.5 6.5 %copy-start.5 = (f32[1,128,1]{2,1,0:T(8,128)S(1)}, f32[1,128,1]{2,1,0:T(8,128)}, u32[]{:S(2)}) copy-start(f32[1,128,1]{2,1,0:T(8,128)} %copy-done.4) | copy-start | bytes 1540
  267.5 4.7 %copy-start.8 = (f32[2560]{0:T(1024)S(1)}, f32[2560]{0:T(1024)}, u32[]{:S(2)}) copy-start(f32[2560]{0:T(1024)} %copy-done.7) | copy-start | bytes 30724
  267.5 4.7 %copy-start.10 = (f32[2560]{0:T(1024)S(1)}, f32[2560]{0:T(1024)}, u32[]{:S(2)}) copy-start(f32[2560]{0:T(1024)} %copy-done.9) | copy-start | bytes 30724
  267.5 4.7 %copy-start.19 = (f32[128]{0:T(128)S(1)}, f32[128]{0:T(128)}, u32[]{:S(2)}) copy-start(f32[128]{0:T(128)} %copy-done.18) | copy-start | bytes 1540
  267.5 4.7 %copy-start.27 = (f32[128]{0:T(128)S(1)}, f32[128]{0:T(128)}, u32[]{:S(2)}) copy-start(f32[128]{0:T(128)} %copy-done.26) | copy-start | bytes 1540
  277.5 1.6 copy-start.15
  281.0 153.0 %all-reduce.2.cloned.1.call-start = ((), (), s32[]{:S(2)}) async-start(), calls=%async_computation.2 | async-start | bytes 344064 | tf_op jit(solution)/shard_map/psum | solution.py:222
  (3 other events, 2.2 us)
Sparse Core Ops, SparseCore 0:
  16.8 46.1 all-gather.6
  64.9 133.5 all-gather.4
  281.1 58.9 reduce-scatter.1
  343.5 90.4 all-reduce.1

commit v2 on v1

--- a/solution.py
+++ b/solution.py
@@ -65,6 +65,33 @@
     )
     d_spin = suffix(d_theta)
     return d_embedded.at[..., 0].add(d_spin).at[..., 1].add(d_east).at[..., 2].add(d_north)
+
+
+def xor_pairs(size, bit):
+    return [(i, i ^ bit) for i in range(size)]
+
+
+def halving_sum(chunks, axis):
+    size = lax.axis_size(axis)
+    me = lax.axis_index(axis)
+    bits = size.bit_length() - 1
+    assert 1 << bits == size
+    buf = chunks.reshape((2,) * bits + chunks.shape[1:])
+    for k in range(bits):
+        mine = (me >> k) & 1
+        keep = lax.dynamic_index_in_dim(buf, mine, axis=bits - 1 - k, keepdims=False)
+        send = lax.dynamic_index_in_dim(buf, 1 - mine, axis=bits - 1 - k, keepdims=False)
+        buf = keep + lax.ppermute(send, axis, xor_pairs(size, 1 << k))
+    return buf
+
+
+def doubling_sum(value, axis):
+    size = lax.axis_size(axis)
+    bits = size.bit_length() - 1
+    assert 1 << bits == size
+    for k in range(bits):
+        value = value + lax.ppermute(value, axis, xor_pairs(size, 1 << k))
+    return value
 
 
 def local(
@@ -97,14 +124,6 @@
         jnp.float32
     )
     text_part = jnp.sum(jnp.where(inside[..., None], picked, 0.0), axis=1)
-    proj_dev = w_proj.shape[0]
-    proj_text = lax.all_gather(
-        jnp.concatenate([w_proj.astype(jnp.float32), text_part], axis=0), "seq", axis=0
-    )
-    proj_rows = proj_text[:, :proj_dev].reshape(ways * proj_dev, w_proj.shape[1])
-    text_raw = jnp.sum(proj_text[:, proj_dev:], axis=0)
-    text_unit, text_len = unit_rows(text_raw)
-
     w_all = lax.all_gather(w_qkv, "seq", axis=0)
 
     hidden_f = hidden.astype(jnp.float32)
@@ -118,9 +137,21 @@
     x_clean = noisy.astype(jnp.float32) - level * eps_pred
     theta, path_east, path_north = local_path(x_clean)
     normed_e, scale_rms = embed(x_clean, path_east, path_north, w_embed, root_rows)
+    proj_dev = w_proj.shape[0]
+    w_all, proj_send, emb_b = lax.optimization_barrier(
+        (
+            w_all,
+            jnp.concatenate([w_proj.astype(jnp.float32), text_part], axis=0),
+            normed_e.astype(jnp.bfloat16),
+        )
+    )
+    proj_text = lax.all_gather(proj_send, "seq", axis=0)
+    proj_rows = proj_text[:, :proj_dev].reshape(ways * proj_dev, w_proj.shape[1])
+    text_raw = jnp.sum(proj_text[:, proj_dev:], axis=0)
+    text_unit, text_len = unit_rows(text_raw)
     projected = jnp.einsum(
         "cfd,hjdk->cfhjk",
-        normed_e.astype(jnp.bfloat16),
+        emb_b,
         w_all,
         preferred_element_type=jnp.float32,
     )
@@ -217,9 +248,9 @@
             jnp.broadcast_to(reward_rows[None], (ways, extra, cols)),
         ],
         axis=1,
-    ).reshape(ways * (rows_dev + extra), cols)
-    block = lax.psum_scatter(stacked, "seq", scatter_dimension=0, tiled=True)
-    block = lax.psum(block, ("sec", "dp"))
+    )
+    block = halving_sum(stacked, "seq")
+    block = doubling_sum(doubling_sum(block, "sec"), "dp")
     grad_w_out = block[:rows_dev]
     group_first = (lax.axis_index("sec") * n_dp + lax.axis_index("dp")) * ways * clips_dev
     all_rewards = block[rows_dev:].reshape(extra * cols)

time: 446 us -> 333 us (0.75)
  waiting for transfers between devices: 317 us -> 204 us
  starting transfers between devices: 0.16 us -> 13.2 us
  matrix products: 58.2 us -> 49.9 us
  other arithmetic: 34.6 us -> 29.8 us
    psum x1 -> x0, waiting for transfers between devices: 93.9 us -> none  [local(): block = lax.psum(block, ('sec', 'dp'))]
    ppermute x0 -> x8, waiting for transfers between devices: none -> 65.8 us  [the longest x4 45.4 us: halving_sum(): buf = keep + lax.ppermute(send, axis, xor_pairs(size, 1 << k))]
    reduce_scatter x1 -> x0, waiting for transfers between devices: 59 us -> none  [local(): block = lax.psum_scatter(stacked, 'seq', scatter_dimension=0, tiled=True)]
    all_gather x1, waiting for transfers between devices: 133 us -> 115 us  [local(): w_all = lax.all_gather(w_qkv, 'seq', axis=0)]
    ppermute x0 -> x8, starting transfers between devices: none -> 13.1 us  [the longest x4 6.73 us: halving_sum(): buf = keep + lax.ppermute(send, axis, xor_pairs(size, 1 << k))]
    all_gather x1, waiting for transfers between devices: 30.1 us -> 22.2 us  [local(): proj_text = lax.all_gather(proj_send, 'seq', axis=0)]
  transfers between devices with their start and end apart: 4 -> 10, of which waited for: 4 -> 10; matrix products, arithmetic and copies ran while one was open for 3% -> 13% of each run, Pallas kernels for 0% -> 0%
where the time goes in v2:
time: 333 us; the launch traced here: 332 us
  waiting for transfers between devices  204 us (61%)
  matrix products  49.9 us (15%)
  other arithmetic  29.8 us (9%)
  local copies, waits for them, and re-layouts  17.5 us (5%)
  between operations  17.5 us (5%)
  starting transfers between devices  13.2 us (4%)
    all_gather x1, waiting for transfers between devices, local(): w_all = lax.all_gather(w_qkv, 'seq', axis=0)  115 us
    ppermute x4, waiting for transfers between devices, halving_sum(): buf = keep + lax.ppermute(send, axis, xor_pairs(size, 1 << k))  45.4 us
    all_gather x1, waiting for transfers between devices, local(): proj_text = lax.all_gather(proj_send, 'seq', axis=0)  22.2 us
    ppermute x4, waiting for transfers between devices, doubling_sum(): value = value + lax.ppermute(value, axis, xor_pairs(size, 1 << k))  20.5 us
    dot_general x1, matrix products, local(): jnp.einsum('cfd,hjdk->cfhjk', emb_b, w_all, preferred_element_type=jnp.fl...  14.6 us
    dot_general x1, matrix products, local(): jnp.einsum('cfhjk,hjdk->cfd', d_proj, w_all, preferred_element_type=jnp.f...  13.6 us
    ppermute x4, starting transfers between devices, halving_sum(): buf = keep + lax.ppermute(send, axis, xor_pairs(size, 1 << k))  6.73 us
  transfers between devices with their start and end apart: 10, of which 10 were waited for; matrix products, arithmetic and copies ran while one was open for 13% of the time, Pallas kernels for 0%

profile of v2, /device:TPU:6, one launch (start us, length us, event | category | flops | bytes accessed | tf_op | source)
XLA Modules:
  0.0 331.7 jit_solution(3095173540981933043)
XLA Ops:
  11.4 1.4 fusion.19
  12.9 2.0 fusion.21
  21.1 5.3 %gather_fusion = bf16[1024,512]{1,0:T(8,128)(2,1)} fusion(bf16[3088,512]{1,0:T(8,128)(2,1)S(1)} %copy-done, s32[1024]{0:T(1024)} %broadcast_clamp_fusion), kind=kCustom, calls=%fused_computation | custom fusion | bytes 2101248 | tf_op jit(solution)/shard_map/jit(_take)/gather | solution.py:123
  28.5 1.6 select_reduce_fusion
  32.6 115.2 %all-gather.5.cloned.1.call-done = bf16[48,2048,128]{2,1,0:T(8,128)(2,1)} async-done(((bf16[3,2048,128]{2,1,0:T(8,128)(2,1)}), bf16[48,2048,128]{2,1,0:T(8,128)(2,1)}) %all-gather.5.cloned.1.call-update) | async-done | bytes 25165840 | tf_op jit(solution)/shard_map/all_gather | solution.py:127
  149.6 14.6 %convolution_bitcast_fusion.1 = f32[1,128,16,3,128]{1,4,3,2,0:T(8,128)S(1)} fusion(bf16[16,3,2048,128]{3,2,1,0:T(8,128)(2,1)} %bitcast.201, bf16[1,128,2048]{2,1,0:T(8,128)(2,1)} %convert_bitcast_fusion), kind=kOutput, calls=%fused_computation.12 | convolution fusion | flops 3221225472 | bytes 28835840 | tf_op jit(solution)/shard_map/cfd,hjdk->cfhjk/dot_general | solution.py:152
  165.7 2.6 convert_reduce_fusion.1
  169.3 22.2 %all-gather.7.cloned.1.call-done = f32[2560,512]{1,0:T(8,128)} async-done(((f32[160,512]{1,0:T(8,128)}), f32[2560,512]{1,0:T(8,128)}) %all-gather.7.cloned.1.call-update) | async-done | bytes 5242896 | tf_op jit(solution)/shard_map/all_gather | solution.py:148
  192.9 2.6 fusion.4
  198.3 5.3 %fusion.1 = f32[1,16,128]{2,0,1:T(1,128)S(1)} fusion(f32[512,1,1]{0,1,2:T(1,128)S(1)} %bitcast.222, f32[16,160,512]{2,1,0:T(8,128)} %bitcast.205), kind=kOutput, calls=%fused_computation.2 | convolution fusion | flops 12582912 | bytes 4204544 | tf_op jit(solution)/shard_map/dot_general | solution.py:190
  208.3 1.6 fusion.29
  210.0 13.6 %multiply_reduce_fusion = (f32[128]{0:T(128)S(1)}, f32[128,2048]{1,0:T(8,128)S(1)}) fusion(f32[128,2048]{1,0:T(8,128)} %copy-done.4, f32[128]{0:T(128)S(1)} %add_sqrt_fusion.3, bf16[16,3,2048,128]{3,2,1,0:T(8,128)(2,1)} %bitcast.202, bf16[128,16,1,128]{0,3,1,2:T(8,128)(2,1)} %multiply_convert_fusion, bf16[128,16,1,128]{0,3,1,2:T(8,128)(2,1)} %get-tuple-element.66, ...), kind=kOutput, calls=%fused_computation.52 | convolution fusion | flops 3223584768 | bytes 28836864 | tf_op jit(solution)/shard_map/cfhjk,hjdk->cfd/dot_general | solution.py:218
  223.6 1.3 multiply_reduce_fusion.8
  225.6 1.9 fusion.55
  228.0 2.5 fusion.65
  232.8 2.0 fusion.15
  234.9 1.4 fusion.18
  237.4 1.4 constant_dynamic-slice_fusion.1
  240.3 3.1 collective-permute-done
  244.5 1.5 bitcast_add_fusion
  246.1 1.5 collective-permute-start.1
  247.6 16.2 %collective-permute-done.1 = f32[2,2,168,256]{3,2,1,0:T(8,128)S(1)} collective-permute-done((f32[2,2,168,256]{3,2,1,0:T(8,128)S(1)}, f32[2,2,168,256]{3,2,1,0:T(8,128)S(1)}, u32[]{:S(2)}, u32[]{:S(2)}) %collective-permute-start.1) | collective-permute-done | bytes 688160 | tf_op jit(solution)/shard_map/ppermute | solution.py:84
  263.9 1.8 collective-permute-start.2
  265.7 15.9 %collective-permute-done.2 = f32[2,168,256]{2,1,0:T(8,128)S(1)} collective-permute-done((f32[2,168,256]{2,1,0:T(8,128)S(1)}, f32[2,168,256]{2,1,0:T(8,128)S(1)}, u32[]{:S(2)}, u32[]{:S(2)}) %collective-permute-start.2) | collective-permute-done | bytes 344096 | tf_op jit(solution)/shard_map/ppermute | solution.py:84
  282.4 3.1 collective-permute-start.3
  285.5 10.2 %collective-permute-done.3 = f32[168,256]{1,0:T(8,128)} collective-permute-done((f32[168,256]{1,0:T(8,128)}, f32[168,256]{1,0:T(8,128)}, u32[]{:S(2)}, u32[]{:S(2)}) %collective-permute-start.3) | collective-permute-done | bytes 172064 | tf_op jit(solution)/shard_map/ppermute | solution.py:84
  296.6 1.6 collective-permute-start.4
  298.2 4.7 %collective-permute-done.4 = f32[168,256]{1,0:T(8,128)S(1)} collective-permute-done((f32[168,256]{1,0:T(8,128)S(1)}, f32[168,256]{1,0:T(8,128)S(1)}, u32[]{:S(2)}, u32[]{:S(2)}) %collective-permute-start.4) | collective-permute-done | bytes 172064 | tf_op jit(solution)/shard_map/ppermute | solution.py:93
  303.0 3.2 collective-permute-start.5
  306.1 3.8 %collective-permute-done.5 = f32[168,256]{1,0:T(8,128)S(1)} collective-permute-done((f32[168,256]{1,0:T(8,128)S(1)}, f32[168,256]{1,0:T(8,128)S(1)}, u32[]{:S(2)}, u32[]{:S(2)}) %collective-permute-start.5) | collective-permute-done | bytes 172064 | tf_op jit(solution)/shard_map/ppermute | solution.py:93
  311.0 5.5 %collective-permute-done.6 = f32[168,256]{1,0:T(8,128)S(1)} collective-permute-done((f32[168,256]{1,0:T(8,128)S(1)}, f32[168,256]{1,0:T(8,128)S(1)}, u32[]{:S(2)}, u32[]{:S(2)}) %collective-permute-start.6) | collective-permute-done | bytes 172064 | tf_op jit(solution)/shard_map/ppermute | solution.py:93
  317.1 6.4 %collective-permute-done.7 = f32[168,256]{1,0:T(8,128)S(1)} collective-permute-done((f32[168,256]{1,0:T(8,128)S(1)}, f32[168,256]{1,0:T(8,128)S(1)}, u32[]{:S(2)}, u32[]{:S(2)}) %collective-permute-start.7) | collective-permute-done | bytes 172064 | tf_op jit(solution)/shard_map/ppermute | solution.py:93
  (160 shorter events, 37.1 us)
Async XLA Ops:
  7.2 14.0 %copy-start = (bf16[3088,512]{1,0:T(8,128)(2,1)S(1)}, bf16[3088,512]{1,0:T(8,128)(2,1)}, u32[]{:S(2)}) copy-start(bf16[3088,512]{1,0:T(8,128)(2,1)} %param.30) | copy-start | bytes 9486340
  7.2 2.9 copy-start.24
  7.2 2.9 copy-start.23
  7.2 5.7 %copy-start.35 = (bf16[1,128,256]{2,1,0:T(8,128)(2,1)S(1)}, bf16[1,128,256]{2,1,0:T(8,128)(2,1)}, u32[]{:S(2)}) copy-start(bf16[1,128,256]{2,1,0:T(8,128)(2,1)} %param.23) | copy-start | bytes 196612
  7.2 140.5 %all-gather.5.cloned.1.call-start = ((), (), s32[]{:S(2)}) async-start(), calls=%async_computation | async-start | bytes 26738688 | tf_op jit(solution)/shard_map/all_gather | solution.py:127
  8.0 183.5 %all-gather.7.cloned.1.call-start = ((), (), s32[]{:S(2)}) async-start(), calls=%async_computation.1 | async-start | bytes 5570560 | tf_op jit(solution)/shard_map/all_gather | solution.py:148
  10.2 4.7 %copy-start.17 = (f32[2560]{0:T(1024)}, f32[2560]{0:T(1024)S(1)}, u32[]{:S(2)}) copy-start(f32[2560]{0:T(1024)S(1)} %get-tuple-element.91) | copy-start | bytes 30724
  10.2 4.7 %copy-start.19 = (f32[2560]{0:T(1024)}, f32[2560]{0:T(1024)S(1)}, u32[]{:S(2)}) copy-start(f32[2560]{0:T(1024)S(1)} %get-tuple-element.90) | copy-start | bytes 30724
  11.4 3.4 %copy-start.25 = (f32[128]{0:T(128)}, f32[128]{0:T(128)S(1)}, u32[]{:S(2)}) copy-start(f32[128]{0:T(128)S(1)} %broadcast_multiply_fusion.3) | copy-start | bytes 1540
  26.5 4.5 %copy-start.21 = (bf16[2,2048]{1,0:T(2,128)(2,1)S(1)}, bf16[2,2048]{1,0:T(2,128)(2,1)}, u32[]{:S(2)}) copy-start(bf16[2,2048]{1,0:T(2,128)(2,1)} %param.27) | copy-start | bytes 24580
  26.5 4.5 %copy-start.9 = (bf16[256,2048]{1,0:T(8,128)(2,1)S(1)}, bf16[256,2048]{1,0:T(8,128)(2,1)}, u32[]{:S(2)}) copy-start(bf16[256,2048]{1,0:T(8,128)(2,1)} %param.26) | copy-start | bytes 3145732
  31.4 118.2 %copy-start.4 = (f32[128,2048]{1,0:T(8,128)}, f32[128,2048]{1,0:T(8,128)S(1)}, u32[]{:S(2)}) copy-start(f32[128,2048]{1,0:T(8,128)S(1)} %get-tuple-element.82) | copy-start | bytes 3145732
  31.4 116.4 %copy-start.36 = (f32[16]{0:T(128)S(1)}, f32[16]{0:T(128)}, u32[]{:S(2)}) copy-start(f32[16]{0:T(128)} %param.33) | copy-start | bytes 196
  31.4 117.6 %copy-start.37 = (s32[16]{0:T(128)S(1)}, s32[16]{0:T(128)}, u32[]{:S(2)}) copy-start(s32[16]{0:T(128)} %param.32) | copy-start | bytes 196
  210.0 13.6 %copy-start.5 = (f32[128,2048]{1,0:T(8,128)S(1)}, f32[128,2048]{1,0:T(8,128)}, u32[]{:S(2)}) copy-start(f32[128,2048]{1,0:T(8,128)} %copy-done.4) | copy-start | bytes 3145732
  223.6 4.2 %copy-start.13 = (f32[1,128,1]{2,1,0:T(8,128)S(1)}, f32[1,128,1]{2,1,0:T(8,128)}, u32[]{:S(2)}) copy-start(f32[1,128,1]{2,1,0:T(8,128)} %copy-done.12) | copy-start | bytes 1540
  223.6 4.1 %copy-start.15 = (f32[1,128,1]{2,1,0:T(8,128)S(1)}, f32[1,128,1]{2,1,0:T(8,128)}, u32[]{:S(2)}) copy-start(f32[1,128,1]{2,1,0:T(8,128)} %copy-done.14) | copy-start | bytes 1540
  227.8 3.6 %copy-start.11 = (f32[1,128,1]{2,1,0:T(8,128)S(1)}, f32[1,128,1]{2,1,0:T(8,128)}, u32[]{:S(2)}) copy-start(f32[1,128,1]{2,1,0:T(8,128)} %copy-done.10) | copy-start | bytes 1540
  228.0 4.7 %copy-start.2 = (bf16[1,128,2560]{2,1,0:T(8,128)(2,1)S(1)}, bf16[1,128,2560]{2,1,0:T(8,128)(2,1)}, u32[]{:S(2)}) copy-start(bf16[1,128,2560]{2,1,0:T(8,128)(2,1)} %param.20) | copy-start | bytes 1966084
  228.0 4.7 %copy-start.18 = (f32[2560]{0:T(1024)S(1)}, f32[2560]{0:T(1024)}, u32[]{:S(2)}) copy-start(f32[2560]{0:T(1024)} %copy-done.17) | copy-start | bytes 30724
  228.0 4.7 %copy-start.26 = (f32[128]{0:T(128)S(1)}, f32[128]{0:T(128)}, u32[]{:S(2)}) copy-start(f32[128]{0:T(128)} %copy-done.25) | copy-start | bytes 1540
  228.0 4.7 %copy-start.34 = (f32[128]{0:T(128)S(1)}, f32[128]{0:T(128)}, u32[]{:S(2)}) copy-start(f32[128]{0:T(128)} %copy-done.33) | copy-start | bytes 1540
  238.8 5.7 %copy-start.3 = (f32[2,2,2,1,168,256]{5,4,3,2,1,0:T(8,128)S(1)}, f32[2,2,2,1,168,256]{5,4,3,2,1,0:T(8,128)}, u32[]{:S(2)}) copy-start(f32[2,2,2,1,168,256]{5,4,3,2,1,0:T(8,128)} %get-tuple-element.69) | copy-start | bytes 4128772
  240.0 3.3 %collective-permute-start = (f32[2,2,2,168,256]{4,3,1,0,2:T(8,128)}, f32[2,2,2,168,256]{4,3,1,0,2:T(8,128)S(1)}, u32[]{:S(2)}, u32[]{:S(2)}) collective-permute-start(f32[2,2,2,168,256]{4,3,1,0,2:T(8,128)} %bitcast.199), channel_id=1, source_target_pairs={{0,1},{1,0},{2,3},{3,2},{4,5},{5,4},{6,7},{7,6},{8,9},{9,8},{10,11... | collective-permute-start | bytes 4128776 | tf_op jit(solution)/shard_map/ppermute | solution.py:84
  246.1 17.7 %collective-permute-start.1 = (f32[2,2,168,256]{3,2,1,0:T(8,128)S(1)}, f32[2,2,168,256]{3,2,1,0:T(8,128)S(1)}, u32[]{:S(2)}, u32[]{:S(2)}) collective-permute-start(f32[2,2,168,256]{3,2,1,0:T(8,128)S(1)} %dynamic-slice_bitcast_fusion), channel_id=1, source_target_pairs={{0,2},{1,3},{2,0},{3,1},{4,6},{5,7},{6,4},{7,5},{8,10},{9,11},{10,... | collective-permute-start | bytes 2064392 | tf_op jit(solution)/shard_map/ppermute | solution.py:84
  263.9 17.8 %collective-permute-start.2 = (f32[2,168,256]{2,1,0:T(8,128)S(1)}, f32[2,168,256]{2,1,0:T(8,128)S(1)}, u32[]{:S(2)}, u32[]{:S(2)}) collective-permute-start(f32[2,168,256]{2,1,0:T(8,128)S(1)} %dynamic-slice_bitcast_fusion.1), channel_id=1, source_target_pairs={{0,4},{1,5},{2,6},{3,7},{4,0},{5,1},{6,2},{7,3},{8,12},{9,13},{10,... | collective-permute-start | bytes 1032200 | tf_op jit(solution)/shard_map/ppermute | solution.py:84
  282.4 13.3 %collective-permute-start.3 = (f32[168,256]{1,0:T(8,128)}, f32[168,256]{1,0:T(8,128)}, u32[]{:S(2)}, u32[]{:S(2)}) collective-permute-start(f32[168,256]{1,0:T(8,128)} %dynamic-slice_bitcast_fusion.2), channel_id=1, source_target_pairs={{0,8},{1,9},{2,10},{3,11},{4,12},{5,13},{6,14},{7,15},{8,0},{9,1},... | collective-permute-start | bytes 516104 | tf_op jit(solution)/shard_map/ppermute | solution.py:84
  285.5 39.4 %copy-start.1 = (bf16[3088,512]{1,0:T(8,128)(2,1)S(1)}, bf16[3088,512]{1,0:T(8,128)(2,1)}, u32[]{:S(2)}) copy-start(bf16[3088,512]{1,0:T(8,128)(2,1)} %param.30) | copy-start | bytes 9486340
  296.6 6.3 %collective-permute-start.4 = (f32[168,256]{1,0:T(8,128)S(1)}, f32[168,256]{1,0:T(8,128)S(1)}, u32[]{:S(2)}, u32[]{:S(2)}) collective-permute-start(f32[168,256]{1,0:T(8,128)S(1)} %bitcast_add_fusion.3), channel_id=1, source_target_pairs={{0,128},{128,0},{1,129},{129,1},{2,130},{130,2},{3,131},{131,3},{4... | collective-permute-start | bytes 516104 | tf_op jit(solution)/shard_map/ppermute | solution.py:93
  303.0 7.0 %collective-permute-start.5 = (f32[168,256]{1,0:T(8,128)S(1)}, f32[168,256]{1,0:T(8,128)S(1)}, u32[]{:S(2)}, u32[]{:S(2)}) collective-permute-start(f32[168,256]{1,0:T(8,128)S(1)} %add.256), channel_id=1, source_target_pairs={{0,16},{16,0},{32,48},{48,32},{64,80},{80,64},{96,112},{112,96},{1... | collective-permute-start | bytes 516104 | tf_op jit(solution)/shard_map/ppermute | solution.py:93
  310.0 6.5 %collective-permute-start.6 = (f32[168,256]{1,0:T(8,128)S(1)}, f32[168,256]{1,0:T(8,128)S(1)}, u32[]{:S(2)}, u32[]{:S(2)}) collective-permute-start(f32[168,256]{1,0:T(8,128)S(1)} %add.257), channel_id=1, source_target_pairs={{0,32},{16,48},{32,0},{48,16},{64,96},{80,112},{96,64},{112,80},{1... | collective-permute-start | bytes 516104 | tf_op jit(solution)/shard_map/ppermute | solution.py:93
  316.5 7.0 %collective-permute-start.7 = (f32[168,256]{1,0:T(8,128)S(1)}, f32[168,256]{1,0:T(8,128)S(1)}, u32[]{:S(2)}, u32[]{:S(2)}) collective-permute-start(f32[168,256]{1,0:T(8,128)S(1)} %add.258), channel_id=1, source_target_pairs={{0,64},{16,80},{32,96},{48,112},{64,0},{80,16},{96,32},{112,48},{1... | collective-permute-start | bytes 516104 | tf_op jit(solution)/shard_map/ppermute | solution.py:93
  (16 other events, 22.0 us)
Sparse Core Ops, SparseCore 0:
  9.9 137.8 all-gather.4
  149.6 41.8 all-gather.6

commit v3 on v2

--- a/solution.py
+++ b/solution.py
@@ -71,7 +71,7 @@
     return [(i, i ^ bit) for i in range(size)]
 
 
-def halving_sum(chunks, axis):
+def halving_sum(chunks, axis, wire_types):
     size = lax.axis_size(axis)
     me = lax.axis_index(axis)
     bits = size.bit_length() - 1
@@ -81,7 +81,8 @@
         mine = (me >> k) & 1
         keep = lax.dynamic_index_in_dim(buf, mine, axis=bits - 1 - k, keepdims=False)
         send = lax.dynamic_index_in_dim(buf, 1 - mine, axis=bits - 1 - k, keepdims=False)
-        buf = keep + lax.ppermute(send, axis, xor_pairs(size, 1 << k))
+        got = lax.ppermute(send.astype(wire_types[k]), axis, xor_pairs(size, 1 << k))
+        buf = keep + got.astype(keep.dtype)
     return buf
 
 
@@ -124,6 +125,7 @@
         jnp.float32
     )
     text_part = jnp.sum(jnp.where(inside[..., None], picked, 0.0), axis=1)
+    text_raw = doubling_sum(text_part, "seq")
     w_all = lax.all_gather(w_qkv, "seq", axis=0)
 
     hidden_f = hidden.astype(jnp.float32)
@@ -137,18 +139,12 @@
     x_clean = noisy.astype(jnp.float32) - level * eps_pred
     theta, path_east, path_north = local_path(x_clean)
     normed_e, scale_rms = embed(x_clean, path_east, path_north, w_embed, root_rows)
-    proj_dev = w_proj.shape[0]
-    w_all, proj_send, emb_b = lax.optimization_barrier(
-        (
-            w_all,
-            jnp.concatenate([w_proj.astype(jnp.float32), text_part], axis=0),
-            normed_e.astype(jnp.bfloat16),
-        )
-    )
-    proj_text = lax.all_gather(proj_send, "seq", axis=0)
-    proj_rows = proj_text[:, :proj_dev].reshape(ways * proj_dev, w_proj.shape[1])
-    text_raw = jnp.sum(proj_text[:, proj_dev:], axis=0)
+    w_all, proj_send, emb_b, text_raw = lax.optimization_barrier(
+        (w_all, w_proj, normed_e.astype(jnp.bfloat16), text_raw)
+    )
     text_unit, text_len = unit_rows(text_raw)
+    proj_b = lax.all_gather(proj_send, "seq", axis=0, tiled=True)
+    proj_rows = proj_b.astype(jnp.float32)
     projected = jnp.einsum(
         "cfd,hjdk->cfhjk",
         emb_b,
@@ -173,9 +169,7 @@
     value_f = value_b.astype(jnp.float32)
     pooled = jnp.einsum("chg,cghd->chd", column_mass, value_f, precision=highest)
     pooled_b = pooled.astype(jnp.bfloat16).reshape(clips_dev, D_REW)
-    motion_emb = jnp.dot(
-        pooled_b, proj_rows.astype(jnp.bfloat16), preferred_element_type=jnp.float32
-    )
+    motion_emb = jnp.dot(pooled_b, proj_b, preferred_element_type=jnp.float32)
     prompts = lax.dynamic_slice_in_dim(prompt_index, me * clips_dev, clips_dev)
     weights = lax.dynamic_slice_in_dim(reward_weight, me * clips_dev, clips_dev)
     choose = (prompts[:, None] == jnp.arange(PROMPTS)[None, :]).astype(jnp.float32)
@@ -249,7 +243,8 @@
         ],
         axis=1,
     )
-    block = halving_sum(stacked, "seq")
+    seq_bits = ways.bit_length() - 1
+    block = halving_sum(stacked, "seq", [jnp.float32] + [jnp.bfloat16] * (seq_bits - 1))
     block = doubling_sum(doubling_sum(block, "sec"), "dp")
     grad_w_out = block[:rows_dev]
     group_first = (lax.axis_index("sec") * n_dp + lax.axis_index("dp")) * ways * clips_dev

time: 333 us -> 310 us (0.931)
  waiting for transfers between devices: 204 us -> 183 us
  starting transfers between devices: 13.2 us -> 26.1 us
  other arithmetic: 29.8 us -> 19.7 us
    ppermute x4, waiting for transfers between devices: 45.4 us -> 27.2 us  [halving_sum(): lax.ppermute(send.astype(wire_types[k]), axis, xor_pairs(size, 1 << k))]
    ppermute x4 -> x8, starting transfers between devices: 6.39 us -> 20 us  [doubling_sum(): value = value + lax.ppermute(value, axis, xor_pairs(size, 1 << k))]
    ppermute x4 -> x8, waiting for transfers between devices: 20.5 us -> 29.1 us  [doubling_sum(): value = value + lax.ppermute(value, axis, xor_pairs(size, 1 << k))]
    all_gather x1, waiting for transfers between devices: 115 us -> 107 us  [local(): w_all = lax.all_gather(w_qkv, 'seq', axis=0)]
  transfers between devices with their start and end apart: 10 -> 14, of which waited for: 10 -> 13; matrix products, arithmetic and copies ran while one was open for 13% -> 11% of each run, Pallas kernels for 0% -> 0%
where the time goes in v3:
time: 310 us; the launch traced here: 308 us
  waiting for transfers between devices  183 us (59%)
  matrix products  46.9 us (15%)
  starting transfers between devices  26.1 us (8%)
  other arithmetic  19.7 us (6%)
  between operations  17.2 us (6%)
  local copies, waits for them, and re-layouts  15.2 us (5%)
    all_gather x1, waiting for transfers between devices, local(): w_all = lax.all_gather(w_qkv, 'seq', axis=0)  107 us
    ppermute x8, waiting for transfers between devices, doubling_sum(): value = value + lax.ppermute(value, axis, xor_pairs(size, 1 << k))  29.1 us
    ppermute x4, waiting for transfers between devices, halving_sum(): lax.ppermute(send.astype(wire_types[k]), axis, xor_pairs(size, 1 << k))  27.2 us
    ppermute x8, starting transfers between devices, doubling_sum(): value = value + lax.ppermute(value, axis, xor_pairs(size, 1 << k))  20 us
    all_gather x1, waiting for transfers between devices, local(): proj_b = lax.all_gather(proj_send, 'seq', axis=0, tiled=True)  19.6 us
    dot_general x1, matrix products, local(): jnp.einsum('cfd,hjdk->cfhjk', emb_b, w_all, preferred_element_type=jnp.fl...  14.6 us
    dot_general x1, matrix products, local(): jnp.einsum('cfhjk,hjdk->cfd', d_proj, w_all, preferred_element_type=jnp.f...  13.7 us
  transfers between devices with their start and end apart: 14, of which 13 were waited for; matrix products, arithmetic and copies ran while one was open for 11% of the time, Pallas kernels for 0%

profile of v3, /device:TPU:6, one launch (start us, length us, event | category | flops | bytes accessed | tf_op | source)
XLA Modules:
  0.0 308.3 jit_solution(14263401615607326272)
XLA Ops:
  9.1 5.1 %gather_fusion = bf16[1024,512]{1,0:T(8,128)(2,1)} fusion(bf16[3088,512]{1,0:T(8,128)(2,1)S(1)} %copy-done, s32[1024]{0:T(1024)S(1)} %broadcast_clamp_fusion), kind=kCustom, calls=%fused_computation | custom fusion | bytes 2101248 | tf_op jit(solution)/shard_map/jit(_take)/gather | solution.py:124
  14.2 1.8 select_reduce_fusion
  19.5 2.0 collective-permute-start.1
  22.0 2.3 collective-permute-done.1
  24.3 3.4 %collective-permute-start.2 = (f32[32,512]{1,0:T(8,128)S(1)}, f32[32,512]{1,0:T(8,128)S(1)}, u32[]{:S(2)}, u32[]{:S(2)}) collective-permute-start(f32[32,512]{1,0:T(8,128)S(1)} %add.244), channel_id=1, source_target_pairs={{0,4},{1,5},{2,6},{3,7},{4,0},{5,1},{6,2},{7,3},{8,12},{9,13},{10,... | collective-permute-start | bytes 196616 | tf_op jit(solution)/shard_map/ppermute | solution.py:94
  27.7 5.2 %collective-permute-done.2 = f32[32,512]{1,0:T(8,128)S(1)} collective-permute-done((f32[32,512]{1,0:T(8,128)S(1)}, f32[32,512]{1,0:T(8,128)S(1)}, u32[]{:S(2)}, u32[]{:S(2)}) %collective-permute-start.2) | collective-permute-done | bytes 65568 | tf_op jit(solution)/shard_map/ppermute | solution.py:94
  32.9 7.4 %collective-permute-start.3 = (f32[32,512]{1,0:T(8,128)S(1)}, f32[32,512]{1,0:T(8,128)S(1)}, u32[]{:S(2)}, u32[]{:S(2)}) collective-permute-start(f32[32,512]{1,0:T(8,128)S(1)} %add.245), channel_id=1, source_target_pairs={{0,8},{1,9},{2,10},{3,11},{4,12},{5,13},{6,14},{7,15},{8,0},{9,1},... | collective-permute-start | bytes 196616 | tf_op jit(solution)/shard_map/ppermute | solution.py:94
  41.2 2.7 collective-permute-done.3
  44.0 106.6 %all-gather.6.cloned.1.call-done = bf16[48,2048,128]{2,1,0:T(8,128)(2,1)} async-done(((bf16[3,2048,128]{2,1,0:T(8,128)(2,1)}), bf16[48,2048,128]{2,1,0:T(8,128)(2,1)}) %all-gather.6.cloned.1.call-update) | async-done | bytes 25165840 | tf_op jit(solution)/shard_map/all_gather | solution.py:129
  152.4 14.6 %convolution_bitcast_fusion.1 = f32[1,128,16,3,128]{1,4,3,2,0:T(8,128)S(1)} fusion(bf16[16,3,2048,128]{3,2,1,0:T(8,128)(2,1)} %bitcast.205, bf16[1,128,2048]{2,1,0:T(8,128)(2,1)} %convert_bitcast_fusion), kind=kOutput, calls=%fused_computation.8 | convolution fusion | flops 3221225472 | bytes 28835840 | tf_op jit(solution)/shard_map/cfd,hjdk->cfhjk/dot_general | solution.py:148
  168.5 2.6 convert_reduce_fusion.1
  173.1 19.6 %all-gather.4.cloned.1.call-done = bf16[2048,512]{1,0:T(8,128)(2,1)} async-done(((bf16[128,512]{1,0:T(8,128)(2,1)}), bf16[2048,512]{1,0:T(8,128)(2,1)}) %all-gather.4.cloned.1.call-update) | async-done | bytes 2097168 | tf_op jit(solution)/shard_map/all_gather | solution.py:146
  192.7 2.0 fusion.64
  196.7 3.4 %fusion.65 = f32[1,2048]{1,0:T(1,128)S(1)} fusion(f32[512,1]{0,1:T(1,128)S(1)} %bitcast.223, bf16[2048,512]{1,0:T(8,128)(2,1)} %all-gather.4.cloned.1.call-done), kind=kOutput, calls=%fused_computation.154 | convolution fusion | flops 12582912 | bytes 2107392 | tf_op jit(solution)/shard_map/dot_general | solution.py:184
  204.1 1.6 fusion.26
  205.7 13.7 %multiply_reduce_fusion = (f32[128]{0:T(128)S(1)}, f32[128,2048]{1,0:T(8,128)S(1)}) fusion(f32[128,2048]{1,0:T(8,128)} %copy-done.4, f32[128]{0:T(128)S(1)} %add_sqrt_fusion.3, bf16[16,3,2048,128]{3,2,1,0:T(8,128)(2,1)} %bitcast.206, bf16[128,16,1,128]{0,3,1,2:T(8,128)(2,1)} %multiply_convert_fusion, bf16[128,16,1,128]{0,3,1,2:T(8,128)(2,1)} %get-tuple-element.68, ...), kind=kOutput, calls=%fused_computation.47 | convolution fusion | flops 3223584768 | bytes 28836864 | tf_op jit(solution)/shard_map/cfhjk,hjdk->cfd/dot_general | solution.py:212
  221.4 1.9 fusion.54
  223.8 2.5 fusion.66
  228.4 2.0 fusion.12
  233.0 1.6 fusion.36
  236.6 3.1 %collective-permute-done.4 = f32[2,2,2,168,256]{4,3,0,1,2:T(8,128)S(1)} collective-permute-done((f32[2,2,2,168,256]{4,3,0,1,2:T(8,128)}, f32[2,2,2,168,256]{4,3,0,1,2:T(8,128)S(1)}, u32[]{:S(2)}, u32[]{:S(2)}) %collective-permute-start.4) | collective-permute-done | bytes 1376288 | tf_op jit(solution)/shard_map/ppermute | solution.py:84
  243.4 9.3 %collective-permute-done.5 = bf16[2,2,168,256]{3,2,0,1:T(8,128)(2,1)S(1)} collective-permute-done((bf16[2,2,168,256]{3,2,0,1:T(8,128)(2,1)S(1)}, bf16[2,2,168,256]{3,2,0,1:T(8,128)(2,1)S(1)}, u32[]{:S(2)}, u32[]{:S(2)}) %collective-permute-start.5) | collective-permute-done | bytes 344096 | tf_op jit(solution)/shard_map/ppermute | solution.py:84
  252.8 1.8 collective-permute-start.6
  254.6 8.6 %collective-permute-done.6 = bf16[2,168,256]{2,1,0:T(8,128)(2,1)S(1)} collective-permute-done((bf16[2,168,256]{2,1,0:T(8,128)(2,1)S(1)}, bf16[2,168,256]{2,1,0:T(8,128)(2,1)S(1)}, u32[]{:S(2)}, u32[]{:S(2)}) %collective-permute-start.6) | collective-permute-done | bytes 172064 | tf_op jit(solution)/shard_map/ppermute | solution.py:84
  263.9 2.9 collective-permute-start.7
  266.8 6.3 %collective-permute-done.7 = bf16[168,256]{1,0:T(8,128)(2,1)} collective-permute-done((bf16[168,256]{1,0:T(8,128)(2,1)}, bf16[168,256]{1,0:T(8,128)(2,1)}, u32[]{:S(2)}, u32[]{:S(2)}) %collective-permute-start.7) | collective-permute-done | bytes 86048 | tf_op jit(solution)/shard_map/ppermute | solution.py:84
  274.0 1.6 collective-permute-start.8
  275.6 3.9 %collective-permute-done.8 = f32[168,256]{1,0:T(8,128)S(1)} collective-permute-done((f32[168,256]{1,0:T(8,128)S(1)}, f32[168,256]{1,0:T(8,128)S(1)}, u32[]{:S(2)}, u32[]{:S(2)}) %collective-permute-start.8) | collective-permute-done | bytes 172064 | tf_op jit(solution)/shard_map/ppermute | solution.py:94
  279.5 3.4 %collective-permute-start.9 = (f32[168,256]{1,0:T(8,128)S(1)}, f32[168,256]{1,0:T(8,128)S(1)}, u32[]{:S(2)}, u32[]{:S(2)}) collective-permute-start(f32[168,256]{1,0:T(8,128)S(1)} %add.272), channel_id=1, source_target_pairs={{0,16},{16,0},{32,48},{48,32},{64,80},{80,64},{96,112},{112,96},{1... | collective-permute-start | bytes 516104 | tf_op jit(solution)/shard_map/ppermute | solution.py:94
  282.9 3.6 %collective-permute-done.9 = f32[168,256]{1,0:T(8,128)S(1)} collective-permute-done((f32[168,256]{1,0:T(8,128)S(1)}, f32[168,256]{1,0:T(8,128)S(1)}, u32[]{:S(2)}, u32[]{:S(2)}) %collective-permute-start.9) | collective-permute-done | bytes 172064 | tf_op jit(solution)/shard_map/ppermute | solution.py:94
  288.0 5.1 %collective-permute-done.10 = f32[168,256]{1,0:T(8,128)S(1)} collective-permute-done((f32[168,256]{1,0:T(8,128)S(1)}, f32[168,256]{1,0:T(8,128)S(1)}, u32[]{:S(2)}, u32[]{:S(2)}) %collective-permute-start.10) | collective-permute-done | bytes 172064 | tf_op jit(solution)/shard_map/ppermute | solution.py:94
  293.9 6.3 %collective-permute-done.11 = f32[168,256]{1,0:T(8,128)S(1)} collective-permute-done((f32[168,256]{1,0:T(8,128)S(1)}, f32[168,256]{1,0:T(8,128)S(1)}, u32[]{:S(2)}, u32[]{:S(2)}) %collective-permute-start.11) | collective-permute-done | bytes 172064 | tf_op jit(solution)/shard_map/ppermute | solution.py:94
  (132 shorter events, 33.4 us)
Async XLA Ops:
  7.2 1.9 copy-start
  7.2 143.3 %all-gather.6.cloned.1.call-start = ((), (), s32[]{:S(2)}) async-start(), calls=%async_computation.1 | async-start | bytes 26738688 | tf_op jit(solution)/shard_map/all_gather | solution.py:129
  7.9 184.8 %all-gather.4.cloned.1.call-start = ((), (), s32[]{:S(2)}) async-start(), calls=%async_computation | async-start | bytes 2228224 | tf_op jit(solution)/shard_map/all_gather | solution.py:146
  9.1 7.6 %copy-start.14 = (bf16[1,2560]{1,0:T(2,128)(2,1)S(1)}, bf16[1,2560]{1,0:T(2,128)(2,1)}, u32[]{:S(2)}) copy-start(bf16[1,2560]{1,0:T(2,128)(2,1)} %param.21) | copy-start | bytes 15364
  9.1 7.6 %copy-start.15 = (bf16[1,2560]{1,0:T(2,128)(2,1)S(1)}, bf16[1,2560]{1,0:T(2,128)(2,1)}, u32[]{:S(2)}) copy-start(bf16[1,2560]{1,0:T(2,128)(2,1)} %param.22) | copy-start | bytes 15364
  14.1 2.6 copy-start.2
  14.2 3.1 %copy-start.9 = (bf16[2560,256]{1,0:T(8,128)(2,1)S(1)}, bf16[2560,256]{1,0:T(8,128)(2,1)}, u32[]{:S(2)}) copy-start(bf16[2560,256]{1,0:T(8,128)(2,1)} %param.25) | copy-start | bytes 3932164
  14.2 3.1 %copy-start.16 = (bf16[1,128,256]{2,1,0:T(8,128)(2,1)S(1)}, bf16[1,128,256]{2,1,0:T(8,128)(2,1)}, u32[]{:S(2)}) copy-start(bf16[1,128,256]{2,1,0:T(8,128)(2,1)} %param.23) | copy-start | bytes 196612
  15.9 3.6 %collective-permute-start = (f32[32,512]{1,0:T(8,128)S(1)}, f32[32,512]{1,0:T(8,128)S(1)}, u32[]{:S(2)}, u32[]{:S(2)}) collective-permute-start(f32[32,512]{1,0:T(8,128)S(1)} %select_reduce_fusion), channel_id=1, source_target_pairs={{0,1},{1,0},{2,3},{3,2},{4,5},{5,4},{6,7},{7,6},{8,9},{9,8},{10,11... | collective-permute-start | bytes 196616 | tf_op jit(solution)/shard_map/ppermute | solution.py:94
  17.3 2.0 copy-start.12
  17.8 3.8 %copy-start.10 = (bf16[256,2048]{1,0:T(8,128)(2,1)S(1)}, bf16[256,2048]{1,0:T(8,128)(2,1)}, u32[]{:S(2)}) copy-start(bf16[256,2048]{1,0:T(8,128)(2,1)} %param.26) | copy-start | bytes 3145732
  19.5 4.8 %collective-permute-start.1 = (f32[32,512]{1,0:T(8,128)S(1)}, f32[32,512]{1,0:T(8,128)S(1)}, u32[]{:S(2)}, u32[]{:S(2)}) collective-permute-start(f32[32,512]{1,0:T(8,128)S(1)} %add.243), channel_id=1, source_target_pairs={{0,2},{1,3},{2,0},{3,1},{4,6},{5,7},{6,4},{7,5},{8,10},{9,11},{10,... | collective-permute-start | bytes 196616 | tf_op jit(solution)/shard_map/ppermute | solution.py:94
  22.0 130.4 %copy-start.4 = (f32[128,2048]{1,0:T(8,128)}, f32[128,2048]{1,0:T(8,128)S(1)}, u32[]{:S(2)}) copy-start(f32[128,2048]{1,0:T(8,128)S(1)} %get-tuple-element.84) | copy-start | bytes 3145732
  22.0 128.6 %copy-start.17 = (s32[16]{0:T(128)S(1)}, s32[16]{0:T(128)}, u32[]{:S(2)}) copy-start(s32[16]{0:T(128)} %param.32) | copy-start | bytes 196
  22.0 129.1 %copy-start.18 = (f32[16]{0:T(128)S(1)}, f32[16]{0:T(128)}, u32[]{:S(2)}) copy-start(f32[16]{0:T(128)} %param.33) | copy-start | bytes 196
  24.3 8.6 %collective-permute-start.2 = (f32[32,512]{1,0:T(8,128)S(1)}, f32[32,512]{1,0:T(8,128)S(1)}, u32[]{:S(2)}, u32[]{:S(2)}) collective-permute-start(f32[32,512]{1,0:T(8,128)S(1)} %add.244), channel_id=1, source_target_pairs={{0,4},{1,5},{2,6},{3,7},{4,0},{5,1},{6,2},{7,3},{8,12},{9,13},{10,... | collective-permute-start | bytes 196616 | tf_op jit(solution)/shard_map/ppermute | solution.py:94
  32.9 11.1 %collective-permute-start.3 = (f32[32,512]{1,0:T(8,128)S(1)}, f32[32,512]{1,0:T(8,128)S(1)}, u32[]{:S(2)}, u32[]{:S(2)}) collective-permute-start(f32[32,512]{1,0:T(8,128)S(1)} %add.245), channel_id=1, source_target_pairs={{0,8},{1,9},{2,10},{3,11},{4,12},{5,13},{6,14},{7,15},{8,0},{9,1},... | collective-permute-start | bytes 196616 | tf_op jit(solution)/shard_map/ppermute | solution.py:94
  196.7 3.9 %copy-start.6 = (f32[16,128,128]{1,2,0:T(8,128)S(1)}, f32[16,128,128]{1,2,0:T(8,128)}, u32[]{:S(2)}) copy-start(f32[16,128,128]{1,2,0:T(8,128)} %get-tuple-element.86) | copy-start | bytes 3145732
  200.1 1.1 copy-start.7
  201.1 1.0 copy-start.11
  205.7 13.7 %copy-start.5 = (f32[128,2048]{1,0:T(8,128)S(1)}, f32[128,2048]{1,0:T(8,128)}, u32[]{:S(2)}) copy-start(f32[128,2048]{1,0:T(8,128)} %copy-done.4) | copy-start | bytes 3145732
  223.7 4.7 %copy-start.3 = (bf16[1,128,2560]{2,1,0:T(8,128)(2,1)S(1)}, bf16[1,128,2560]{2,1,0:T(8,128)(2,1)}, u32[]{:S(2)}) copy-start(bf16[1,128,2560]{2,1,0:T(8,128)(2,1)} %param.20) | copy-start | bytes 1966084
  236.4 3.3 %collective-permute-start.4 = (f32[2,2,2,168,256]{4,3,0,1,2:T(8,128)}, f32[2,2,2,168,256]{4,3,0,1,2:T(8,128)S(1)}, u32[]{:S(2)}, u32[]{:S(2)}) collective-permute-start(f32[2,2,2,168,256]{4,3,0,1,2:T(8,128)} %bitcast.203), channel_id=1, source_target_pairs={{0,1},{1,0},{2,3},{3,2},{4,5},{5,4},{6,7},{7,6},{8,9},{9,8},{10,11... | collective-permute-start | bytes 4128776 | tf_op jit(solution)/shard_map/ppermute | solution.py:84
  239.7 1.1 copy-start.8
  242.4 10.3 %collective-permute-start.5 = (bf16[2,2,168,256]{3,2,0,1:T(8,128)(2,1)S(1)}, bf16[2,2,168,256]{3,2,0,1:T(8,128)(2,1)S(1)}, u32[]{:S(2)}, u32[]{:S(2)}) collective-permute-start(bf16[2,2,168,256]{3,2,0,1:T(8,128)(2,1)S(1)} %fusion.28), channel_id=1, source_target_pairs={{0,2},{1,3},{2,0},{3,1},{4,6},{5,7},{6,4},{7,5},{8,10},{9,11},{10,... | collective-permute-start | bytes 1032200 | tf_op jit(solution)/shard_map/ppermute | solution.py:84
  252.8 10.4 %collective-permute-start.6 = (bf16[2,168,256]{2,1,0:T(8,128)(2,1)S(1)}, bf16[2,168,256]{2,1,0:T(8,128)(2,1)S(1)}, u32[]{:S(2)}, u32[]{:S(2)}) collective-permute-start(bf16[2,168,256]{2,1,0:T(8,128)(2,1)S(1)} %fusion.33), channel_id=1, source_target_pairs={{0,4},{1,5},{2,6},{3,7},{4,0},{5,1},{6,2},{7,3},{8,12},{9,13},{10,... | collective-permute-start | bytes 516104 | tf_op jit(solution)/shard_map/ppermute | solution.py:84
  263.9 9.2 %collective-permute-start.7 = (bf16[168,256]{1,0:T(8,128)(2,1)}, bf16[168,256]{1,0:T(8,128)(2,1)}, u32[]{:S(2)}, u32[]{:S(2)}) collective-permute-start(bf16[168,256]{1,0:T(8,128)(2,1)} %fusion.34), channel_id=1, source_target_pairs={{0,8},{1,9},{2,10},{3,11},{4,12},{5,13},{6,14},{7,15},{8,0},{9,1},... | collective-permute-start | bytes 258056 | tf_op jit(solution)/shard_map/ppermute | solution.py:84
  266.8 34.7 %copy-start.1 = (bf16[3088,512]{1,0:T(8,128)(2,1)S(1)}, bf16[3088,512]{1,0:T(8,128)(2,1)}, u32[]{:S(2)}) copy-start(bf16[3088,512]{1,0:T(8,128)(2,1)} %param.30) | copy-start | bytes 9486340
  274.0 5.5 %collective-permute-start.8 = (f32[168,256]{1,0:T(8,128)S(1)}, f32[168,256]{1,0:T(8,128)S(1)}, u32[]{:S(2)}, u32[]{:S(2)}) collective-permute-start(f32[168,256]{1,0:T(8,128)S(1)} %bitcast_add_fusion.3), channel_id=1, source_target_pairs={{0,128},{128,0},{1,129},{129,1},{2,130},{130,2},{3,131},{131,3},{4... | collective-permute-start | bytes 516104 | tf_op jit(solution)/shard_map/ppermute | solution.py:94
  279.5 7.0 %collective-permute-start.9 = (f32[168,256]{1,0:T(8,128)S(1)}, f32[168,256]{1,0:T(8,128)S(1)}, u32[]{:S(2)}, u32[]{:S(2)}) collective-permute-start(f32[168,256]{1,0:T(8,128)S(1)} %add.272), channel_id=1, source_target_pairs={{0,16},{16,0},{32,48},{48,32},{64,80},{80,64},{96,112},{112,96},{1... | collective-permute-start | bytes 516104 | tf_op jit(solution)/shard_map/ppermute | solution.py:94
  286.5 6.6 %collective-permute-start.10 = (f32[168,256]{1,0:T(8,128)S(1)}, f32[168,256]{1,0:T(8,128)S(1)}, u32[]{:S(2)}, u32[]{:S(2)}) collective-permute-start(f32[168,256]{1,0:T(8,128)S(1)} %add.273), channel_id=1, source_target_pairs={{0,32},{16,48},{32,0},{48,16},{64,96},{80,112},{96,64},{112,80},{1... | collective-permute-start | bytes 516104 | tf_op jit(solution)/shard_map/ppermute | solution.py:94
  293.2 7.0 %collective-permute-start.11 = (f32[168,256]{1,0:T(8,128)S(1)}, f32[168,256]{1,0:T(8,128)S(1)}, u32[]{:S(2)}, u32[]{:S(2)}) collective-permute-start(f32[168,256]{1,0:T(8,128)S(1)} %add.274), channel_id=1, source_target_pairs={{0,64},{16,80},{32,96},{48,112},{64,0},{80,16},{96,32},{112,48},{1... | collective-permute-start | bytes 516104 | tf_op jit(solution)/shard_map/ppermute | solution.py:94
  (1 other events, 0.9 us)
Sparse Core Ops, SparseCore 0:
  9.9 140.6 all-gather.5
  152.4 40.3 all-gather.3

commit v4 on v3

--- a/solution.py
+++ b/solution.py
@@ -84,6 +84,19 @@
         got = lax.ppermute(send.astype(wire_types[k]), axis, xor_pairs(size, 1 << k))
         buf = keep + got.astype(keep.dtype)
     return buf
+
+
+def doubling_gather(value, axis):
+    size = lax.axis_size(axis)
+    me = lax.axis_index(axis)
+    bits = size.bit_length() - 1
+    assert 1 << bits == size
+    held = value[None]
+    for k in reversed(range(bits)):
+        held = jnp.concatenate([held, lax.ppermute(held, axis, xor_pairs(size, 1 << k))], axis=0)
+    wanted = jnp.arange(size) ^ me
+    position = sum(((wanted >> k) & 1) << (bits - 1 - k) for k in range(bits))
+    return jnp.take(held, position, axis=0)
 
 
 def doubling_sum(value, axis):
@@ -139,11 +152,11 @@
     x_clean = noisy.astype(jnp.float32) - level * eps_pred
     theta, path_east, path_north = local_path(x_clean)
     normed_e, scale_rms = embed(x_clean, path_east, path_north, w_embed, root_rows)
-    w_all, proj_send, emb_b, text_raw = lax.optimization_barrier(
-        (w_all, w_proj, normed_e.astype(jnp.bfloat16), text_raw)
+    proj_b = doubling_gather(w_proj, "seq").reshape(ways * w_proj.shape[0], w_proj.shape[1])
+    w_all, proj_b, emb_b, text_raw = lax.optimization_barrier(
+        (w_all, proj_b, normed_e.astype(jnp.bfloat16), text_raw)
     )
     text_unit, text_len = unit_rows(text_raw)
-    proj_b = lax.all_gather(proj_send, "seq", axis=0, tiled=True)
     proj_rows = proj_b.astype(jnp.float32)
     projected = jnp.einsum(
         "cfd,hjdk->cfhjk",

time: 310 us -> 314 us (1.013)
  local copies, waits for them, and re-layouts: 15.2 us -> 25.2 us
  waiting for transfers between devices: 183 us -> 174 us
  other arithmetic: 19.7 us -> 23.8 us
    all_gather x1, waiting for transfers between devices: 107 us -> 59 us  [local(): w_all = lax.all_gather(w_qkv, 'seq', axis=0)]
    ppermute x0 -> x4, waiting for transfers between devices: none -> 46 us  [doubling_gather(): lax.ppermute(held, axis, xor_pairs(size, 1 << k))]
    all_gather x1 -> x0, waiting for transfers between devices: 19.6 us -> none  [local(): proj_b = lax.all_gather(proj_send, 'seq', axis=0, tiled=True)]
    ppermute x8, waiting for transfers between devices: 29.1 us -> 39.1 us  [doubling_sum(): value = value + lax.ppermute(value, axis, xor_pairs(size, 1 << k))]
    ppermute x0 -> x4, starting transfers between devices: none -> 9.25 us  [doubling_gather(): lax.ppermute(held, axis, xor_pairs(size, 1 << k))]
    ppermute x8, starting transfers between devices: 20 us -> 13 us  [doubling_sum(): value = value + lax.ppermute(value, axis, xor_pairs(size, 1 << k))]
    unnamed x40 -> x86, local copies, waits for them, and re-layouts: 2.82 us -> 7.57 us
  transfers between devices with their start and end apart: 14 -> 17, of which waited for: 13 -> 15; matrix products, arithmetic and copies ran while one was open for 11% -> 7% of each run, Pallas kernels for 0% -> 0%
where the time goes in v4:
time: 314 us; the launch traced here: 313 us
  waiting for transfers between devices  174 us (55%)
  matrix products  47 us (15%)
  starting transfers between devices  26.1 us (8%)
  local copies, waits for them, and re-layouts  25.2 us (8%)
  other arithmetic  23.8 us (8%)
  between operations  17.3 us (6%)
    all_gather x1, waiting for transfers between devices, local(): w_all = lax.all_gather(w_qkv, 'seq', axis=0)  59 us
    ppermute x4, waiting for transfers between devices, doubling_gather(): lax.ppermute(held, axis, xor_pairs(size, 1 << k))  46 us
    ppermute x8, waiting for transfers between devices, doubling_sum(): value = value + lax.ppermute(value, axis, xor_pairs(size, 1 << k))  39.1 us
    ppermute x4, waiting for transfers between devices, halving_sum(): lax.ppermute(send.astype(wire_types[k]), axis, xor_pairs(size, 1 << k))  29.2 us
    dot_general x1, matrix products, local(): jnp.einsum('cfd,hjdk->cfhjk', emb_b, w_all, preferred_element_type=jnp.fl...  14.6 us
    dot_general x1, matrix products, local(): jnp.einsum('cfhjk,hjdk->cfd', d_proj, w_all, preferred_element_type=jnp.f...  13.8 us
    ppermute x8, starting transfers between devices, doubling_sum(): value = value + lax.ppermute(value, axis, xor_pairs(size, 1 << k))  13 us
    ppermute x4, starting transfers between devices, doubling_gather(): lax.ppermute(held, axis, xor_pairs(size, 1 << k))  9.25 us
  transfers between devices with their start and end apart: 17, of which 15 were waited for; matrix products, arithmetic and copies ran while one was open for 7% of the time, Pallas kernels for 0%

profile of v4, /device:TPU:6, one launch (start us, length us, event | category | flops | bytes accessed | tf_op | source)
XLA Modules:
  0.0 313.5 jit_solution(16493742711278210383)
XLA Ops:
  9.1 5.1 %gather_fusion.1 = bf16[1024,512]{1,0:T(8,128)(2,1)} fusion(bf16[3088,512]{1,0:T(8,128)(2,1)S(1)} %copy-done, s32[1024]{0:T(1024)S(1)} %broadcast_clamp_fusion), kind=kCustom, calls=%fused_computation.1 | custom fusion | bytes 2101248 | tf_op jit(solution)/shard_map/jit(_take)/gather | solution.py:137
  14.2 1.8 select_reduce_fusion
  16.0 7.3 %collective-permute-start = (bf16[1,128,512]{2,1,0:T(8,128)(2,1)S(1)}, bf16[1,128,512]{2,1,0:T(8,128)(2,1)S(1)}, u32[]{:S(2)}, u32[]{:S(2)}) collective-permute-start(bf16[1,128,512]{2,1,0:T(8,128)(2,1)S(1)} %bitcast.218), channel_id=1, source_target_pairs={{0,8},{1,9},{2,10},{3,11},{4,12},{5,13},{6,14},{7,15},{8,0},{9,1},... | collective-permute-start | bytes 393224 | tf_op jit(solution)/shard_map/ppermute | solution.py:96
  28.2 3.4 %collective-permute-done = bf16[1,128,512]{2,1,0:T(8,128)(2,1)S(1)} collective-permute-done((bf16[1,128,512]{2,1,0:T(8,128)(2,1)S(1)}, bf16[1,128,512]{2,1,0:T(8,128)(2,1)S(1)}, u32[]{:S(2)}, u32[]{:S(2)}) %collective-permute-start) | collective-permute-done | bytes 131104 | tf_op jit(solution)/shard_map/ppermute | solution.py:96
  31.6 1.9 collective-permute-start.1
  34.0 18.1 %collective-permute-done.1 = bf16[2,128,512]{2,1,0:T(8,128)(2,1)S(1)} collective-permute-done((bf16[2,128,512]{2,1,0:T(8,128)(2,1)S(1)}, bf16[2,128,512]{2,1,0:T(8,128)(2,1)S(1)}, u32[]{:S(2)}, u32[]{:S(2)}) %collective-permute-start.1) | collective-permute-done | bytes 262176 | tf_op jit(solution)/shard_map/ppermute | solution.py:96
  53.2 24.5 %collective-permute-done.2 = bf16[4,128,512]{2,1,0:T(8,128)(2,1)S(1)} collective-permute-done((bf16[4,128,512]{2,1,0:T(8,128)(2,1)S(1)}, bf16[4,128,512]{2,1,0:T(8,128)(2,1)S(1)}, u32[]{:S(2)}, u32[]{:S(2)}) %collective-permute-start.2) | collective-permute-done | bytes 524320 | tf_op jit(solution)/shard_map/ppermute | solution.py:96
  81.6 6.1 %collective-permute-done.5 = f32[32,512]{1,0:T(8,128)S(1)} collective-permute-done((f32[32,512]{1,0:T(8,128)S(1)}, f32[32,512]{1,0:T(8,128)S(1)}, u32[]{:S(2)}, u32[]{:S(2)}) %collective-permute-start.5) | collective-permute-done | bytes 65568 | tf_op jit(solution)/shard_map/ppermute | solution.py:107
  87.8 7.8 %collective-permute-done.6 = f32[32,512]{1,0:T(8,128)S(1)} collective-permute-done((f32[32,512]{1,0:T(8,128)S(1)}, f32[32,512]{1,0:T(8,128)S(1)}, u32[]{:S(2)}, u32[]{:S(2)}) %collective-permute-start.6) | collective-permute-done | bytes 65568 | tf_op jit(solution)/shard_map/ppermute | solution.py:107
  95.6 6.8 %collective-permute-start.7 = (f32[32,512]{1,0:T(8,128)S(1)}, f32[32,512]{1,0:T(8,128)S(1)}, u32[]{:S(2)}, u32[]{:S(2)}) collective-permute-start(f32[32,512]{1,0:T(8,128)S(1)} %add.310), channel_id=1, source_target_pairs={{0,8},{1,9},{2,10},{3,11},{4,12},{5,13},{6,14},{7,15},{8,0},{9,1},... | collective-permute-start | bytes 196616 | tf_op jit(solution)/shard_map/ppermute | solution.py:107
  103.1 4.3 %collective-permute-done.7 = f32[32,512]{1,0:T(8,128)S(1)} collective-permute-done((f32[32,512]{1,0:T(8,128)S(1)}, f32[32,512]{1,0:T(8,128)S(1)}, u32[]{:S(2)}, u32[]{:S(2)}) %collective-permute-start.7) | collective-permute-done | bytes 65568 | tf_op jit(solution)/shard_map/ppermute | solution.py:107
  110.1 2.3 gather_fusion
  112.4 1.8 bitcast_select_fusion
  114.2 59.0 %all-gather.3.cloned.1.call-done = bf16[48,2048,128]{2,1,0:T(8,128)(2,1)} async-done(((bf16[3,2048,128]{2,1,0:T(8,128)(2,1)}), bf16[48,2048,128]{2,1,0:T(8,128)(2,1)}) %all-gather.3.cloned.1.call-update) | async-done | bytes 25165840 | tf_op jit(solution)/shard_map/all_gather | solution.py:142
  173.3 14.6 %convolution_bitcast_fusion.1 = f32[1,128,16,3,128]{1,4,3,2,0:T(8,128)S(1)} fusion(bf16[16,3,2048,128]{3,2,1,0:T(8,128)(2,1)} %bitcast.213, bf16[1,128,2048]{2,1,0:T(8,128)(2,1)} %convert_bitcast_fusion), kind=kOutput, calls=%fused_computation.10 | convolution fusion | flops 3221225472 | bytes 28835840 | tf_op jit(solution)/shard_map/cfd,hjdk->cfhjk/dot_general | solution.py:161
  189.5 2.6 convert_reduce_fusion.1
  193.9 2.0 fusion.65
  197.8 3.4 %fusion.66 = f32[1,2048]{1,0:T(1,128)S(1)} fusion(f32[512,1]{0,1:T(1,128)S(1)} %bitcast.235, bf16[2048,512]{1,0:T(8,128)(2,1)} %bitcast_select_fusion), kind=kOutput, calls=%fused_computation.170 | convolution fusion | flops 12582912 | bytes 2107392 | tf_op jit(solution)/shard_map/dot_general | solution.py:197
  206.9 13.8 %multiply_reduce_fusion = (f32[128]{0:T(128)S(1)}, f32[128,2048]{1,0:T(8,128)S(1)}) fusion(f32[128,2048]{1,0:T(8,128)} %copy-done.5, f32[128]{0:T(128)S(1)} %copy-done.28, bf16[16,3,2048,128]{3,2,1,0:T(8,128)(2,1)} %bitcast.214, bf16[128,16,1,128]{0,3,1,2:T(8,128)(2,1)} %multiply_convert_fusion, bf16[128,16,1,128]{0,3,1,2:T(8,128)(2,1)} %get-tuple-element.68, ...), kind=kOutput, calls=%fused_computation.50 | convolution fusion | flops 3223584768 | bytes 28836864 | tf_op jit(solution)/shard_map/cfhjk,hjdk->cfd/dot_general | solution.py:225
  222.8 2.0 fusion.55
  225.2 2.5 fusion.67
  229.9 2.0 fusion.12
  239.2 3.1 collective-permute-done.8
  245.7 9.6 %collective-permute-done.9 = bf16[2,2,168,256]{3,2,0,1:T(8,128)(2,1)S(1)} collective-permute-done((bf16[2,2,168,256]{3,2,0,1:T(8,128)(2,1)S(1)}, bf16[2,2,168,256]{3,2,0,1:T(8,128)(2,1)S(1)}, u32[]{:S(2)}, u32[]{:S(2)}) %collective-permute-start.9) | collective-permute-done | bytes 344096 | tf_op jit(solution)/shard_map/ppermute | solution.py:84
  257.4 9.4 %collective-permute-done.10 = bf16[2,168,256]{2,1,0:T(8,128)(2,1)} collective-permute-done((bf16[2,168,256]{2,1,0:T(8,128)(2,1)S(1)}, bf16[2,168,256]{2,1,0:T(8,128)(2,1)}, u32[]{:S(2)}, u32[]{:S(2)}) %collective-permute-start.10) | collective-permute-done | bytes 172064 | tf_op jit(solution)/shard_map/ppermute | solution.py:84
  268.7 1.8 collective-permute-start.11
  270.5 7.1 %collective-permute-done.11 = bf16[168,256]{1,0:T(8,128)(2,1)} collective-permute-done((bf16[168,256]{1,0:T(8,128)(2,1)}, bf16[168,256]{1,0:T(8,128)(2,1)}, u32[]{:S(2)}, u32[]{:S(2)}) %collective-permute-start.11) | collective-permute-done | bytes 86048 | tf_op jit(solution)/shard_map/ppermute | solution.py:84
  280.0 4.1 %collective-permute-done.12 = f32[168,256]{1,0:T(8,128)S(1)} collective-permute-done((f32[168,256]{1,0:T(8,128)S(1)}, f32[168,256]{1,0:T(8,128)S(1)}, u32[]{:S(2)}, u32[]{:S(2)}) %collective-permute-start.12) | collective-permute-done | bytes 172064 | tf_op jit(solution)/shard_map/ppermute | solution.py:107
  284.2 3.1 collective-permute-start.13
  287.4 3.9 %collective-permute-done.13 = f32[168,256]{1,0:T(8,128)S(1)} collective-permute-done((f32[168,256]{1,0:T(8,128)S(1)}, f32[168,256]{1,0:T(8,128)S(1)}, u32[]{:S(2)}, u32[]{:S(2)}) %collective-permute-start.13) | collective-permute-done | bytes 172064 | tf_op jit(solution)/shard_map/ppermute | solution.py:107
  292.2 6.1 %collective-permute-done.14 = f32[168,256]{1,0:T(8,128)S(1)} collective-permute-done((f32[168,256]{1,0:T(8,128)S(1)}, f32[168,256]{1,0:T(8,128)S(1)}, u32[]{:S(2)}, u32[]{:S(2)}) %collective-permute-start.14) | collective-permute-done | bytes 172064 | tf_op jit(solution)/shard_map/ppermute | solution.py:107
  298.4 6.9 %collective-permute-done.15 = f32[168,256]{1,0:T(8,128)S(1)} collective-permute-done((f32[168,256]{1,0:T(8,128)S(1)}, f32[168,256]{1,0:T(8,128)S(1)}, u32[]{:S(2)}, u32[]{:S(2)}) %collective-permute-start.15) | collective-permute-done | bytes 172064 | tf_op jit(solution)/shard_map/ppermute | solution.py:107
  (193 shorter events, 48.1 us)
Async XLA Ops:
  7.2 166.0 %all-gather.3.cloned.1.call-start = ((), (), s32[]{:S(2)}) async-start(), calls=%async_computation | async-start | bytes 26738688 | tf_op jit(solution)/shard_map/all_gather | solution.py:142
  9.1 14.9 %copy-start.23 = (bf16[1,2560]{1,0:T(2,128)(2,1)S(1)}, bf16[1,2560]{1,0:T(2,128)(2,1)}, u32[]{:S(2)}) copy-start(bf16[1,2560]{1,0:T(2,128)(2,1)} %param.21) | copy-start | bytes 15364
  9.1 14.9 %copy-start.24 = (bf16[1,2560]{1,0:T(2,128)(2,1)S(1)}, bf16[1,2560]{1,0:T(2,128)(2,1)}, u32[]{:S(2)}) copy-start(bf16[1,2560]{1,0:T(2,128)(2,1)} %param.22) | copy-start | bytes 15364
  14.2 9.9 %copy-start.2 = (bf16[1,128,2560]{2,1,0:T(8,128)(2,1)S(1)}, bf16[1,128,2560]{2,1,0:T(8,128)(2,1)}, u32[]{:S(2)}) copy-start(bf16[1,128,2560]{2,1,0:T(8,128)(2,1)} %param.20) | copy-start | bytes 1966084
  14.2 11.0 %copy-start.12 = (bf16[2560,256]{1,0:T(8,128)(2,1)S(1)}, bf16[2560,256]{1,0:T(8,128)(2,1)}, u32[]{:S(2)}) copy-start(bf16[2560,256]{1,0:T(8,128)(2,1)} %param.25) | copy-start | bytes 3932164
  14.2 11.0 %copy-start.37 = (bf16[1,128,256]{2,1,0:T(8,128)(2,1)S(1)}, bf16[1,128,256]{2,1,0:T(8,128)(2,1)}, u32[]{:S(2)}) copy-start(bf16[1,128,256]{2,1,0:T(8,128)(2,1)} %param.23) | copy-start | bytes 196612
  15.9 65.5 %collective-permute-start.4 = (f32[32,512]{1,0:T(8,128)S(1)}, f32[32,512]{1,0:T(8,128)S(1)}, u32[]{:S(2)}, u32[]{:S(2)}) collective-permute-start(f32[32,512]{1,0:T(8,128)S(1)} %select_reduce_fusion), channel_id=1, source_target_pairs={{0,1},{1,0},{2,3},{3,2},{4,5},{5,4},{6,7},{7,6},{8,9},{9,8},{10,11... | collective-permute-start | bytes 196616 | tf_op jit(solution)/shard_map/ppermute | solution.py:107
  16.0 15.6 %collective-permute-start = (bf16[1,128,512]{2,1,0:T(8,128)(2,1)S(1)}, bf16[1,128,512]{2,1,0:T(8,128)(2,1)S(1)}, u32[]{:S(2)}, u32[]{:S(2)}) collective-permute-start(bf16[1,128,512]{2,1,0:T(8,128)(2,1)S(1)} %bitcast.218), channel_id=1, source_target_pairs={{0,8},{1,9},{2,10},{3,11},{4,12},{5,13},{6,14},{7,15},{8,0},{9,1},... | collective-permute-start | bytes 393224 | tf_op jit(solution)/shard_map/ppermute | solution.py:96
  25.7 7.8 %copy-start.13 = (bf16[256,2048]{1,0:T(8,128)(2,1)S(1)}, bf16[256,2048]{1,0:T(8,128)(2,1)}, u32[]{:S(2)}) copy-start(bf16[256,2048]{1,0:T(8,128)(2,1)} %param.26) | copy-start | bytes 3145732
  27.0 7.0 %copy-start.33 = (f32[1,128]{1,0:T(1,128)}, f32[1,128]{1,0:T(1,128)S(1)}, u32[]{:S(2)}) copy-start(f32[1,128]{1,0:T(1,128)S(1)} %reduce_window_sum.30) | copy-start | bytes 1540
  31.6 20.4 %collective-permute-start.1 = (bf16[2,128,512]{2,1,0:T(8,128)(2,1)S(1)}, bf16[2,128,512]{2,1,0:T(8,128)(2,1)S(1)}, u32[]{:S(2)}, u32[]{:S(2)}) collective-permute-start(bf16[2,128,512]{2,1,0:T(8,128)(2,1)S(1)} %pad_maximum_fusion.4), channel_id=1, source_target_pairs={{0,4},{1,5},{2,6},{3,7},{4,0},{5,1},{6,2},{7,3},{8,12},{9,13},{10,... | collective-permute-start | bytes 786440 | tf_op jit(solution)/shard_map/ppermute | solution.py:96
  34.0 44.8 %copy-start.5 = (f32[128,2048]{1,0:T(8,128)}, f32[128,2048]{1,0:T(8,128)S(1)}, u32[]{:S(2)}) copy-start(f32[128,2048]{1,0:T(8,128)S(1)} %get-tuple-element.84) | copy-start | bytes 3145732
  52.1 25.6 %collective-permute-start.2 = (bf16[4,128,512]{2,1,0:T(8,128)(2,1)S(1)}, bf16[4,128,512]{2,1,0:T(8,128)(2,1)S(1)}, u32[]{:S(2)}, u32[]{:S(2)}) collective-permute-start(bf16[4,128,512]{2,1,0:T(8,128)(2,1)S(1)} %pad_maximum_fusion.3), channel_id=1, source_target_pairs={{0,2},{1,3},{2,0},{3,1},{4,6},{5,7},{6,4},{7,5},{8,10},{9,11},{10,... | collective-permute-start | bytes 1572872 | tf_op jit(solution)/shard_map/ppermute | solution.py:96
  52.2 26.6 %copy-start.27 = (f32[128]{0:T(128)}, f32[128]{0:T(128)S(1)}, u32[]{:S(2)}) copy-start(f32[128]{0:T(128)S(1)} %add_sqrt_fusion.3) | copy-start | bytes 1540
  53.2 26.4 %copy-start.38 = (s32[16]{0:T(128)S(1)}, s32[16]{0:T(128)}, u32[]{:S(2)}) copy-start(s32[16]{0:T(128)} %param.32) | copy-start | bytes 196
  53.2 27.0 %copy-start.39 = (f32[16]{0:T(128)S(1)}, f32[16]{0:T(128)}, u32[]{:S(2)}) copy-start(f32[16]{0:T(128)} %param.33) | copy-start | bytes 196
  78.8 30.2 %collective-permute-start.3 = (bf16[8,128,512]{2,1,0:T(8,128)(2,1)}, bf16[8,128,512]{2,1,0:T(8,128)(2,1)S(1)}, u32[]{:S(2)}, u32[]{:S(2)}) collective-permute-start(bf16[8,128,512]{2,1,0:T(8,128)(2,1)} %pad_maximum_fusion.2), channel_id=1, source_target_pairs={{0,1},{1,0},{2,3},{3,2},{4,5},{5,4},{6,7},{7,6},{8,9},{9,8},{10,11... | collective-permute-start | bytes 3145736 | tf_op jit(solution)/shard_map/ppermute | solution.py:96
  81.4 6.3 %collective-permute-start.5 = (f32[32,512]{1,0:T(8,128)S(1)}, f32[32,512]{1,0:T(8,128)S(1)}, u32[]{:S(2)}, u32[]{:S(2)}) collective-permute-start(f32[32,512]{1,0:T(8,128)S(1)} %add.308), channel_id=1, source_target_pairs={{0,2},{1,3},{2,0},{3,1},{4,6},{5,7},{6,4},{7,5},{8,10},{9,11},{10,... | collective-permute-start | bytes 196616 | tf_op jit(solution)/shard_map/ppermute | solution.py:107
  87.7 7.9 %collective-permute-start.6 = (f32[32,512]{1,0:T(8,128)S(1)}, f32[32,512]{1,0:T(8,128)S(1)}, u32[]{:S(2)}, u32[]{:S(2)}) collective-permute-start(f32[32,512]{1,0:T(8,128)S(1)} %add.309), channel_id=1, source_target_pairs={{0,4},{1,5},{2,6},{3,7},{4,0},{5,1},{6,2},{7,3},{8,12},{9,13},{10,... | collective-permute-start | bytes 196616 | tf_op jit(solution)/shard_map/ppermute | solution.py:107
  95.6 11.7 %collective-permute-start.7 = (f32[32,512]{1,0:T(8,128)S(1)}, f32[32,512]{1,0:T(8,128)S(1)}, u32[]{:S(2)}, u32[]{:S(2)}) collective-permute-start(f32[32,512]{1,0:T(8,128)S(1)} %add.310), channel_id=1, source_target_pairs={{0,8},{1,9},{2,10},{3,11},{4,12},{5,13},{6,14},{7,15},{8,0},{9,1},... | collective-permute-start | bytes 196616 | tf_op jit(solution)/shard_map/ppermute | solution.py:107
  206.9 13.9 %copy-start.6 = (f32[128,2048]{1,0:T(8,128)S(1)}, f32[128,2048]{1,0:T(8,128)}, u32[]{:S(2)}) copy-start(f32[128,2048]{1,0:T(8,128)} %copy-done.5) | copy-start | bytes 3145732
  206.9 13.9 %copy-start.18 = (f32[1,2048]{1,0:T(1,128)S(1)}, f32[1,2048]{1,0:T(1,128)}, u32[]{:S(2)}) copy-start(f32[1,2048]{1,0:T(1,128)} %copy-done.17) | copy-start | bytes 24580
  206.9 13.9 %copy-start.20 = (f32[1,2048]{1,0:T(1,128)S(1)}, f32[1,2048]{1,0:T(1,128)}, u32[]{:S(2)}) copy-start(f32[1,2048]{1,0:T(1,128)} %copy-done.19) | copy-start | bytes 24580
  239.0 3.3 %collective-permute-start.8 = (f32[2,2,2,168,256]{4,3,0,1,2:T(8,128)}, f32[2,2,2,168,256]{4,3,0,1,2:T(8,128)S(1)}, u32[]{:S(2)}, u32[]{:S(2)}) collective-permute-start(f32[2,2,2,168,256]{4,3,0,1,2:T(8,128)} %bitcast.211), channel_id=1, source_target_pairs={{0,1},{1,0},{2,3},{3,2},{4,5},{5,4},{6,7},{7,6},{8,9},{9,8},{10,11... | collective-permute-start | bytes 4128776 | tf_op jit(solution)/shard_map/ppermute | solution.py:84
  245.0 10.3 %collective-permute-start.9 = (bf16[2,2,168,256]{3,2,0,1:T(8,128)(2,1)S(1)}, bf16[2,2,168,256]{3,2,0,1:T(8,128)(2,1)S(1)}, u32[]{:S(2)}, u32[]{:S(2)}) collective-permute-start(bf16[2,2,168,256]{3,2,0,1:T(8,128)(2,1)S(1)} %fusion.28), channel_id=1, source_target_pairs={{0,2},{1,3},{2,0},{3,1},{4,6},{5,7},{6,4},{7,5},{8,10},{9,11},{10,... | collective-permute-start | bytes 1032200 | tf_op jit(solution)/shard_map/ppermute | solution.py:84
  256.3 10.5 %collective-permute-start.10 = (bf16[2,168,256]{2,1,0:T(8,128)(2,1)S(1)}, bf16[2,168,256]{2,1,0:T(8,128)(2,1)}, u32[]{:S(2)}, u32[]{:S(2)}) collective-permute-start(bf16[2,168,256]{2,1,0:T(8,128)(2,1)S(1)} %fusion.33), channel_id=1, source_target_pairs={{0,4},{1,5},{2,6},{3,7},{4,0},{5,1},{6,2},{7,3},{8,12},{9,13},{10,... | collective-permute-start | bytes 516104 | tf_op jit(solution)/shard_map/ppermute | solution.py:84
  266.8 39.8 %copy-start.1 = (bf16[3088,512]{1,0:T(8,128)(2,1)S(1)}, bf16[3088,512]{1,0:T(8,128)(2,1)}, u32[]{:S(2)}) copy-start(bf16[3088,512]{1,0:T(8,128)(2,1)} %param.30) | copy-start | bytes 9486340
  268.7 8.9 %collective-permute-start.11 = (bf16[168,256]{1,0:T(8,128)(2,1)}, bf16[168,256]{1,0:T(8,128)(2,1)}, u32[]{:S(2)}, u32[]{:S(2)}) collective-permute-start(bf16[168,256]{1,0:T(8,128)(2,1)} %fusion.34), channel_id=1, source_target_pairs={{0,8},{1,9},{2,10},{3,11},{4,12},{5,13},{6,14},{7,15},{8,0},{9,1},... | collective-permute-start | bytes 258056 | tf_op jit(solution)/shard_map/ppermute | solution.py:84
  278.5 5.7 %collective-permute-start.12 = (f32[168,256]{1,0:T(8,128)S(1)}, f32[168,256]{1,0:T(8,128)S(1)}, u32[]{:S(2)}, u32[]{:S(2)}) collective-permute-start(f32[168,256]{1,0:T(8,128)S(1)} %bitcast_add_fusion.3), channel_id=1, source_target_pairs={{0,128},{128,0},{1,129},{129,1},{2,130},{130,2},{3,131},{131,3},{4... | collective-permute-start | bytes 516104 | tf_op jit(solution)/shard_map/ppermute | solution.py:107
  284.2 7.0 %collective-permute-start.13 = (f32[168,256]{1,0:T(8,128)S(1)}, f32[168,256]{1,0:T(8,128)S(1)}, u32[]{:S(2)}, u32[]{:S(2)}) collective-permute-start(f32[168,256]{1,0:T(8,128)S(1)} %add.337), channel_id=1, source_target_pairs={{0,16},{16,0},{32,48},{48,32},{64,80},{80,64},{96,112},{112,96},{1... | collective-permute-start | bytes 516104 | tf_op jit(solution)/shard_map/ppermute | solution.py:107
  291.2 7.0 %collective-permute-start.14 = (f32[168,256]{1,0:T(8,128)S(1)}, f32[168,256]{1,0:T(8,128)S(1)}, u32[]{:S(2)}, u32[]{:S(2)}) collective-permute-start(f32[168,256]{1,0:T(8,128)S(1)} %add.338), channel_id=1, source_target_pairs={{0,32},{16,48},{32,0},{48,16},{64,96},{80,112},{96,64},{112,80},{1... | collective-permute-start | bytes 516104 | tf_op jit(solution)/shard_map/ppermute | solution.py:107
  298.3 7.0 %collective-permute-start.15 = (f32[168,256]{1,0:T(8,128)S(1)}, f32[168,256]{1,0:T(8,128)S(1)}, u32[]{:S(2)}, u32[]{:S(2)}) collective-permute-start(f32[168,256]{1,0:T(8,128)S(1)} %add.339), channel_id=1, source_target_pairs={{0,64},{16,80},{32,96},{48,112},{64,0},{80,16},{96,32},{112,48},{1... | collective-permute-start | bytes 516104 | tf_op jit(solution)/shard_map/ppermute | solution.py:107
  (25 other events, 68.2 us)
Sparse Core Ops, SparseCore 0:
  9.9 163.2 all-gather.2

commit v5 on v3

--- a/solution.py
+++ b/solution.py
@@ -84,6 +84,20 @@
         got = lax.ppermute(send.astype(wire_types[k]), axis, xor_pairs(size, 1 << k))
         buf = keep + got.astype(keep.dtype)
     return buf
+
+
+def quad_sum(value, axes, low_bit, high_bit):
+    size = 1
+    for axis in axes:
+        size *= lax.axis_size(axis)
+    me = 0
+    for axis in axes:
+        me = me * lax.axis_size(axis) + lax.axis_index(axis)
+    offsets = [0, 1 << low_bit, 1 << high_bit, (1 << low_bit) | (1 << high_bit)]
+    vals = [value] + [lax.ppermute(value, axes, xor_pairs(size, d)) for d in offsets[1:]]
+    position = ((me >> low_bit) & 1) + 2 * ((me >> high_bit) & 1)
+    members = jnp.take(jnp.stack(vals), jnp.arange(4) ^ position, axis=0)
+    return (members[0] + members[1]) + (members[2] + members[3])
 
 
 def doubling_sum(value, axis):
@@ -245,7 +259,10 @@
     )
     seq_bits = ways.bit_length() - 1
     block = halving_sum(stacked, "seq", [jnp.float32] + [jnp.bfloat16] * (seq_bits - 1))
-    block = doubling_sum(doubling_sum(block, "sec"), "dp")
+    if lax.axis_size("sec") * lax.axis_size("dp") == 16:
+        block = quad_sum(quad_sum(block, ("sec", "dp"), 1, 3), ("sec", "dp"), 0, 2)
+    else:
+        block = doubling_sum(doubling_sum(block, "sec"), "dp")
     grad_w_out = block[:rows_dev]
     group_first = (lax.axis_index("sec") * n_dp + lax.axis_index("dp")) * ways * clips_dev
     all_rewards = block[rows_dev:].reshape(extra * cols)

time: 310 us -> 311 us (level)
  waiting for transfers between devices: 183 us -> 178 us
    ppermute x8 -> x4, waiting for transfers between devices: 29.1 us -> 10.2 us  [doubling_sum(): value = value + lax.ppermute(value, axis, xor_pairs(size, 1 << k))]
    ppermute x0 -> x6, waiting for transfers between devices: none -> 13.6 us  [quad_sum(): lax.ppermute(value, axes, xor_pairs(size, d))]
    ppermute x0 -> x6, starting transfers between devices: none -> 10.2 us  [quad_sum(): lax.ppermute(value, axes, xor_pairs(size, d))]
    ppermute x8 -> x4, starting transfers between devices: 20 us -> 12.8 us  [doubling_sum(): value = value + lax.ppermute(value, axis, xor_pairs(size, 1 << k))]
    gather x0 -> x2, local copies, waits for them, and re-layouts: none -> 3.28 us  [quad_sum(): members = jnp.take(jnp.stack(vals), jnp.arange(4) ^ position, axis=0)]
  transfers between devices with their start and end apart: 14 -> 16, of which waited for: 13 -> 14; matrix products, arithmetic and copies ran while one was open for 11% -> 11% of each run, Pallas kernels for 0% -> 0%
where the time goes in v5:
time: 311 us; the launch traced here: 309 us
  waiting for transfers between devices  178 us (57%)
  matrix products  45.8 us (15%)
  starting transfers between devices  29.2 us (9%)
  other arithmetic  22.3 us (7%)
  between operations  17.2 us (6%)
  local copies, waits for them, and re-layouts  16.9 us (5%)
    all_gather x1, waiting for transfers between devices, local(): w_all = lax.all_gather(w_qkv, 'seq', axis=0)  107 us
    ppermute x4, waiting for transfers between devices, halving_sum(): lax.ppermute(send.astype(wire_types[k]), axis, xor_pairs(size, 1 << k))  27.2 us
    all_gather x1, waiting for transfers between devices, local(): proj_b = lax.all_gather(proj_send, 'seq', axis=0, tiled=True)  19.6 us
    dot_general x1, matrix products, local(): jnp.einsum('cfd,hjdk->cfhjk', emb_b, w_all, preferred_element_type=jnp.fl...  14.6 us
    dot_general x1, matrix products, local(): jnp.einsum('cfhjk,hjdk->cfd', d_proj, w_all, preferred_element_type=jnp.f...  13.7 us
    ppermute x6, waiting for transfers between devices, quad_sum(): lax.ppermute(value, axes, xor_pairs(size, d))  13.6 us
    ppermute x4, starting transfers between devices, doubling_sum(): value = value + lax.ppermute(value, axis, xor_pairs(size, 1 << k))  12.8 us
    ppermute x4, waiting for transfers between devices, doubling_sum(): value = value + lax.ppermute(value, axis, xor_pairs(size, 1 << k))  10.2 us
  transfers between devices with their start and end apart: 16, of which 14 were waited for; matrix products, arithmetic and copies ran while one was open for 11% of the time, Pallas kernels for 0%

profile of v5, /device:TPU:6, one launch (start us, length us, event | category | flops | bytes accessed | tf_op | source)
XLA Modules:
  0.0 309.2 jit_solution(7859859260145000836)
XLA Ops:
  9.1 5.1 %gather_fusion = bf16[1024,512]{1,0:T(8,128)(2,1)} fusion(bf16[3088,512]{1,0:T(8,128)(2,1)S(1)} %copy-done, s32[1024]{0:T(1024)S(1)} %broadcast_clamp_fusion), kind=kCustom, calls=%fused_computation.2 | custom fusion | bytes 2101248 | tf_op jit(solution)/shard_map/jit(_take)/gather | solution.py:138
  14.2 1.8 select_reduce_fusion
  19.5 2.0 collective-permute-start.1
  22.0 2.3 collective-permute-done.1
  24.3 3.4 %collective-permute-start.2 = (f32[32,512]{1,0:T(8,128)S(1)}, f32[32,512]{1,0:T(8,128)S(1)}, u32[]{:S(2)}, u32[]{:S(2)}) collective-permute-start(f32[32,512]{1,0:T(8,128)S(1)} %add.272), channel_id=1, source_target_pairs={{0,4},{1,5},{2,6},{3,7},{4,0},{5,1},{6,2},{7,3},{8,12},{9,13},{10,... | collective-permute-start | bytes 196616 | tf_op jit(solution)/shard_map/ppermute | solution.py:108
  27.7 5.2 %collective-permute-done.2 = f32[32,512]{1,0:T(8,128)S(1)} collective-permute-done((f32[32,512]{1,0:T(8,128)S(1)}, f32[32,512]{1,0:T(8,128)S(1)}, u32[]{:S(2)}, u32[]{:S(2)}) %collective-permute-start.2) | collective-permute-done | bytes 65568 | tf_op jit(solution)/shard_map/ppermute | solution.py:108
  32.9 7.4 %collective-permute-start.3 = (f32[32,512]{1,0:T(8,128)S(1)}, f32[32,512]{1,0:T(8,128)S(1)}, u32[]{:S(2)}, u32[]{:S(2)}) collective-permute-start(f32[32,512]{1,0:T(8,128)S(1)} %add.273), channel_id=1, source_target_pairs={{0,8},{1,9},{2,10},{3,11},{4,12},{5,13},{6,14},{7,15},{8,0},{9,1},... | collective-permute-start | bytes 196616 | tf_op jit(solution)/shard_map/ppermute | solution.py:108
  41.2 2.7 collective-permute-done.3
  44.0 106.6 %all-gather.6.cloned.1.call-done = bf16[48,2048,128]{2,1,0:T(8,128)(2,1)} async-done(((bf16[3,2048,128]{2,1,0:T(8,128)(2,1)}), bf16[48,2048,128]{2,1,0:T(8,128)(2,1)}) %all-gather.6.cloned.1.call-update) | async-done | bytes 25165840 | tf_op jit(solution)/shard_map/all_gather | solution.py:143
  152.4 14.6 %convolution_bitcast_fusion.1 = f32[1,128,16,3,128]{1,4,3,2,0:T(8,128)S(1)} fusion(bf16[16,3,2048,128]{3,2,1,0:T(8,128)(2,1)} %bitcast.215, bf16[1,128,2048]{2,1,0:T(8,128)(2,1)} %convert_bitcast_fusion), kind=kOutput, calls=%fused_computation.10 | convolution fusion | flops 3221225472 | bytes 28835840 | tf_op jit(solution)/shard_map/cfd,hjdk->cfhjk/dot_general | solution.py:162
  168.5 2.6 convert_reduce_fusion.1
  173.1 19.6 %all-gather.4.cloned.1.call-done = bf16[2048,512]{1,0:T(8,128)(2,1)} async-done(((bf16[128,512]{1,0:T(8,128)(2,1)}), bf16[2048,512]{1,0:T(8,128)(2,1)}) %all-gather.4.cloned.1.call-update) | async-done | bytes 2097168 | tf_op jit(solution)/shard_map/all_gather | solution.py:160
  192.7 2.0 fusion.66
  196.7 3.4 %fusion.67 = f32[1,2048]{1,0:T(1,128)S(1)} fusion(f32[512,1]{0,1:T(1,128)S(1)} %bitcast.241, bf16[2048,512]{1,0:T(8,128)(2,1)} %all-gather.4.cloned.1.call-done), kind=kOutput, calls=%fused_computation.171 | convolution fusion | flops 12582912 | bytes 2107392 | tf_op jit(solution)/shard_map/dot_general | solution.py:198
  204.1 1.6 fusion.26
  205.7 13.7 %multiply_reduce_fusion = (f32[128]{0:T(128)S(1)}, f32[128,2048]{1,0:T(8,128)S(1)}) fusion(f32[128,2048]{1,0:T(8,128)} %copy-done.5, f32[128]{0:T(128)S(1)} %add_sqrt_fusion.3, bf16[16,3,2048,128]{3,2,1,0:T(8,128)(2,1)} %bitcast.216, bf16[128,16,1,128]{0,3,1,2:T(8,128)(2,1)} %multiply_convert_fusion, bf16[128,16,1,128]{0,3,1,2:T(8,128)(2,1)} %get-tuple-element.69, ...), kind=kOutput, calls=%fused_computation.49 | convolution fusion | flops 3223584768 | bytes 28836864 | tf_op jit(solution)/shard_map/cfhjk,hjdk->cfd/dot_general | solution.py:226
  221.4 1.9 fusion.56
  223.8 2.5 fusion.68
  228.4 2.0 fusion.12
  234.6 3.2 %collective-permute-done.4 = f32[2,2,2,168,256]{4,3,2,1,0:T(8,128)} collective-permute-done((f32[2,2,2,168,256]{4,3,2,1,0:T(8,128)}, f32[2,2,2,168,256]{4,3,2,1,0:T(8,128)}, u32[]{:S(2)}, u32[]{:S(2)}) %collective-permute-start.4) | collective-permute-done | bytes 1376288 | tf_op jit(solution)/shard_map/ppermute | solution.py:84
  241.4 9.4 %collective-permute-done.5 = bf16[2,2,168,256]{3,2,1,0:T(8,128)(2,1)S(1)} collective-permute-done((bf16[2,2,168,256]{3,2,1,0:T(8,128)(2,1)S(1)}, bf16[2,2,168,256]{3,2,1,0:T(8,128)(2,1)S(1)}, u32[]{:S(2)}, u32[]{:S(2)}) %collective-permute-start.5) | collective-permute-done | bytes 344096 | tf_op jit(solution)/shard_map/ppermute | solution.py:84
  252.0 1.8 collective-permute-start.6
  253.9 8.7 %collective-permute-done.6 = bf16[2,168,256]{2,1,0:T(8,128)(2,1)S(1)} collective-permute-done((bf16[2,168,256]{2,1,0:T(8,128)(2,1)S(1)}, bf16[2,168,256]{2,1,0:T(8,128)(2,1)S(1)}, u32[]{:S(2)}, u32[]{:S(2)}) %collective-permute-start.6) | collective-permute-done | bytes 172064 | tf_op jit(solution)/shard_map/ppermute | solution.py:84
  262.6 3.0 collective-permute-start.7
  265.6 6.0 %collective-permute-done.7 = bf16[168,256]{1,0:T(8,128)(2,1)S(1)} collective-permute-done((bf16[168,256]{1,0:T(8,128)(2,1)S(1)}, bf16[168,256]{1,0:T(8,128)(2,1)S(1)}, u32[]{:S(2)}, u32[]{:S(2)}) %collective-permute-start.7) | collective-permute-done | bytes 86048 | tf_op jit(solution)/shard_map/ppermute | solution.py:84
  275.2 3.4 %collective-permute-done.8 = f32[168,256]{1,0:T(8,128)S(1)} collective-permute-done((f32[168,256]{1,0:T(8,128)S(1)}, f32[168,256]{1,0:T(8,128)S(1)}, u32[]{:S(2)}, u32[]{:S(2)}) %collective-permute-start.8) | collective-permute-done | bytes 172064 | tf_op jit(solution)/shard_map/ppermute | solution.py:97
  278.5 3.3 %collective-permute-done.9 = f32[168,256]{1,0:T(8,128)S(1)} collective-permute-done((f32[168,256]{1,0:T(8,128)S(1)}, f32[168,256]{1,0:T(8,128)S(1)}, u32[]{:S(2)}, u32[]{:S(2)}) %collective-permute-start.9) | collective-permute-done | bytes 172064 | tf_op jit(solution)/shard_map/ppermute | solution.py:97
  282.7 3.1 %collective-permute-start.11 = (f32[168,256]{1,0:T(8,128)S(1)}, f32[168,256]{1,0:T(8,128)S(1)}, u32[]{:S(2)}, u32[]{:S(2)}) collective-permute-start(f32[168,256]{1,0:T(8,128)S(1)} %fusion.86), channel_id=1, source_target_pairs={{0,16},{16,0},{32,48},{48,32},{64,80},{80,64},{96,112},{112,96},{1... | collective-permute-start | bytes 516104 | tf_op jit(solution)/shard_map/ppermute | solution.py:97
  286.9 2.4 collective-permute-start.13
  289.7 3.7 %collective-permute-done.12 = f32[168,256]{1,0:T(8,128)S(1)} collective-permute-done((f32[168,256]{1,0:T(8,128)S(1)}, f32[168,256]{1,0:T(8,128)S(1)}, u32[]{:S(2)}, u32[]{:S(2)}) %collective-permute-start.12) | collective-permute-done | bytes 172064 | tf_op jit(solution)/shard_map/ppermute | solution.py:97
  293.4 2.8 collective-permute-done.13
  297.1 2.7 gather_fusion.2
  (145 shorter events, 38.3 us)
Async XLA Ops:
  7.2 1.9 copy-start
  7.2 143.3 %all-gather.6.cloned.1.call-start = ((), (), s32[]{:S(2)}) async-start(), calls=%async_computation.1 | async-start | bytes 26738688 | tf_op jit(solution)/shard_map/all_gather | solution.py:143
  7.9 184.8 %all-gather.4.cloned.1.call-start = ((), (), s32[]{:S(2)}) async-start(), calls=%async_computation | async-start | bytes 2228224 | tf_op jit(solution)/shard_map/all_gather | solution.py:160
  9.1 7.6 %copy-start.14 = (bf16[1,2560]{1,0:T(2,128)(2,1)S(1)}, bf16[1,2560]{1,0:T(2,128)(2,1)}, u32[]{:S(2)}) copy-start(bf16[1,2560]{1,0:T(2,128)(2,1)} %param.23) | copy-start | bytes 15364
  9.1 7.6 %copy-start.15 = (bf16[1,2560]{1,0:T(2,128)(2,1)S(1)}, bf16[1,2560]{1,0:T(2,128)(2,1)}, u32[]{:S(2)}) copy-start(bf16[1,2560]{1,0:T(2,128)(2,1)} %param.24) | copy-start | bytes 15364
  14.1 2.6 copy-start.2
  14.2 3.1 %copy-start.9 = (bf16[2560,256]{1,0:T(8,128)(2,1)S(1)}, bf16[2560,256]{1,0:T(8,128)(2,1)}, u32[]{:S(2)}) copy-start(bf16[2560,256]{1,0:T(8,128)(2,1)} %param.27) | copy-start | bytes 3932164
  14.2 3.1 %copy-start.16 = (bf16[1,128,256]{2,1,0:T(8,128)(2,1)S(1)}, bf16[1,128,256]{2,1,0:T(8,128)(2,1)}, u32[]{:S(2)}) copy-start(bf16[1,128,256]{2,1,0:T(8,128)(2,1)} %param.25) | copy-start | bytes 196612
  15.9 3.6 %collective-permute-start = (f32[32,512]{1,0:T(8,128)S(1)}, f32[32,512]{1,0:T(8,128)S(1)}, u32[]{:S(2)}, u32[]{:S(2)}) collective-permute-start(f32[32,512]{1,0:T(8,128)S(1)} %select_reduce_fusion), channel_id=1, source_target_pairs={{0,1},{1,0},{2,3},{3,2},{4,5},{5,4},{6,7},{7,6},{8,9},{9,8},{10,11... | collective-permute-start | bytes 196616 | tf_op jit(solution)/shard_map/ppermute | solution.py:108
  17.3 2.0 copy-start.12
  17.8 3.8 %copy-start.10 = (bf16[256,2048]{1,0:T(8,128)(2,1)S(1)}, bf16[256,2048]{1,0:T(8,128)(2,1)}, u32[]{:S(2)}) copy-start(bf16[256,2048]{1,0:T(8,128)(2,1)} %param.28) | copy-start | bytes 3145732
  19.5 4.8 %collective-permute-start.1 = (f32[32,512]{1,0:T(8,128)S(1)}, f32[32,512]{1,0:T(8,128)S(1)}, u32[]{:S(2)}, u32[]{:S(2)}) collective-permute-start(f32[32,512]{1,0:T(8,128)S(1)} %add.271), channel_id=1, source_target_pairs={{0,2},{1,3},{2,0},{3,1},{4,6},{5,7},{6,4},{7,5},{8,10},{9,11},{10,... | collective-permute-start | bytes 196616 | tf_op jit(solution)/shard_map/ppermute | solution.py:108
  22.0 130.4 %copy-start.5 = (f32[128,2048]{1,0:T(8,128)}, f32[128,2048]{1,0:T(8,128)S(1)}, u32[]{:S(2)}) copy-start(f32[128,2048]{1,0:T(8,128)S(1)} %get-tuple-element.83) | copy-start | bytes 3145732
  22.0 128.6 %copy-start.17 = (s32[16]{0:T(128)S(1)}, s32[16]{0:T(128)}, u32[]{:S(2)}) copy-start(s32[16]{0:T(128)} %param.34) | copy-start | bytes 196
  22.0 129.1 %copy-start.18 = (f32[16]{0:T(128)S(1)}, f32[16]{0:T(128)}, u32[]{:S(2)}) copy-start(f32[16]{0:T(128)} %param.35) | copy-start | bytes 196
  24.3 8.6 %collective-permute-start.2 = (f32[32,512]{1,0:T(8,128)S(1)}, f32[32,512]{1,0:T(8,128)S(1)}, u32[]{:S(2)}, u32[]{:S(2)}) collective-permute-start(f32[32,512]{1,0:T(8,128)S(1)} %add.272), channel_id=1, source_target_pairs={{0,4},{1,5},{2,6},{3,7},{4,0},{5,1},{6,2},{7,3},{8,12},{9,13},{10,... | collective-permute-start | bytes 196616 | tf_op jit(solution)/shard_map/ppermute | solution.py:108
  32.9 11.1 %collective-permute-start.3 = (f32[32,512]{1,0:T(8,128)S(1)}, f32[32,512]{1,0:T(8,128)S(1)}, u32[]{:S(2)}, u32[]{:S(2)}) collective-permute-start(f32[32,512]{1,0:T(8,128)S(1)} %add.273), channel_id=1, source_target_pairs={{0,8},{1,9},{2,10},{3,11},{4,12},{5,13},{6,14},{7,15},{8,0},{9,1},... | collective-permute-start | bytes 196616 | tf_op jit(solution)/shard_map/ppermute | solution.py:108
  196.7 3.9 %copy-start.7 = (f32[16,128,128]{1,2,0:T(8,128)S(1)}, f32[16,128,128]{1,2,0:T(8,128)}, u32[]{:S(2)}) copy-start(f32[16,128,128]{1,2,0:T(8,128)} %get-tuple-element.85) | copy-start | bytes 3145732
  205.7 13.7 %copy-start.6 = (f32[128,2048]{1,0:T(8,128)S(1)}, f32[128,2048]{1,0:T(8,128)}, u32[]{:S(2)}) copy-start(f32[128,2048]{1,0:T(8,128)} %copy-done.5) | copy-start | bytes 3145732
  223.7 4.7 %copy-start.3 = (bf16[1,128,2560]{2,1,0:T(8,128)(2,1)S(1)}, bf16[1,128,2560]{2,1,0:T(8,128)(2,1)}, u32[]{:S(2)}) copy-start(bf16[1,128,2560]{2,1,0:T(8,128)(2,1)} %param.22) | copy-start | bytes 1966084
  234.3 3.5 %collective-permute-start.4 = (f32[2,2,2,168,256]{4,3,2,1,0:T(8,128)}, f32[2,2,2,168,256]{4,3,2,1,0:T(8,128)}, u32[]{:S(2)}, u32[]{:S(2)}) collective-permute-start(f32[2,2,2,168,256]{4,3,2,1,0:T(8,128)} %dynamic-slice_bitcast_fusion), channel_id=1, source_target_pairs={{0,1},{1,0},{2,3},{3,2},{4,5},{5,4},{6,7},{7,6},{8,9},{9,8},{10,11... | collective-permute-start | bytes 4128776 | tf_op jit(solution)/shard_map/ppermute | solution.py:84
  239.3 1.1 copy-start.4
  240.4 10.4 %collective-permute-start.5 = (bf16[2,2,168,256]{3,2,1,0:T(8,128)(2,1)S(1)}, bf16[2,2,168,256]{3,2,1,0:T(8,128)(2,1)S(1)}, u32[]{:S(2)}, u32[]{:S(2)}) collective-permute-start(bf16[2,2,168,256]{3,2,1,0:T(8,128)(2,1)S(1)} %fusion.28), channel_id=1, source_target_pairs={{0,2},{1,3},{2,0},{3,1},{4,6},{5,7},{6,4},{7,5},{8,10},{9,11},{10,... | collective-permute-start | bytes 1032200 | tf_op jit(solution)/shard_map/ppermute | solution.py:84
  252.0 10.5 %collective-permute-start.6 = (bf16[2,168,256]{2,1,0:T(8,128)(2,1)S(1)}, bf16[2,168,256]{2,1,0:T(8,128)(2,1)S(1)}, u32[]{:S(2)}, u32[]{:S(2)}) collective-permute-start(bf16[2,168,256]{2,1,0:T(8,128)(2,1)S(1)} %fusion.33), channel_id=1, source_target_pairs={{0,4},{1,5},{2,6},{3,7},{4,0},{5,1},{6,2},{7,3},{8,12},{9,13},{10,... | collective-permute-start | bytes 516104 | tf_op jit(solution)/shard_map/ppermute | solution.py:84
  262.6 9.0 %collective-permute-start.7 = (bf16[168,256]{1,0:T(8,128)(2,1)S(1)}, bf16[168,256]{1,0:T(8,128)(2,1)S(1)}, u32[]{:S(2)}, u32[]{:S(2)}) collective-permute-start(bf16[168,256]{1,0:T(8,128)(2,1)S(1)} %fusion.36), channel_id=1, source_target_pairs={{0,8},{1,9},{2,10},{3,11},{4,12},{5,13},{6,14},{7,15},{8,0},{9,1},... | collective-permute-start | bytes 258056 | tf_op jit(solution)/shard_map/ppermute | solution.py:84
  271.6 7.0 %collective-permute-start.8 = (f32[168,256]{1,0:T(8,128)S(1)}, f32[168,256]{1,0:T(8,128)S(1)}, u32[]{:S(2)}, u32[]{:S(2)}) collective-permute-start(f32[168,256]{1,0:T(8,128)S(1)} %bitcast_add_fusion.3), channel_id=1, source_target_pairs={{0,32},{16,48},{32,0},{48,16},{64,96},{80,112},{96,64},{112,80},{1... | collective-permute-start | bytes 516104 | tf_op jit(solution)/shard_map/ppermute | solution.py:97
  272.7 9.2 %collective-permute-start.9 = (f32[168,256]{1,0:T(8,128)S(1)}, f32[168,256]{1,0:T(8,128)S(1)}, u32[]{:S(2)}, u32[]{:S(2)}) collective-permute-start(f32[168,256]{1,0:T(8,128)S(1)} %bitcast_add_fusion.3), channel_id=1, source_target_pairs={{0,128},{16,144},{32,160},{48,176},{64,192},{80,208},{96,224},{112... | collective-permute-start | bytes 516104 | tf_op jit(solution)/shard_map/ppermute | solution.py:97
  274.0 7.8 %collective-permute-start.10 = (f32[168,256]{1,0:T(8,128)S(1)}, f32[168,256]{1,0:T(8,128)S(1)}, u32[]{:S(2)}, u32[]{:S(2)}) collective-permute-start(f32[168,256]{1,0:T(8,128)S(1)} %bitcast_add_fusion.3), channel_id=1, source_target_pairs={{0,160},{16,176},{32,128},{48,144},{64,224},{80,240},{96,192},{112... | collective-permute-start | bytes 516104 | tf_op jit(solution)/shard_map/ppermute | solution.py:97
  282.7 7.0 %collective-permute-start.11 = (f32[168,256]{1,0:T(8,128)S(1)}, f32[168,256]{1,0:T(8,128)S(1)}, u32[]{:S(2)}, u32[]{:S(2)}) collective-permute-start(f32[168,256]{1,0:T(8,128)S(1)} %fusion.86), channel_id=1, source_target_pairs={{0,16},{16,0},{32,48},{48,32},{64,80},{80,64},{96,112},{112,96},{1... | collective-permute-start | bytes 516104 | tf_op jit(solution)/shard_map/ppermute | solution.py:97
  285.8 7.6 %collective-permute-start.12 = (f32[168,256]{1,0:T(8,128)S(1)}, f32[168,256]{1,0:T(8,128)S(1)}, u32[]{:S(2)}, u32[]{:S(2)}) collective-permute-start(f32[168,256]{1,0:T(8,128)S(1)} %fusion.86), channel_id=1, source_target_pairs={{0,64},{16,80},{32,96},{48,112},{64,0},{80,16},{96,32},{112,48},{1... | collective-permute-start | bytes 516104 | tf_op jit(solution)/shard_map/ppermute | solution.py:97
  286.9 9.3 %collective-permute-start.13 = (f32[168,256]{1,0:T(8,128)S(1)}, f32[168,256]{1,0:T(8,128)S(1)}, u32[]{:S(2)}, u32[]{:S(2)}) collective-permute-start(f32[168,256]{1,0:T(8,128)S(1)} %fusion.86), channel_id=1, source_target_pairs={{0,80},{16,64},{32,112},{48,96},{64,16},{80,0},{96,48},{112,32},{1... | collective-permute-start | bytes 516104 | tf_op jit(solution)/shard_map/ppermute | solution.py:97
  297.1 5.2 %copy-start.1 = (bf16[3088,512]{1,0:T(8,128)(2,1)S(1)}, bf16[3088,512]{1,0:T(8,128)(2,1)}, u32[]{:S(2)}) copy-start(bf16[3088,512]{1,0:T(8,128)(2,1)} %param.32) | copy-start | bytes 9486340
  (3 other events, 3.0 us)
Sparse Core Ops, SparseCore 0:
  9.9 140.6 all-gather.5
  152.4 40.3 all-gather.3

commit v6 on v3

--- a/solution.py
+++ b/solution.py
@@ -126,7 +126,19 @@
     )
     text_part = jnp.sum(jnp.where(inside[..., None], picked, 0.0), axis=1)
     text_raw = doubling_sum(text_part, "seq")
-    w_all = lax.all_gather(w_qkv, "seq", axis=0)
+    proj_size = w_proj.shape[0] * w_proj.shape[1]
+    spare = -(-proj_size // (w_qkv.shape[0] * head_size))
+    spare = -(-spare // 16) * 16
+    proj_spare = jnp.pad(w_proj.reshape(-1), (0, w_qkv.shape[0] * spare * head_size - proj_size))
+    w_ext = jnp.concatenate(
+        [w_qkv, proj_spare.reshape(w_qkv.shape[0], spare, head_size)], axis=1
+    )
+    w_all = lax.all_gather(w_ext, "seq", axis=0)
+    proj_gathered = (
+        w_all[:, :, D_REW:, :]
+        .reshape(ways, -1)[:, :proj_size]
+        .reshape(ways * w_proj.shape[0], w_proj.shape[1])
+    )
 
     hidden_f = hidden.astype(jnp.float32)
     centred = hidden_f - jnp.mean(hidden_f, axis=-1, keepdims=True)
@@ -139,15 +151,16 @@
     x_clean = noisy.astype(jnp.float32) - level * eps_pred
     theta, path_east, path_north = local_path(x_clean)
     normed_e, scale_rms = embed(x_clean, path_east, path_north, w_embed, root_rows)
-    w_all, proj_send, emb_b, text_raw = lax.optimization_barrier(
-        (w_all, w_proj, normed_e.astype(jnp.bfloat16), text_raw)
+    emb_b = normed_e.astype(jnp.bfloat16)
+    emb_ext = jnp.pad(emb_b, ((0, 0), (0, 0), (0, w_all.shape[2] - D_REW)))
+    w_all, proj_b, emb_ext, text_raw = lax.optimization_barrier(
+        (w_all, proj_gathered, emb_ext, text_raw)
     )
     text_unit, text_len = unit_rows(text_raw)
-    proj_b = lax.all_gather(proj_send, "seq", axis=0, tiled=True)
     proj_rows = proj_b.astype(jnp.float32)
     projected = jnp.einsum(
         "cfd,hjdk->cfhjk",
-        emb_b,
+        emb_ext,
         w_all,
         preferred_element_type=jnp.float32,
     )
@@ -210,6 +223,7 @@
     d_key = (d_ku - key_unit * jnp.sum(key_unit * d_ku, axis=-1, keepdims=True)) / key_len
     d_proj = jnp.stack([d_query, d_key, d_value], axis=3).astype(jnp.bfloat16)
     d_emb = jnp.einsum("cfhjk,hjdk->cfd", d_proj, w_all, preferred_element_type=jnp.float32)
+    d_emb = d_emb[..., :D_REW]
     d_motion = motion_grad(d_emb, normed_e, scale_rms, x_clean, theta, embed_rows, root_rows)
     d_eps_b = (-level * d_motion).astype(jnp.bfloat16)
     d_mod = jnp.einsum("cfe,de->cfd", d_eps_b, w_out, preferred_element_type=jnp.float32)

time: 310 us -> 310 us (level)
  waiting for transfers between devices: 183 us -> 168 us
  local copies, waits for them, and re-layouts: 15.2 us -> 22.7 us
  other arithmetic: 19.7 us -> 23 us
    all_gather x2 -> x1, waiting for transfers between devices: 126 us -> 114 us  [local(): w_all = lax.all_gather(w_ext, 'seq', axis=0)]
    ppermute x4, starting transfers between devices: 6.02 us -> 9.38 us  [halving_sum(): lax.ppermute(send.astype(wire_types[k]), axis, xor_pairs(size, 1 << k))]
  transfers between devices with their start and end apart: 14 -> 13, of which waited for: 13 -> 12; matrix products, arithmetic and copies ran while one was open for 11% -> 4% of each run, Pallas kernels for 0% -> 0%
where the time goes in v6:
time: 310 us; the launch traced here: 309 us
  waiting for transfers between devices  168 us (54%)
  matrix products  49.1 us (16%)
  starting transfers between devices  28.4 us (9%)
  other arithmetic  23 us (7%)
  local copies, waits for them, and re-layouts  22.7 us (7%)
  between operations  17.2 us (6%)
    all_gather x1, waiting for transfers between devices, local(): w_all = lax.all_gather(w_ext, 'seq', axis=0)  114 us
    ppermute x8, waiting for transfers between devices, doubling_sum(): value = value + lax.ppermute(value, axis, xor_pairs(size, 1 << k))  30.2 us
    ppermute x4, waiting for transfers between devices, halving_sum(): lax.ppermute(send.astype(wire_types[k]), axis, xor_pairs(size, 1 << k))  24.4 us
    ppermute x8, starting transfers between devices, doubling_sum(): value = value + lax.ppermute(value, axis, xor_pairs(size, 1 << k))  18.9 us
    dot_general x1, matrix products, local(): jnp.einsum('cfhjk,hjdk->cfd', d_proj, w_all, preferred_element_type=jnp.f...  15.4 us
    dot_general x1, matrix products, local(): jnp.einsum('cfd,hjdk->cfhjk', emb_ext, w_all, preferred_element_type=jnp....  15.2 us
    ppermute x4, starting transfers between devices, halving_sum(): lax.ppermute(send.astype(wire_types[k]), axis, xor_pairs(size, 1 << k))  9.38 us
  transfers between devices with their start and end apart: 13, of which 12 were waited for; matrix products, arithmetic and copies ran while one was open for 4% of the time, Pallas kernels for 0%

profile of v6, /device:TPU:6, one launch (start us, length us, event | category | flops | bytes accessed | tf_op | source)
XLA Modules:
  0.0 308.9 jit_solution(14369338888454213871)
XLA Ops:
  8.4 2.7 pad_maximum_fusion.1
  11.9 5.1 %gather_fusion = bf16[1024,512]{1,0:T(8,128)(2,1)} fusion(bf16[3088,512]{1,0:T(8,128)(2,1)S(1)} %copy-done, s32[1024]{0:T(1024)S(1)} %broadcast_clamp_fusion), kind=kCustom, calls=%fused_computation | custom fusion | bytes 2101248 | tf_op jit(solution)/shard_map/jit(_take)/gather | solution.py:124
  17.0 1.8 select_reduce_fusion
  22.4 2.0 collective-permute-start.1
  24.8 2.9 collective-permute-done.1
  27.8 3.5 %collective-permute-start.2 = (f32[32,512]{1,0:T(8,128)S(1)}, f32[32,512]{1,0:T(8,128)S(1)}, u32[]{:S(2)}, u32[]{:S(2)}) collective-permute-start(f32[32,512]{1,0:T(8,128)S(1)} %add.248), channel_id=1, source_target_pairs={{0,4},{1,5},{2,6},{3,7},{4,0},{5,1},{6,2},{7,3},{8,12},{9,13},{10,... | collective-permute-start | bytes 196616 | tf_op jit(solution)/shard_map/ppermute | solution.py:94
  31.3 5.2 %collective-permute-done.2 = f32[32,512]{1,0:T(8,128)S(1)} collective-permute-done((f32[32,512]{1,0:T(8,128)S(1)}, f32[32,512]{1,0:T(8,128)S(1)}, u32[]{:S(2)}, u32[]{:S(2)}) %collective-permute-start.2) | collective-permute-done | bytes 65568 | tf_op jit(solution)/shard_map/ppermute | solution.py:94
  36.6 7.3 %collective-permute-start.3 = (f32[32,512]{1,0:T(8,128)S(1)}, f32[32,512]{1,0:T(8,128)S(1)}, u32[]{:S(2)}, u32[]{:S(2)}) collective-permute-start(f32[32,512]{1,0:T(8,128)S(1)} %add.249), channel_id=1, source_target_pairs={{0,8},{1,9},{2,10},{3,11},{4,12},{5,13},{6,14},{7,15},{8,0},{9,1},... | collective-permute-start | bytes 196616 | tf_op jit(solution)/shard_map/ppermute | solution.py:94
  48.2 113.9 %all-gather.3.cloned.1.call-done = bf16[48,2224,128]{2,1,0:T(8,128)(2,1)} async-done(((bf16[3,2224,128]{2,1,0:T(8,128)(2,1)}), bf16[48,2224,128]{2,1,0:T(8,128)(2,1)}) %all-gather.3.cloned.1.call-update) | async-done | bytes 27328528 | tf_op jit(solution)/shard_map/all_gather | solution.py:136
  162.1 1.8 slice.128
  164.6 2.2 reshape.742
  166.9 15.2 %convolution_bitcast_fusion.1 = f32[1,128,16,3,128]{1,4,3,2,0:T(8,128)S(1)} fusion(bf16[16,3,2224,128]{3,2,1,0:T(8,128)(2,1)} %bitcast.223, bf16[1,128,2224]{2,1,0:T(8,128)(2,1)} %pad.15), kind=kOutput, calls=%fused_computation.9 | convolution fusion | flops 3498049536 | bytes 31043584 | tf_op jit(solution)/shard_map/cfd,hjdk->cfhjk/dot_general | solution.py:161
  183.5 2.6 convert_reduce_fusion.1
  188.0 2.0 fusion.69
  191.9 3.4 %fusion.70 = f32[1,2048]{1,0:T(1,128)S(1)} fusion(f32[512,1]{0,1:T(1,128)S(1)} %bitcast.246, bf16[2048,512]{1,0:T(8,128)(2,1)} %reshape.742), kind=kOutput, calls=%fused_computation.160 | convolution fusion | flops 12582912 | bytes 2107392 | tf_op jit(solution)/shard_map/dot_general | solution.py:197
  200.9 15.4 %convolution_bitcast_fusion = f32[1,128,2224]{2,1,0:T(8,128)} fusion(bf16[16,3,2224,128]{3,2,1,0:T(8,128)(2,1)} %bitcast.224, bf16[128,16,1,128]{0,3,1,2:T(8,128)(2,1)} %multiply_convert_fusion, bf16[128,16,1,128]{0,3,1,2:T(8,128)(2,1)} %get-tuple-element.68, bf16[128,16,1,128]{0,3,1,2:T(8,128)(2,1)} %get-tuple-element.67), kind=kOutput, calls=%fused_computation.3 | convolution fusion | flops 3499622400 | bytes 30040064 | tf_op jit(solution)/shard_map/cfhjk,hjdk->cfd/dot_general | solution.py:225
  216.3 1.6 fusion.24
  219.8 1.9 fusion.58
  222.2 2.5 fusion.21
  226.9 2.0 fusion.12
  236.2 3.1 collective-permute-done.4
  241.9 2.4 collective-permute-start.5
  244.3 8.5 %collective-permute-done.5 = bf16[2,2,168,256]{3,2,0,1:T(8,128)(2,1)S(1)} collective-permute-done((bf16[2,2,168,256]{3,2,0,1:T(8,128)(2,1)S(1)}, bf16[2,2,168,256]{3,2,0,1:T(8,128)(2,1)S(1)}, u32[]{:S(2)}, u32[]{:S(2)}) %collective-permute-start.5) | collective-permute-done | bytes 344096 | tf_op jit(solution)/shard_map/ppermute | solution.py:84
  252.9 2.0 collective-permute-start.6
  255.0 8.7 %collective-permute-done.6 = bf16[2,168,256]{2,1,0:T(8,128)(2,1)S(1)} collective-permute-done((bf16[2,168,256]{2,1,0:T(8,128)(2,1)S(1)}, bf16[2,168,256]{2,1,0:T(8,128)(2,1)S(1)}, u32[]{:S(2)}, u32[]{:S(2)}) %collective-permute-start.6) | collective-permute-done | bytes 172064 | tf_op jit(solution)/shard_map/ppermute | solution.py:84
  264.3 4.7 %collective-permute-start.7 = (bf16[168,256]{1,0:T(8,128)(2,1)}, bf16[168,256]{1,0:T(8,128)(2,1)}, u32[]{:S(2)}, u32[]{:S(2)}) collective-permute-start(bf16[168,256]{1,0:T(8,128)(2,1)} %fusion.38), channel_id=1, source_target_pairs={{0,8},{1,9},{2,10},{3,11},{4,12},{5,13},{6,14},{7,15},{8,0},{9,1},... | collective-permute-start | bytes 258056 | tf_op jit(solution)/shard_map/ppermute | solution.py:84
  269.1 4.1 %collective-permute-done.7 = bf16[168,256]{1,0:T(8,128)(2,1)} collective-permute-done((bf16[168,256]{1,0:T(8,128)(2,1)}, bf16[168,256]{1,0:T(8,128)(2,1)}, u32[]{:S(2)}, u32[]{:S(2)}) %collective-permute-start.7) | collective-permute-done | bytes 86048 | tf_op jit(solution)/shard_map/ppermute | solution.py:84
  275.6 3.9 %collective-permute-done.8 = f32[168,256]{1,0:T(8,128)S(1)} collective-permute-done((f32[168,256]{1,0:T(8,128)S(1)}, f32[168,256]{1,0:T(8,128)S(1)}, u32[]{:S(2)}, u32[]{:S(2)}) %collective-permute-start.8) | collective-permute-done | bytes 172064 | tf_op jit(solution)/shard_map/ppermute | solution.py:94
  279.6 3.2 %collective-permute-start.9 = (f32[168,256]{1,0:T(8,128)S(1)}, f32[168,256]{1,0:T(8,128)S(1)}, u32[]{:S(2)}, u32[]{:S(2)}) collective-permute-start(f32[168,256]{1,0:T(8,128)S(1)} %add.276), channel_id=1, source_target_pairs={{0,16},{16,0},{32,48},{48,32},{64,80},{80,64},{96,112},{112,96},{1... | collective-permute-start | bytes 516104 | tf_op jit(solution)/shard_map/ppermute | solution.py:94
  282.8 3.8 %collective-permute-done.9 = f32[168,256]{1,0:T(8,128)S(1)} collective-permute-done((f32[168,256]{1,0:T(8,128)S(1)}, f32[168,256]{1,0:T(8,128)S(1)}, u32[]{:S(2)}, u32[]{:S(2)}) %collective-permute-start.9) | collective-permute-done | bytes 172064 | tf_op jit(solution)/shard_map/ppermute | solution.py:94
  287.6 6.1 %collective-permute-done.10 = f32[168,256]{1,0:T(8,128)S(1)} collective-permute-done((f32[168,256]{1,0:T(8,128)S(1)}, f32[168,256]{1,0:T(8,128)S(1)}, u32[]{:S(2)}, u32[]{:S(2)}) %collective-permute-start.10) | collective-permute-done | bytes 172064 | tf_op jit(solution)/shard_map/ppermute | solution.py:94
  294.1 6.6 %collective-permute-done.11 = f32[168,256]{1,0:T(8,128)S(1)} collective-permute-done((f32[168,256]{1,0:T(8,128)S(1)}, f32[168,256]{1,0:T(8,128)S(1)}, u32[]{:S(2)}, u32[]{:S(2)}) %collective-permute-start.11) | collective-permute-done | bytes 172064 | tf_op jit(solution)/shard_map/ppermute | solution.py:94
  (142 shorter events, 39.6 us)
Async XLA Ops:
  7.2 4.7 %copy-start = (bf16[3088,512]{1,0:T(8,128)(2,1)S(1)}, bf16[3088,512]{1,0:T(8,128)(2,1)}, u32[]{:S(2)}) copy-start(bf16[3088,512]{1,0:T(8,128)(2,1)} %param.30) | copy-start | bytes 9486340
  7.2 155.0 %all-gather.3.cloned.1.call-start = ((), (), s32[]{:S(2)}) async-start(), calls=%async_computation | async-start | bytes 29036544 | tf_op jit(solution)/shard_map/all_gather | solution.py:136
  11.9 7.6 %copy-start.16 = (bf16[1,2560]{1,0:T(2,128)(2,1)S(1)}, bf16[1,2560]{1,0:T(2,128)(2,1)}, u32[]{:S(2)}) copy-start(bf16[1,2560]{1,0:T(2,128)(2,1)} %param.21) | copy-start | bytes 15364
  11.9 7.6 %copy-start.17 = (bf16[1,2560]{1,0:T(2,128)(2,1)S(1)}, bf16[1,2560]{1,0:T(2,128)(2,1)}, u32[]{:S(2)}) copy-start(bf16[1,2560]{1,0:T(2,128)(2,1)} %param.22) | copy-start | bytes 15364
  17.0 2.6 copy-start.2
  17.0 3.1 %copy-start.11 = (bf16[2560,256]{1,0:T(8,128)(2,1)S(1)}, bf16[2560,256]{1,0:T(8,128)(2,1)}, u32[]{:S(2)}) copy-start(bf16[2560,256]{1,0:T(8,128)(2,1)} %param.25) | copy-start | bytes 3932164
  17.0 3.1 %copy-start.18 = (bf16[1,128,256]{2,1,0:T(8,128)(2,1)S(1)}, bf16[1,128,256]{2,1,0:T(8,128)(2,1)}, u32[]{:S(2)}) copy-start(bf16[1,128,256]{2,1,0:T(8,128)(2,1)} %param.23) | copy-start | bytes 196612
  18.8 3.6 %collective-permute-start = (f32[32,512]{1,0:T(8,128)S(1)}, f32[32,512]{1,0:T(8,128)S(1)}, u32[]{:S(2)}, u32[]{:S(2)}) collective-permute-start(f32[32,512]{1,0:T(8,128)S(1)} %select_reduce_fusion), channel_id=1, source_target_pairs={{0,1},{1,0},{2,3},{3,2},{4,5},{5,4},{6,7},{7,6},{8,9},{9,8},{10,11... | collective-permute-start | bytes 196616 | tf_op jit(solution)/shard_map/ppermute | solution.py:94
  20.1 2.0 copy-start.14
  20.6 3.8 %copy-start.12 = (bf16[256,2048]{1,0:T(8,128)(2,1)S(1)}, bf16[256,2048]{1,0:T(8,128)(2,1)}, u32[]{:S(2)}) copy-start(bf16[256,2048]{1,0:T(8,128)(2,1)} %param.26) | copy-start | bytes 3145732
  22.4 5.4 %collective-permute-start.1 = (f32[32,512]{1,0:T(8,128)S(1)}, f32[32,512]{1,0:T(8,128)S(1)}, u32[]{:S(2)}, u32[]{:S(2)}) collective-permute-start(f32[32,512]{1,0:T(8,128)S(1)} %add.247), channel_id=1, source_target_pairs={{0,2},{1,3},{2,0},{3,1},{4,6},{5,7},{6,4},{7,5},{8,10},{9,11},{10,... | collective-permute-start | bytes 196616 | tf_op jit(solution)/shard_map/ppermute | solution.py:94
  24.8 20.0 %copy-start.4 = (f32[128,2048]{1,0:T(8,128)}, f32[128,2048]{1,0:T(8,128)S(1)}, u32[]{:S(2)}) copy-start(f32[128,2048]{1,0:T(8,128)S(1)} %get-tuple-element.84) | copy-start | bytes 3145732
  27.8 8.7 %collective-permute-start.2 = (f32[32,512]{1,0:T(8,128)S(1)}, f32[32,512]{1,0:T(8,128)S(1)}, u32[]{:S(2)}, u32[]{:S(2)}) collective-permute-start(f32[32,512]{1,0:T(8,128)S(1)} %add.248), channel_id=1, source_target_pairs={{0,4},{1,5},{2,6},{3,7},{4,0},{5,1},{6,2},{7,3},{8,12},{9,13},{10,... | collective-permute-start | bytes 196616 | tf_op jit(solution)/shard_map/ppermute | solution.py:94
  36.5 8.3 %copy-start.19 = (s32[16]{0:T(128)S(1)}, s32[16]{0:T(128)}, u32[]{:S(2)}) copy-start(s32[16]{0:T(128)} %param.32) | copy-start | bytes 196
  36.6 8.9 %copy-start.20 = (f32[16]{0:T(128)S(1)}, f32[16]{0:T(128)}, u32[]{:S(2)}) copy-start(f32[16]{0:T(128)} %param.33) | copy-start | bytes 196
  36.6 11.7 %collective-permute-start.3 = (f32[32,512]{1,0:T(8,128)S(1)}, f32[32,512]{1,0:T(8,128)S(1)}, u32[]{:S(2)}, u32[]{:S(2)}) collective-permute-start(f32[32,512]{1,0:T(8,128)S(1)} %add.249), channel_id=1, source_target_pairs={{0,8},{1,9},{2,10},{3,11},{4,12},{5,13},{6,14},{7,15},{8,0},{9,1},... | collective-permute-start | bytes 196616 | tf_op jit(solution)/shard_map/ppermute | solution.py:94
  191.9 3.9 %copy-start.7 = (f32[16,128,128]{1,2,0:T(8,128)S(1)}, f32[16,128,128]{1,2,0:T(8,128)}, u32[]{:S(2)}) copy-start(f32[16,128,128]{1,2,0:T(8,128)} %get-tuple-element.86) | copy-start | bytes 3145732
  195.3 1.1 copy-start.9
  200.9 15.4 %copy-start.5 = (f32[128,2048]{1,0:T(8,128)S(1)}, f32[128,2048]{1,0:T(8,128)}, u32[]{:S(2)}) copy-start(f32[128,2048]{1,0:T(8,128)} %copy-done.4) | copy-start | bytes 3145732
  216.3 1.6 copy-start.8
  222.2 4.7 %copy-start.3 = (bf16[1,128,2560]{2,1,0:T(8,128)(2,1)S(1)}, bf16[1,128,2560]{2,1,0:T(8,128)(2,1)}, u32[]{:S(2)}) copy-start(bf16[1,128,2560]{2,1,0:T(8,128)(2,1)} %param.20) | copy-start | bytes 1966084
  234.7 5.7 %copy-start.6 = (f32[2,2,2,1,168,256]{5,4,3,2,1,0:T(8,128)S(1)}, f32[2,2,2,1,168,256]{5,4,3,2,1,0:T(8,128)}, u32[]{:S(2)}) copy-start(f32[2,2,2,1,168,256]{5,4,3,2,1,0:T(8,128)} %get-tuple-element.71) | copy-start | bytes 4128772
  235.9 3.3 %collective-permute-start.4 = (f32[2,2,2,168,256]{4,3,0,1,2:T(8,128)}, f32[2,2,2,168,256]{4,3,0,1,2:T(8,128)S(1)}, u32[]{:S(2)}, u32[]{:S(2)}) collective-permute-start(f32[2,2,2,168,256]{4,3,0,1,2:T(8,128)} %bitcast.220), channel_id=1, source_target_pairs={{0,1},{1,0},{2,3},{3,2},{4,5},{5,4},{6,7},{7,6},{8,9},{9,8},{10,11... | collective-permute-start | bytes 4128776 | tf_op jit(solution)/shard_map/ppermute | solution.py:84
  239.3 1.1 copy-start.10
  241.9 10.9 %collective-permute-start.5 = (bf16[2,2,168,256]{3,2,0,1:T(8,128)(2,1)S(1)}, bf16[2,2,168,256]{3,2,0,1:T(8,128)(2,1)S(1)}, u32[]{:S(2)}, u32[]{:S(2)}) collective-permute-start(bf16[2,2,168,256]{3,2,0,1:T(8,128)(2,1)S(1)} %fusion.32), channel_id=1, source_target_pairs={{0,2},{1,3},{2,0},{3,1},{4,6},{5,7},{6,4},{7,5},{8,10},{9,11},{10,... | collective-permute-start | bytes 1032200 | tf_op jit(solution)/shard_map/ppermute | solution.py:84
  252.9 10.7 %collective-permute-start.6 = (bf16[2,168,256]{2,1,0:T(8,128)(2,1)S(1)}, bf16[2,168,256]{2,1,0:T(8,128)(2,1)S(1)}, u32[]{:S(2)}, u32[]{:S(2)}) collective-permute-start(bf16[2,168,256]{2,1,0:T(8,128)(2,1)S(1)} %fusion.37), channel_id=1, source_target_pairs={{0,4},{1,5},{2,6},{3,7},{4,0},{5,1},{6,2},{7,3},{8,12},{9,13},{10,... | collective-permute-start | bytes 516104 | tf_op jit(solution)/shard_map/ppermute | solution.py:84
  264.3 8.8 %collective-permute-start.7 = (bf16[168,256]{1,0:T(8,128)(2,1)}, bf16[168,256]{1,0:T(8,128)(2,1)}, u32[]{:S(2)}, u32[]{:S(2)}) collective-permute-start(bf16[168,256]{1,0:T(8,128)(2,1)} %fusion.38), channel_id=1, source_target_pairs={{0,8},{1,9},{2,10},{3,11},{4,12},{5,13},{6,14},{7,15},{8,0},{9,1},... | collective-permute-start | bytes 258056 | tf_op jit(solution)/shard_map/ppermute | solution.py:84
  269.0 33.0 %copy-start.1 = (bf16[3088,512]{1,0:T(8,128)(2,1)S(1)}, bf16[3088,512]{1,0:T(8,128)(2,1)}, u32[]{:S(2)}) copy-start(bf16[3088,512]{1,0:T(8,128)(2,1)} %param.30) | copy-start | bytes 9486340
  274.1 5.5 %collective-permute-start.8 = (f32[168,256]{1,0:T(8,128)S(1)}, f32[168,256]{1,0:T(8,128)S(1)}, u32[]{:S(2)}, u32[]{:S(2)}) collective-permute-start(f32[168,256]{1,0:T(8,128)S(1)} %bitcast_add_fusion.3), channel_id=1, source_target_pairs={{0,128},{128,0},{1,129},{129,1},{2,130},{130,2},{3,131},{131,3},{4... | collective-permute-start | bytes 516104 | tf_op jit(solution)/shard_map/ppermute | solution.py:94
  279.6 7.0 %collective-permute-start.9 = (f32[168,256]{1,0:T(8,128)S(1)}, f32[168,256]{1,0:T(8,128)S(1)}, u32[]{:S(2)}, u32[]{:S(2)}) collective-permute-start(f32[168,256]{1,0:T(8,128)S(1)} %add.276), channel_id=1, source_target_pairs={{0,16},{16,0},{32,48},{48,32},{64,80},{80,64},{96,112},{112,96},{1... | collective-permute-start | bytes 516104 | tf_op jit(solution)/shard_map/ppermute | solution.py:94
  286.6 7.0 %collective-permute-start.10 = (f32[168,256]{1,0:T(8,128)S(1)}, f32[168,256]{1,0:T(8,128)S(1)}, u32[]{:S(2)}, u32[]{:S(2)}) collective-permute-start(f32[168,256]{1,0:T(8,128)S(1)} %add.277), channel_id=1, source_target_pairs={{0,32},{16,48},{32,0},{48,16},{64,96},{80,112},{96,64},{112,80},{1... | collective-permute-start | bytes 516104 | tf_op jit(solution)/shard_map/ppermute | solution.py:94
  293.7 7.0 %collective-permute-start.11 = (f32[168,256]{1,0:T(8,128)S(1)}, f32[168,256]{1,0:T(8,128)S(1)}, u32[]{:S(2)}, u32[]{:S(2)}) collective-permute-start(f32[168,256]{1,0:T(8,128)S(1)} %add.278), channel_id=1, source_target_pairs={{0,64},{16,80},{32,96},{48,112},{64,0},{80,16},{96,32},{112,48},{1... | collective-permute-start | bytes 516104 | tf_op jit(solution)/shard_map/ppermute | solution.py:94
  (2 other events, 1.8 us)
Sparse Core Ops, SparseCore 0:
  11.2 150.8 all-gather.2

commit v7 on v3

--- a/solution.py
+++ b/solution.py
@@ -71,7 +71,7 @@
     return [(i, i ^ bit) for i in range(size)]
 
 
-def halving_sum(chunks, axis, wire_types):
+def halving_sum(chunks, axis, wire_types, ride=None):
     size = lax.axis_size(axis)
     me = lax.axis_index(axis)
     bits = size.bit_length() - 1
@@ -83,7 +83,9 @@
         send = lax.dynamic_index_in_dim(buf, 1 - mine, axis=bits - 1 - k, keepdims=False)
         got = lax.ppermute(send.astype(wire_types[k]), axis, xor_pairs(size, 1 << k))
         buf = keep + got.astype(keep.dtype)
-    return buf
+        if k == 0:
+            buf, ride = lax.optimization_barrier((buf, ride))
+    return buf, ride
 
 
 def doubling_sum(value, axis):
@@ -139,8 +141,8 @@
     x_clean = noisy.astype(jnp.float32) - level * eps_pred
     theta, path_east, path_north = local_path(x_clean)
     normed_e, scale_rms = embed(x_clean, path_east, path_north, w_embed, root_rows)
-    w_all, proj_send, emb_b, text_raw = lax.optimization_barrier(
-        (w_all, w_proj, normed_e.astype(jnp.bfloat16), text_raw)
+    w_all, proj_send, emb_b, text_raw, modulated_t = lax.optimization_barrier(
+        (w_all, w_proj, normed_e.astype(jnp.bfloat16), text_raw, jnp.swapaxes(modulated, 1, 2))
     )
     text_unit, text_len = unit_rows(text_raw)
     proj_b = lax.all_gather(proj_send, "seq", axis=0, tiled=True)
@@ -212,17 +214,9 @@
     d_emb = jnp.einsum("cfhjk,hjdk->cfd", d_proj, w_all, preferred_element_type=jnp.float32)
     d_motion = motion_grad(d_emb, normed_e, scale_rms, x_clean, theta, embed_rows, root_rows)
     d_eps_b = (-level * d_motion).astype(jnp.bfloat16)
-    d_mod = jnp.einsum("cfe,de->cfd", d_eps_b, w_out, preferred_element_type=jnp.float32)
-    d_norm = d_mod * gain
-    grad_hidden = (
-        inv_std
-        * (
-            d_norm
-            - jnp.mean(d_norm, axis=-1, keepdims=True)
-            - normed_h * jnp.mean(d_norm * normed_h, axis=-1, keepdims=True)
-        )
-    ).astype(jnp.bfloat16)
-    grad_term = jnp.einsum("cfd,cfe->de", modulated, d_eps_b, preferred_element_type=jnp.float32)
+    grad_term = jnp.einsum(
+        "cdf,cfe->de", modulated_t, d_eps_b, preferred_element_type=jnp.float32
+    )
 
     rows_dev = w_out.shape[0] // ways
     cols = grad_term.shape[1]
@@ -244,7 +238,19 @@
         axis=1,
     )
     seq_bits = ways.bit_length() - 1
-    block = halving_sum(stacked, "seq", [jnp.float32] + [jnp.bfloat16] * (seq_bits - 1))
+    block, d_eps_b = halving_sum(
+        stacked, "seq", [jnp.float32] + [jnp.bfloat16] * (seq_bits - 1), ride=d_eps_b
+    )
+    d_mod = jnp.einsum("cfe,de->cfd", d_eps_b, w_out, preferred_element_type=jnp.float32)
+    d_norm = d_mod * gain
+    grad_hidden = (
+        inv_std
+        * (
+            d_norm
+            - jnp.mean(d_norm, axis=-1, keepdims=True)
+            - normed_h * jnp.mean(d_norm * normed_h, axis=-1, keepdims=True)
+        )
+    ).astype(jnp.bfloat16)
     block = doubling_sum(doubling_sum(block, "sec"), "dp")
     grad_w_out = block[:rows_dev]
     group_first = (lax.axis_index("sec") * n_dp + lax.axis_index("dp")) * ways * clips_dev

time: 310 us -> 304 us (0.981)
  waiting for transfers between devices: 183 us -> 177 us
    all_gather x1, waiting for transfers between devices: 107 us -> 103 us  [local(): w_all = lax.all_gather(w_qkv, 'seq', axis=0)]
  transfers between devices with their start and end apart: 14 -> 14, of which waited for: 13 -> 13; matrix products, arithmetic and copies ran while one was open for 11% -> 14% of each run, Pallas kernels for 0% -> 0%
where the time goes in v7:
time: 304 us
  waiting for transfers between devices  177 us (58%)
  matrix products  45.8 us (15%)
  starting transfers between devices  24.6 us (8%)
  other arithmetic  21.4 us (7%)
  local copies, waits for them, and re-layouts  18 us (6%)
  between operations  17.2 us (6%)
    all_gather x1, waiting for transfers between devices, local(): w_all = lax.all_gather(w_qkv, 'seq', axis=0)  103 us
    ppermute x4, waiting for transfers between devices, halving_sum(): lax.ppermute(send.astype(wire_types[k]), axis, xor_pairs(size, 1 << k))  27.4 us
    ppermute x8, waiting for transfers between devices, doubling_sum(): value = value + lax.ppermute(value, axis, xor_pairs(size, 1 << k))  27.1 us
    ppermute x8, starting transfers between devices, doubling_sum(): value = value + lax.ppermute(value, axis, xor_pairs(size, 1 << k))  18.7 us
    all_gather x1, waiting for transfers between devices, local(): proj_b = lax.all_gather(proj_send, 'seq', axis=0, tiled=True)  18.2 us
    dot_general x1, matrix products, local(): jnp.einsum('cfd,hjdk->cfhjk', emb_b, w_all, preferred_element_type=jnp.fl...  14.6 us
    dot_general x1, matrix products, local(): jnp.einsum('cfhjk,hjdk->cfd', d_proj, w_all, preferred_element_type=jnp.f...  13.7 us
  transfers between devices with their start and end apart: 14, of which 13 were waited for; matrix products, arithmetic and copies ran while one was open for 14% of the time, Pallas kernels for 0%

profile of v7, /device:TPU:6, one launch (start us, length us, event | category | flops | bytes accessed | tf_op | source)
XLA Modules:
  0.0 303.9 jit_solution(9093042948010538498)
XLA Ops:
  9.1 5.1 %gather_fusion = bf16[1024,512]{1,0:T(8,128)(2,1)} fusion(bf16[3088,512]{1,0:T(8,128)(2,1)S(1)} %copy-done, s32[1024]{0:T(1024)S(1)} %broadcast_clamp_fusion), kind=kCustom, calls=%fused_computation | custom fusion | bytes 2101248 | tf_op jit(solution)/shard_map/jit(_take)/gather | solution.py:126
  14.2 1.8 select_reduce_fusion
  20.8 2.0 collective-permute-start.1
  23.3 2.9 collective-permute-done.1
  26.3 3.4 %collective-permute-start.2 = (f32[32,512]{1,0:T(8,128)S(1)}, f32[32,512]{1,0:T(8,128)S(1)}, u32[]{:S(2)}, u32[]{:S(2)}) collective-permute-start(f32[32,512]{1,0:T(8,128)S(1)} %add.244), channel_id=1, source_target_pairs={{0,4},{1,5},{2,6},{3,7},{4,0},{5,1},{6,2},{7,3},{8,12},{9,13},{10,... | collective-permute-start | bytes 196616 | tf_op jit(solution)/shard_map/ppermute | solution.py:96
  29.7 5.2 %collective-permute-done.2 = f32[32,512]{1,0:T(8,128)S(1)} collective-permute-done((f32[32,512]{1,0:T(8,128)S(1)}, f32[32,512]{1,0:T(8,128)S(1)}, u32[]{:S(2)}, u32[]{:S(2)}) %collective-permute-start.2) | collective-permute-done | bytes 65568 | tf_op jit(solution)/shard_map/ppermute | solution.py:96
  34.9 7.6 %collective-permute-start.3 = (f32[32,512]{1,0:T(8,128)S(1)}, f32[32,512]{1,0:T(8,128)S(1)}, u32[]{:S(2)}, u32[]{:S(2)}) collective-permute-start(f32[32,512]{1,0:T(8,128)S(1)} %add.245), channel_id=1, source_target_pairs={{0,8},{1,9},{2,10},{3,11},{4,12},{5,13},{6,14},{7,15},{8,0},{9,1},... | collective-permute-start | bytes 196616 | tf_op jit(solution)/shard_map/ppermute | solution.py:96
  43.5 3.6 %collective-permute-done.3 = f32[32,512]{1,0:T(8,128)S(1)} collective-permute-done((f32[32,512]{1,0:T(8,128)S(1)}, f32[32,512]{1,0:T(8,128)S(1)}, u32[]{:S(2)}, u32[]{:S(2)}) %collective-permute-start.3) | collective-permute-done | bytes 65568 | tf_op jit(solution)/shard_map/ppermute | solution.py:96
  47.1 103.4 %all-gather.6.cloned.1.call-done = bf16[48,2048,128]{2,1,0:T(8,128)(2,1)} async-done(((bf16[3,2048,128]{2,1,0:T(8,128)(2,1)}), bf16[48,2048,128]{2,1,0:T(8,128)(2,1)}) %all-gather.6.cloned.1.call-update) | async-done | bytes 25165840 | tf_op jit(solution)/shard_map/all_gather | solution.py:131
  152.4 14.6 %convolution_bitcast_fusion.1 = f32[1,128,16,3,128]{1,4,3,2,0:T(8,128)S(1)} fusion(bf16[16,3,2048,128]{3,2,1,0:T(8,128)(2,1)} %bitcast.205, bf16[1,128,2048]{2,1,0:T(8,128)(2,1)} %convert_bitcast_fusion), kind=kOutput, calls=%fused_computation.8 | convolution fusion | flops 3221225472 | bytes 28835840 | tf_op jit(solution)/shard_map/cfd,hjdk->cfhjk/dot_general | solution.py:150
  168.5 2.6 convert_reduce_fusion.1
  172.1 2.2 copy.72
  175.3 18.2 %all-gather.4.cloned.1.call-done = bf16[2048,512]{1,0:T(8,128)(2,1)} async-done(((bf16[128,512]{1,0:T(8,128)(2,1)}), bf16[2048,512]{1,0:T(8,128)(2,1)}) %all-gather.4.cloned.1.call-update) | async-done | bytes 2097168 | tf_op jit(solution)/shard_map/all_gather | solution.py:148
  193.5 2.0 fusion.64
  197.5 3.4 %fusion.65 = f32[1,2048]{1,0:T(1,128)S(1)} fusion(f32[512,1]{0,1:T(1,128)S(1)} %bitcast.223, bf16[2048,512]{1,0:T(8,128)(2,1)} %all-gather.4.cloned.1.call-done), kind=kOutput, calls=%fused_computation.154 | convolution fusion | flops 12582912 | bytes 2107392 | tf_op jit(solution)/shard_map/dot_general | solution.py:186
  204.9 1.5 fusion.26
  206.4 13.7 %multiply_reduce_fusion = (f32[128]{0:T(128)S(1)}, f32[128,2048]{1,0:T(8,128)S(1)}) fusion(f32[128,2048]{1,0:T(8,128)} %copy-done.7, f32[128]{0:T(128)S(1)} %add_sqrt_fusion.3, bf16[16,3,2048,128]{3,2,1,0:T(8,128)(2,1)} %bitcast.206, bf16[128,16,1,128]{0,3,1,2:T(8,128)(2,1)} %multiply_convert_fusion, bf16[128,16,1,128]{0,3,1,2:T(8,128)(2,1)} %get-tuple-element.74, ...), kind=kOutput, calls=%fused_computation.47 | convolution fusion | flops 3223584768 | bytes 28836864 | tf_op jit(solution)/shard_map/cfhjk,hjdk->cfd/dot_general | solution.py:214
  222.1 1.9 fusion.54
  224.5 2.5 fusion.66
  232.8 3.1 %collective-permute-done.4 = f32[2,2,2,168,256]{4,3,0,1,2:T(8,128)S(1)} collective-permute-done((f32[2,2,2,168,256]{4,3,0,1,2:T(8,128)}, f32[2,2,2,168,256]{4,3,0,1,2:T(8,128)S(1)}, u32[]{:S(2)}, u32[]{:S(2)}) %collective-permute-start.4) | collective-permute-done | bytes 1376288 | tf_op jit(solution)/shard_map/ppermute | solution.py:84
  237.1 1.5 bitcast_add_fusion
  239.5 9.4 %collective-permute-done.5 = bf16[2,2,168,256]{3,2,0,1:T(8,128)(2,1)S(1)} collective-permute-done((bf16[2,2,168,256]{3,2,0,1:T(8,128)(2,1)S(1)}, bf16[2,2,168,256]{3,2,0,1:T(8,128)(2,1)S(1)}, u32[]{:S(2)}, u32[]{:S(2)}) %collective-permute-start.5) | collective-permute-done | bytes 344096 | tf_op jit(solution)/shard_map/ppermute | solution.py:84
  249.0 1.6 collective-permute-start.6
  250.6 8.8 %collective-permute-done.6 = bf16[2,168,256]{2,1,0:T(8,128)(2,1)S(1)} collective-permute-done((bf16[2,168,256]{2,1,0:T(8,128)(2,1)S(1)}, bf16[2,168,256]{2,1,0:T(8,128)(2,1)S(1)}, u32[]{:S(2)}, u32[]{:S(2)}) %collective-permute-start.6) | collective-permute-done | bytes 172064 | tf_op jit(solution)/shard_map/ppermute | solution.py:84
  259.5 3.1 %collective-permute-start.7 = (bf16[168,256]{1,0:T(8,128)(2,1)S(1)}, bf16[168,256]{1,0:T(8,128)(2,1)S(1)}, u32[]{:S(2)}, u32[]{:S(2)}) collective-permute-start(bf16[168,256]{1,0:T(8,128)(2,1)S(1)} %fusion.34), channel_id=1, source_target_pairs={{0,8},{1,9},{2,10},{3,11},{4,12},{5,13},{6,14},{7,15},{8,0},{9,1},... | collective-permute-start | bytes 258056 | tf_op jit(solution)/shard_map/ppermute | solution.py:84
  262.6 6.1 %collective-permute-done.7 = bf16[168,256]{1,0:T(8,128)(2,1)S(1)} collective-permute-done((bf16[168,256]{1,0:T(8,128)(2,1)S(1)}, bf16[168,256]{1,0:T(8,128)(2,1)S(1)}, u32[]{:S(2)}, u32[]{:S(2)}) %collective-permute-start.7) | collective-permute-done | bytes 86048 | tf_op jit(solution)/shard_map/ppermute | solution.py:84
  270.2 2.0 fusion.12
  274.4 3.0 %collective-permute-start.9 = (f32[168,256]{1,0:T(8,128)S(1)}, f32[168,256]{1,0:T(8,128)S(1)}, u32[]{:S(2)}, u32[]{:S(2)}) collective-permute-start(f32[168,256]{1,0:T(8,128)S(1)} %add.272), channel_id=1, source_target_pairs={{0,16},{16,0},{32,48},{48,32},{64,80},{80,64},{96,112},{112,96},{1... | collective-permute-start | bytes 516104 | tf_op jit(solution)/shard_map/ppermute | solution.py:96
  277.4 3.9 %collective-permute-done.9 = f32[168,256]{1,0:T(8,128)S(1)} collective-permute-done((f32[168,256]{1,0:T(8,128)S(1)}, f32[168,256]{1,0:T(8,128)S(1)}, u32[]{:S(2)}, u32[]{:S(2)}) %collective-permute-start.9) | collective-permute-done | bytes 172064 | tf_op jit(solution)/shard_map/ppermute | solution.py:96
  282.3 6.4 %collective-permute-done.10 = f32[168,256]{1,0:T(8,128)S(1)} collective-permute-done((f32[168,256]{1,0:T(8,128)S(1)}, f32[168,256]{1,0:T(8,128)S(1)}, u32[]{:S(2)}, u32[]{:S(2)}) %collective-permute-start.10) | collective-permute-done | bytes 172064 | tf_op jit(solution)/shard_map/ppermute | solution.py:96
  288.8 2.8 fusion.15
  291.6 4.1 %collective-permute-done.11 = f32[168,256]{1,0:T(8,128)S(1)} collective-permute-done((f32[168,256]{1,0:T(8,128)S(1)}, f32[168,256]{1,0:T(8,128)S(1)}, u32[]{:S(2)}, u32[]{:S(2)}) %collective-permute-start.11) | collective-permute-done | bytes 172064 | tf_op jit(solution)/shard_map/ppermute | solution.py:96
  (142 shorter events, 33.1 us)
Async XLA Ops:
  7.2 1.9 copy-start
  7.2 143.4 %all-gather.6.cloned.1.call-start = ((), (), s32[]{:S(2)}) async-start(), calls=%async_computation.1 | async-start | bytes 26738688 | tf_op jit(solution)/shard_map/all_gather | solution.py:131
  7.9 185.6 %all-gather.4.cloned.1.call-start = ((), (), s32[]{:S(2)}) async-start(), calls=%async_computation | async-start | bytes 2228224 | tf_op jit(solution)/shard_map/all_gather | solution.py:148
  9.1 7.6 %copy-start.18 = (bf16[1,2560]{1,0:T(2,128)(2,1)S(1)}, bf16[1,2560]{1,0:T(2,128)(2,1)}, u32[]{:S(2)}) copy-start(bf16[1,2560]{1,0:T(2,128)(2,1)} %param.21) | copy-start | bytes 15364
  9.1 7.6 %copy-start.19 = (bf16[1,2560]{1,0:T(2,128)(2,1)S(1)}, bf16[1,2560]{1,0:T(2,128)(2,1)}, u32[]{:S(2)}) copy-start(bf16[1,2560]{1,0:T(2,128)(2,1)} %param.22) | copy-start | bytes 15364
  14.1 2.6 copy-start.2
  14.2 3.1 %copy-start.13 = (bf16[2560,256]{1,0:T(8,128)(2,1)S(1)}, bf16[2560,256]{1,0:T(8,128)(2,1)}, u32[]{:S(2)}) copy-start(bf16[2560,256]{1,0:T(8,128)(2,1)} %param.25) | copy-start | bytes 3932164
  14.2 3.1 %copy-start.20 = (bf16[1,128,256]{2,1,0:T(8,128)(2,1)S(1)}, bf16[1,128,256]{2,1,0:T(8,128)(2,1)}, u32[]{:S(2)}) copy-start(bf16[1,128,256]{2,1,0:T(8,128)(2,1)} %param.23) | copy-start | bytes 196612
  15.9 4.9 %collective-permute-start = (f32[32,512]{1,0:T(8,128)S(1)}, f32[32,512]{1,0:T(8,128)S(1)}, u32[]{:S(2)}, u32[]{:S(2)}) collective-permute-start(f32[32,512]{1,0:T(8,128)S(1)} %select_reduce_fusion), channel_id=1, source_target_pairs={{0,1},{1,0},{2,3},{3,2},{4,5},{5,4},{6,7},{7,6},{8,9},{9,8},{10,11... | collective-permute-start | bytes 196616 | tf_op jit(solution)/shard_map/ppermute | solution.py:96
  17.3 2.0 copy-start.16
  18.4 4.4 %copy-start.14 = (bf16[256,2048]{1,0:T(8,128)(2,1)S(1)}, bf16[256,2048]{1,0:T(8,128)(2,1)}, u32[]{:S(2)}) copy-start(bf16[256,2048]{1,0:T(8,128)(2,1)} %param.26) | copy-start | bytes 3145732
  20.8 5.4 %collective-permute-start.1 = (f32[32,512]{1,0:T(8,128)S(1)}, f32[32,512]{1,0:T(8,128)S(1)}, u32[]{:S(2)}, u32[]{:S(2)}) collective-permute-start(f32[32,512]{1,0:T(8,128)S(1)} %add.243), channel_id=1, source_target_pairs={{0,2},{1,3},{2,0},{3,1},{4,6},{5,7},{6,4},{7,5},{8,10},{9,11},{10,... | collective-permute-start | bytes 196616 | tf_op jit(solution)/shard_map/ppermute | solution.py:96
  23.3 129.1 %copy-start.7 = (f32[128,2048]{1,0:T(8,128)}, f32[128,2048]{1,0:T(8,128)S(1)}, u32[]{:S(2)}) copy-start(f32[128,2048]{1,0:T(8,128)S(1)} %get-tuple-element.88) | copy-start | bytes 3145732
  23.3 127.3 %copy-start.21 = (s32[16]{0:T(128)S(1)}, s32[16]{0:T(128)}, u32[]{:S(2)}) copy-start(s32[16]{0:T(128)} %param.32) | copy-start | bytes 196
  23.3 127.9 %copy-start.22 = (f32[16]{0:T(128)S(1)}, f32[16]{0:T(128)}, u32[]{:S(2)}) copy-start(f32[16]{0:T(128)} %param.33) | copy-start | bytes 196
  26.3 8.6 %collective-permute-start.2 = (f32[32,512]{1,0:T(8,128)S(1)}, f32[32,512]{1,0:T(8,128)S(1)}, u32[]{:S(2)}, u32[]{:S(2)}) collective-permute-start(f32[32,512]{1,0:T(8,128)S(1)} %add.244), channel_id=1, source_target_pairs={{0,4},{1,5},{2,6},{3,7},{4,0},{5,1},{6,2},{7,3},{8,12},{9,13},{10,... | collective-permute-start | bytes 196616 | tf_op jit(solution)/shard_map/ppermute | solution.py:96
  34.9 12.2 %collective-permute-start.3 = (f32[32,512]{1,0:T(8,128)S(1)}, f32[32,512]{1,0:T(8,128)S(1)}, u32[]{:S(2)}, u32[]{:S(2)}) collective-permute-start(f32[32,512]{1,0:T(8,128)S(1)} %add.245), channel_id=1, source_target_pairs={{0,8},{1,9},{2,10},{3,11},{4,12},{5,13},{6,14},{7,15},{8,0},{9,1},... | collective-permute-start | bytes 196616 | tf_op jit(solution)/shard_map/ppermute | solution.py:96
  197.4 3.9 %copy-start.9 = (f32[16,128,128]{1,2,0:T(8,128)S(1)}, f32[16,128,128]{1,2,0:T(8,128)}, u32[]{:S(2)}) copy-start(f32[16,128,128]{1,2,0:T(8,128)} %get-tuple-element.90) | copy-start | bytes 3145732
  206.4 13.7 %copy-start.8 = (f32[128,2048]{1,0:T(8,128)S(1)}, f32[128,2048]{1,0:T(8,128)}, u32[]{:S(2)}) copy-start(f32[128,2048]{1,0:T(8,128)} %copy-done.7) | copy-start | bytes 3145732
  224.5 4.7 %copy-start.10 = (bf16[1,2560,128]{2,1,0:T(8,128)(2,1)S(1)}, bf16[1,2560,128]{2,1,0:T(8,128)(2,1)}, u32[]{:S(2)}) copy-start(bf16[1,2560,128]{2,1,0:T(8,128)(2,1)} %copy.72) | copy-start | bytes 1966084
  231.4 5.7 %copy-start.6 = (f32[2,2,2,1,168,256]{5,4,3,2,1,0:T(8,128)S(1)}, f32[2,2,2,1,168,256]{5,4,3,2,1,0:T(8,128)}, u32[]{:S(2)}) copy-start(f32[2,2,2,1,168,256]{5,4,3,2,1,0:T(8,128)} %get-tuple-element.77) | copy-start | bytes 4128772
  232.6 3.3 %collective-permute-start.4 = (f32[2,2,2,168,256]{4,3,0,1,2:T(8,128)}, f32[2,2,2,168,256]{4,3,0,1,2:T(8,128)S(1)}, u32[]{:S(2)}, u32[]{:S(2)}) collective-permute-start(f32[2,2,2,168,256]{4,3,0,1,2:T(8,128)} %bitcast.203), channel_id=1, source_target_pairs={{0,1},{1,0},{2,3},{3,2},{4,5},{5,4},{6,7},{7,6},{8,9},{9,8},{10,11... | collective-permute-start | bytes 4128776 | tf_op jit(solution)/shard_map/ppermute | solution.py:84
  238.6 10.3 %collective-permute-start.5 = (bf16[2,2,168,256]{3,2,0,1:T(8,128)(2,1)S(1)}, bf16[2,2,168,256]{3,2,0,1:T(8,128)(2,1)S(1)}, u32[]{:S(2)}, u32[]{:S(2)}) collective-permute-start(bf16[2,2,168,256]{3,2,0,1:T(8,128)(2,1)S(1)} %fusion.28), channel_id=1, source_target_pairs={{0,2},{1,3},{2,0},{3,1},{4,6},{5,7},{6,4},{7,5},{8,10},{9,11},{10,... | collective-permute-start | bytes 1032200 | tf_op jit(solution)/shard_map/ppermute | solution.py:84
  239.5 30.7 %copy-start.3 = (bf16[1,128,2560]{2,1,0:T(8,128)(2,1)S(1)}, bf16[1,128,2560]{2,1,0:T(8,128)(2,1)}, u32[]{:S(2)}) copy-start(bf16[1,128,2560]{2,1,0:T(8,128)(2,1)} %param.20) | copy-start | bytes 1966084
  249.0 10.4 %collective-permute-start.6 = (bf16[2,168,256]{2,1,0:T(8,128)(2,1)S(1)}, bf16[2,168,256]{2,1,0:T(8,128)(2,1)S(1)}, u32[]{:S(2)}, u32[]{:S(2)}) collective-permute-start(bf16[2,168,256]{2,1,0:T(8,128)(2,1)S(1)} %fusion.33), channel_id=1, source_target_pairs={{0,4},{1,5},{2,6},{3,7},{4,0},{5,1},{6,2},{7,3},{8,12},{9,13},{10,... | collective-permute-start | bytes 516104 | tf_op jit(solution)/shard_map/ppermute | solution.py:84
  259.5 9.2 %collective-permute-start.7 = (bf16[168,256]{1,0:T(8,128)(2,1)S(1)}, bf16[168,256]{1,0:T(8,128)(2,1)S(1)}, u32[]{:S(2)}, u32[]{:S(2)}) collective-permute-start(bf16[168,256]{1,0:T(8,128)(2,1)S(1)} %fusion.34), channel_id=1, source_target_pairs={{0,8},{1,9},{2,10},{3,11},{4,12},{5,13},{6,14},{7,15},{8,0},{9,1},... | collective-permute-start | bytes 258056 | tf_op jit(solution)/shard_map/ppermute | solution.py:84
  268.7 5.6 %collective-permute-start.8 = (f32[168,256]{1,0:T(8,128)S(1)}, f32[168,256]{1,0:T(8,128)S(1)}, u32[]{:S(2)}, u32[]{:S(2)}) collective-permute-start(f32[168,256]{1,0:T(8,128)S(1)} %bitcast_add_fusion.3), channel_id=1, source_target_pairs={{0,128},{128,0},{1,129},{129,1},{2,130},{130,2},{3,131},{131,3},{4... | collective-permute-start | bytes 516104 | tf_op jit(solution)/shard_map/ppermute | solution.py:96
  273.4 15.4 %copy-start.4 = (bf16[1,128,2560]{2,1,0:T(8,128)(2,1)S(1)}, bf16[1,128,2560]{2,1,0:T(8,128)(2,1)}, u32[]{:S(2)}) copy-start(bf16[1,128,2560]{2,1,0:T(8,128)(2,1)} %param.20) | copy-start | bytes 1966084
  274.4 7.0 %collective-permute-start.9 = (f32[168,256]{1,0:T(8,128)S(1)}, f32[168,256]{1,0:T(8,128)S(1)}, u32[]{:S(2)}, u32[]{:S(2)}) collective-permute-start(f32[168,256]{1,0:T(8,128)S(1)} %add.272), channel_id=1, source_target_pairs={{0,16},{16,0},{32,48},{48,32},{64,80},{80,64},{96,112},{112,96},{1... | collective-permute-start | bytes 516104 | tf_op jit(solution)/shard_map/ppermute | solution.py:96
  281.4 7.3 %collective-permute-start.10 = (f32[168,256]{1,0:T(8,128)S(1)}, f32[168,256]{1,0:T(8,128)S(1)}, u32[]{:S(2)}, u32[]{:S(2)}) collective-permute-start(f32[168,256]{1,0:T(8,128)S(1)} %add.273), channel_id=1, source_target_pairs={{0,32},{16,48},{32,0},{48,16},{64,96},{80,112},{96,64},{112,80},{1... | collective-permute-start | bytes 516104 | tf_op jit(solution)/shard_map/ppermute | solution.py:96
  288.7 8.3 %copy-start.1 = (bf16[3088,512]{1,0:T(8,128)(2,1)S(1)}, bf16[3088,512]{1,0:T(8,128)(2,1)}, u32[]{:S(2)}) copy-start(bf16[3088,512]{1,0:T(8,128)(2,1)} %param.30) | copy-start | bytes 9486340
  288.7 7.0 %collective-permute-start.11 = (f32[168,256]{1,0:T(8,128)S(1)}, f32[168,256]{1,0:T(8,128)S(1)}, u32[]{:S(2)}, u32[]{:S(2)}) collective-permute-start(f32[168,256]{1,0:T(8,128)S(1)} %add.274), channel_id=1, source_target_pairs={{0,64},{16,80},{32,96},{48,112},{64,0},{80,16},{96,32},{112,48},{1... | collective-permute-start | bytes 516104 | tf_op jit(solution)/shard_map/ppermute | solution.py:96
  (5 other events, 5.2 us)
Sparse Core Ops, SparseCore 0:
  9.9 140.6 all-gather.5
  152.4 41.0 all-gather.3

commit v8 on v7

--- a/solution.py
+++ b/solution.py
@@ -86,6 +86,19 @@
         if k == 0:
             buf, ride = lax.optimization_barrier((buf, ride))
     return buf, ride
+
+
+def doubling_gather(value, axis):
+    size = lax.axis_size(axis)
+    me = lax.axis_index(axis)
+    bits = size.bit_length() - 1
+    assert 1 << bits == size
+    held = value[None]
+    for k in reversed(range(bits)):
+        held = jnp.concatenate([held, lax.ppermute(held, axis, xor_pairs(size, 1 << k))], axis=0)
+    wanted = jnp.arange(size) ^ me
+    position = sum(((wanted >> k) & 1) << (bits - 1 - k) for k in range(bits))
+    return jnp.take(held, position, axis=0)
 
 
 def doubling_sum(value, axis):
@@ -145,7 +158,7 @@
         (w_all, w_proj, normed_e.astype(jnp.bfloat16), text_raw, jnp.swapaxes(modulated, 1, 2))
     )
     text_unit, text_len = unit_rows(text_raw)
-    proj_b = lax.all_gather(proj_send, "seq", axis=0, tiled=True)
+    proj_b = doubling_gather(proj_send, "seq").reshape(ways * w_proj.shape[0], w_proj.shape[1])
     proj_rows = proj_b.astype(jnp.float32)
     projected = jnp.einsum(
         "cfd,hjdk->cfhjk",

time: 304 us -> 330 us (1.086)
  local copies, waits for them, and re-layouts: 18 us -> 30.3 us
  other arithmetic: 21.4 us -> 27.3 us
    ppermute x0 -> x4, waiting for transfers between devices: none -> 20.9 us  [doubling_gather(): lax.ppermute(held, axis, xor_pairs(size, 1 << k))]
    all_gather x1 -> x0, waiting for transfers between devices: 18.2 us -> none  [local(): proj_b = lax.all_gather(proj_send, 'seq', axis=0, tiled=True)]
    ppermute x0 -> x4, starting transfers between devices: none -> 6.66 us  [doubling_gather(): lax.ppermute(held, axis, xor_pairs(size, 1 << k))]
    unnamed x48 -> x122, local copies, waits for them, and re-layouts: 3.92 us -> 9.59 us
    gather x0 -> x1, local copies, waits for them, and re-layouts: none -> 3.81 us  [doubling_gather(): return jnp.take(held, position, axis=0)]
  transfers between devices with their start and end apart: 14 -> 17, of which waited for: 13 -> 14; matrix products, arithmetic and copies ran while one was open for 14% -> 15% of each run, Pallas kernels for 0% -> 0%
where the time goes in v8:
time: 330 us; the launch traced here: 329 us
  waiting for transfers between devices  179 us (54%)
  matrix products  47.3 us (14%)
  local copies, waits for them, and re-layouts  30.3 us (9%)
  starting transfers between devices  27.6 us (8%)
  other arithmetic  27.3 us (8%)
  between operations  17.5 us (5%)
    all_gather x1, waiting for transfers between devices, local(): w_all = lax.all_gather(w_qkv, 'seq', axis=0)  100 us
    ppermute x4, waiting for transfers between devices, halving_sum(): lax.ppermute(send.astype(wire_types[k]), axis, xor_pairs(size, 1 << k))  29.4 us
    ppermute x8, waiting for transfers between devices, doubling_sum(): value = value + lax.ppermute(value, axis, xor_pairs(size, 1 << k))  27.9 us
    ppermute x4, waiting for transfers between devices, doubling_gather(): lax.ppermute(held, axis, xor_pairs(size, 1 << k))  20.9 us
    ppermute x8, starting transfers between devices, doubling_sum(): value = value + lax.ppermute(value, axis, xor_pairs(size, 1 << k))  17.7 us
    dot_general x1, matrix products, local(): jnp.einsum('cfd,hjdk->cfhjk', emb_b, w_all, preferred_element_type=jnp.fl...  14.6 us
    dot_general x1, matrix products, local(): jnp.einsum('cfhjk,hjdk->cfd', d_proj, w_all, preferred_element_type=jnp.f...  13.6 us
    unnamed x122, local copies, waits for them, and re-layouts  9.59 us
  transfers between devices with their start and end apart: 17, of which 14 were waited for; matrix products, arithmetic and copies ran while one was open for 15% of the time, Pallas kernels for 0%

profile of v8, /device:TPU:6, one launch (start us, length us, event | category | flops | bytes accessed | tf_op | source)
XLA Modules:
  0.0 329.0 jit_solution(8977212623012462129)
XLA Ops:
  9.1 5.1 %gather_fusion = bf16[1024,512]{1,0:T(8,128)(2,1)} fusion(bf16[3088,512]{1,0:T(8,128)(2,1)S(1)} %copy-done, s32[1024]{0:T(1024)S(1)} %broadcast_clamp_fusion), kind=kCustom, calls=%fused_computation | custom fusion | bytes 2101248 | tf_op jit(solution)/shard_map/jit(_take)/gather | solution.py:139
  25.0 2.0 collective-permute-start.1
  27.0 4.3 %collective-permute-done.1 = f32[32,512]{1,0:T(8,128)S(1)} collective-permute-done((f32[32,512]{1,0:T(8,128)S(1)}, f32[32,512]{1,0:T(8,128)S(1)}, u32[]{:S(2)}, u32[]{:S(2)}) %collective-permute-start.1) | collective-permute-done | bytes 65568 | tf_op jit(solution)/shard_map/ppermute | solution.py:109
  31.3 3.3 %collective-permute-start.2 = (f32[32,512]{1,0:T(8,128)S(1)}, f32[32,512]{1,0:T(8,128)S(1)}, u32[]{:S(2)}, u32[]{:S(2)}) collective-permute-start(f32[32,512]{1,0:T(8,128)S(1)} %add.301), channel_id=1, source_target_pairs={{0,4},{1,5},{2,6},{3,7},{4,0},{5,1},{6,2},{7,3},{8,12},{9,13},{10,... | collective-permute-start | bytes 196616 | tf_op jit(solution)/shard_map/ppermute | solution.py:109
  35.2 4.9 %collective-permute-done.2 = f32[32,512]{1,0:T(8,128)S(1)} collective-permute-done((f32[32,512]{1,0:T(8,128)S(1)}, f32[32,512]{1,0:T(8,128)S(1)}, u32[]{:S(2)}, u32[]{:S(2)}) %collective-permute-start.2) | collective-permute-done | bytes 65568 | tf_op jit(solution)/shard_map/ppermute | solution.py:109
  40.1 6.5 %collective-permute-start.3 = (f32[32,512]{1,0:T(8,128)S(1)}, f32[32,512]{1,0:T(8,128)S(1)}, u32[]{:S(2)}, u32[]{:S(2)}) collective-permute-start(f32[32,512]{1,0:T(8,128)S(1)} %add.302), channel_id=1, source_target_pairs={{0,8},{1,9},{2,10},{3,11},{4,12},{5,13},{6,14},{7,15},{8,0},{9,1},... | collective-permute-start | bytes 196616 | tf_op jit(solution)/shard_map/ppermute | solution.py:109
  47.2 3.8 %collective-permute-done.3 = f32[32,512]{1,0:T(8,128)S(1)} collective-permute-done((f32[32,512]{1,0:T(8,128)S(1)}, f32[32,512]{1,0:T(8,128)S(1)}, u32[]{:S(2)}, u32[]{:S(2)}) %collective-permute-start.3) | collective-permute-done | bytes 65568 | tf_op jit(solution)/shard_map/ppermute | solution.py:109
  51.1 100.3 %all-gather.3.cloned.1.call-done = bf16[48,2048,128]{2,1,0:T(8,128)(2,1)} async-done(((bf16[3,2048,128]{2,1,0:T(8,128)(2,1)}), bf16[48,2048,128]{2,1,0:T(8,128)(2,1)}) %all-gather.3.cloned.1.call-update) | async-done | bytes 25165840 | tf_op jit(solution)/shard_map/all_gather | solution.py:144
  151.3 4.8 %collective-permute-start.4 = (bf16[1,128,512]{2,1,0:T(8,128)(2,1)S(1)}, bf16[1,128,512]{2,1,0:T(8,128)(2,1)S(1)}, u32[]{:S(2)}, u32[]{:S(2)}) collective-permute-start(bf16[1,128,512]{2,1,0:T(8,128)(2,1)S(1)} %bitcast.208), channel_id=1, source_target_pairs={{0,8},{1,9},{2,10},{3,11},{4,12},{5,13},{6,14},{7,15},{8,0},{9,1},... | collective-permute-start | bytes 393224 | tf_op jit(solution)/shard_map/ppermute | solution.py:98
  156.1 14.6 %convolution_bitcast_fusion.1 = f32[1,128,16,3,128]{1,4,3,2,0:T(8,128)S(1)} fusion(bf16[16,3,2048,128]{3,2,1,0:T(8,128)(2,1)} %bitcast.204, bf16[1,128,2048]{2,1,0:T(8,128)(2,1)} %convert_bitcast_fusion), kind=kOutput, calls=%fused_computation.10 | convolution fusion | flops 3221225472 | bytes 28835840 | tf_op jit(solution)/shard_map/cfd,hjdk->cfhjk/dot_general | solution.py:163
  175.5 11.7 %collective-permute-done.5 = bf16[2,128,512]{2,1,0:T(8,128)(2,1)S(1)} collective-permute-done((bf16[2,128,512]{2,1,0:T(8,128)(2,1)S(1)}, bf16[2,128,512]{2,1,0:T(8,128)(2,1)S(1)}, u32[]{:S(2)}, u32[]{:S(2)}) %collective-permute-start.5) | collective-permute-done | bytes 262176 | tf_op jit(solution)/shard_map/ppermute | solution.py:98
  188.1 2.6 convert_reduce_fusion.1
  192.3 9.1 %collective-permute-done.6 = bf16[4,128,512]{2,1,0:T(8,128)(2,1)} collective-permute-done((bf16[4,128,512]{2,1,0:T(8,128)(2,1)}, bf16[4,128,512]{2,1,0:T(8,128)(2,1)}, u32[]{:S(2)}, u32[]{:S(2)}) %collective-permute-start.6) | collective-permute-done | bytes 524320 | tf_op jit(solution)/shard_map/ppermute | solution.py:98
  201.4 2.1 pad_maximum_fusion.2
  203.5 2.2 copy.72
  213.5 2.3 constant_dynamic-update-slice_fusion
  215.8 3.8 %gather_fusion.1 = bf16[16,128,512]{2,1,0:T(8,128)(2,1)} fusion(bf16[16,128,512]{2,1,0:T(8,128)(2,1)} %constant_dynamic-update-slice_fusion, s32[1024]{0:T(1024)} %pad_clamp_fusion), kind=kCustom, calls=%fused_computation.1 | custom fusion | bytes 4194368 | tf_op jit(solution)/shard_map/jit(_take)/gather | solution.py:101
  219.6 2.0 fusion.24
  223.7 3.5 %fusion.23 = f32[1,16,128]{2,0,1:T(1,128)S(1)} fusion(f32[512,1,1]{0,1,2:T(1,128)S(1)} %bitcast.231, bf16[16,128,512]{2,1,0:T(8,128)(2,1)} %gather_fusion.1, pred[16]{0:T(512)(128)(4,1)S(1)} %copy-done.57), kind=kOutput, calls=%fused_computation.64 | convolution fusion | flops 13631488 | bytes 2107408 | tf_op jit(solution)/shard_map/dot_general | solution.py:199
  232.7 13.6 %multiply_reduce_fusion = (f32[128]{0:T(128)S(1)}, f32[128,2048]{1,0:T(8,128)S(1)}) fusion(f32[128,2048]{1,0:T(8,128)} %copy-done.7, f32[128]{0:T(128)S(1)} %copy-done.46, bf16[16,3,2048,128]{3,2,1,0:T(8,128)(2,1)} %bitcast.205, bf16[128,16,1,128]{0,3,1,2:T(8,128)(2,1)} %multiply_convert_fusion, bf16[128,16,1,128]{0,3,1,2:T(8,128)(2,1)} %get-tuple-element.74, ...), kind=kOutput, calls=%fused_computation.50 | convolution fusion | flops 3223584768 | bytes 28836864 | tf_op jit(solution)/shard_map/cfhjk,hjdk->cfd/dot_general | solution.py:227
  248.4 1.9 fusion.58
  250.8 2.5 fusion.70
  259.4 3.0 collective-permute-done.8
  265.4 10.0 %collective-permute-done.9 = bf16[2,2,168,256]{3,2,0,1:T(8,128)(2,1)S(1)} collective-permute-done((bf16[2,2,168,256]{3,2,0,1:T(8,128)(2,1)S(1)}, bf16[2,2,168,256]{3,2,0,1:T(8,128)(2,1)S(1)}, u32[]{:S(2)}, u32[]{:S(2)}) %collective-permute-start.9) | collective-permute-done | bytes 344096 | tf_op jit(solution)/shard_map/ppermute | solution.py:84
  276.4 9.4 %collective-permute-done.10 = bf16[2,168,256]{2,1,0:T(8,128)(2,1)S(1)} collective-permute-done((bf16[2,168,256]{2,1,0:T(8,128)(2,1)S(1)}, bf16[2,168,256]{2,1,0:T(8,128)(2,1)S(1)}, u32[]{:S(2)}, u32[]{:S(2)}) %collective-permute-start.10) | collective-permute-done | bytes 172064 | tf_op jit(solution)/shard_map/ppermute | solution.py:84
  287.3 7.0 %collective-permute-done.11 = bf16[168,256]{1,0:T(8,128)(2,1)S(1)} collective-permute-done((bf16[168,256]{1,0:T(8,128)(2,1)S(1)}, bf16[168,256]{1,0:T(8,128)(2,1)S(1)}, u32[]{:S(2)}, u32[]{:S(2)}) %collective-permute-start.11) | collective-permute-done | bytes 86048 | tf_op jit(solution)/shard_map/ppermute | solution.py:84
  296.0 2.0 fusion.12
  299.9 3.1 collective-permute-start.13
  303.0 3.9 %collective-permute-done.13 = f32[168,256]{1,0:T(8,128)S(1)} collective-permute-done((f32[168,256]{1,0:T(8,128)S(1)}, f32[168,256]{1,0:T(8,128)S(1)}, u32[]{:S(2)}, u32[]{:S(2)}) %collective-permute-start.13) | collective-permute-done | bytes 172064 | tf_op jit(solution)/shard_map/ppermute | solution.py:109
  307.9 6.0 %collective-permute-done.14 = f32[168,256]{1,0:T(8,128)S(1)} collective-permute-done((f32[168,256]{1,0:T(8,128)S(1)}, f32[168,256]{1,0:T(8,128)S(1)}, u32[]{:S(2)}, u32[]{:S(2)}) %collective-permute-start.14) | collective-permute-done | bytes 172064 | tf_op jit(solution)/shard_map/ppermute | solution.py:109
  314.0 2.6 fusion.15
  316.6 4.3 %collective-permute-done.15 = f32[168,256]{1,0:T(8,128)S(1)} collective-permute-done((f32[168,256]{1,0:T(8,128)S(1)}, f32[168,256]{1,0:T(8,128)S(1)}, u32[]{:S(2)}, u32[]{:S(2)}) %collective-permute-start.15) | collective-permute-done | bytes 172064 | tf_op jit(solution)/shard_map/ppermute | solution.py:109
  (228 shorter events, 53.2 us)
Async XLA Ops:
  7.2 144.1 %all-gather.3.cloned.1.call-start = ((), (), s32[]{:S(2)}) async-start(), calls=%async_computation | async-start | bytes 26738688 | tf_op jit(solution)/shard_map/all_gather | solution.py:144
  15.9 9.0 %collective-permute-start = (f32[32,512]{1,0:T(8,128)S(1)}, f32[32,512]{1,0:T(8,128)S(1)}, u32[]{:S(2)}, u32[]{:S(2)}) collective-permute-start(f32[32,512]{1,0:T(8,128)S(1)} %select_reduce_fusion), channel_id=1, source_target_pairs={{0,1},{1,0},{2,3},{3,2},{4,5},{5,4},{6,7},{7,6},{8,9},{9,8},{10,11... | collective-permute-start | bytes 196616 | tf_op jit(solution)/shard_map/ppermute | solution.py:109
  20.6 130.7 %copy-start.7 = (f32[128,2048]{1,0:T(8,128)}, f32[128,2048]{1,0:T(8,128)S(1)}, u32[]{:S(2)}) copy-start(f32[128,2048]{1,0:T(8,128)S(1)} %get-tuple-element.88) | copy-start | bytes 3145732
  20.7 130.6 %copy-start.12 = (bf16[128,512]{1,0:T(8,128)(2,1)S(1)}, bf16[128,512]{1,0:T(8,128)(2,1)}, u32[]{:S(2)}) copy-start(bf16[128,512]{1,0:T(8,128)(2,1)} %param.29) | copy-start | bytes 393220
  25.0 6.3 %collective-permute-start.1 = (f32[32,512]{1,0:T(8,128)S(1)}, f32[32,512]{1,0:T(8,128)S(1)}, u32[]{:S(2)}, u32[]{:S(2)}) collective-permute-start(f32[32,512]{1,0:T(8,128)S(1)} %add.300), channel_id=1, source_target_pairs={{0,2},{1,3},{2,0},{3,1},{4,6},{5,7},{6,4},{7,5},{8,10},{9,11},{10,... | collective-permute-start | bytes 196616 | tf_op jit(solution)/shard_map/ppermute | solution.py:109
  31.3 8.8 %collective-permute-start.2 = (f32[32,512]{1,0:T(8,128)S(1)}, f32[32,512]{1,0:T(8,128)S(1)}, u32[]{:S(2)}, u32[]{:S(2)}) collective-permute-start(f32[32,512]{1,0:T(8,128)S(1)} %add.301), channel_id=1, source_target_pairs={{0,4},{1,5},{2,6},{3,7},{4,0},{5,1},{6,2},{7,3},{8,12},{9,13},{10,... | collective-permute-start | bytes 196616 | tf_op jit(solution)/shard_map/ppermute | solution.py:109
  40.1 10.9 %collective-permute-start.3 = (f32[32,512]{1,0:T(8,128)S(1)}, f32[32,512]{1,0:T(8,128)S(1)}, u32[]{:S(2)}, u32[]{:S(2)}) collective-permute-start(f32[32,512]{1,0:T(8,128)S(1)} %add.302), channel_id=1, source_target_pairs={{0,8},{1,9},{2,10},{3,11},{4,12},{5,13},{6,14},{7,15},{8,0},{9,1},... | collective-permute-start | bytes 196616 | tf_op jit(solution)/shard_map/ppermute | solution.py:109
  51.0 120.0 %copy-start.25 = (f32[32,512]{1,0:T(8,128)}, f32[32,512]{1,0:T(8,128)S(1)}, u32[]{:S(2)}) copy-start(f32[32,512]{1,0:T(8,128)S(1)} %add.303) | copy-start | bytes 196612
  151.3 20.4 %collective-permute-start.4 = (bf16[1,128,512]{2,1,0:T(8,128)(2,1)S(1)}, bf16[1,128,512]{2,1,0:T(8,128)(2,1)S(1)}, u32[]{:S(2)}, u32[]{:S(2)}) collective-permute-start(bf16[1,128,512]{2,1,0:T(8,128)(2,1)S(1)} %bitcast.208), channel_id=1, source_target_pairs={{0,8},{1,9},{2,10},{3,11},{4,12},{5,13},{6,14},{7,15},{8,0},{9,1},... | collective-permute-start | bytes 393224 | tf_op jit(solution)/shard_map/ppermute | solution.py:98
  172.4 14.8 %copy-start.14 = (bf16[1,128,512]{2,1,0:T(8,128)(2,1)S(1)}, bf16[1,128,512]{2,1,0:T(8,128)(2,1)}, u32[]{:S(2)}) copy-start(bf16[1,128,512]{2,1,0:T(8,128)(2,1)} %copy-done.13) | copy-start | bytes 393220
  172.4 14.8 %collective-permute-start.5 = (bf16[2,128,512]{2,1,0:T(8,128)(2,1)S(1)}, bf16[2,128,512]{2,1,0:T(8,128)(2,1)S(1)}, u32[]{:S(2)}, u32[]{:S(2)}) collective-permute-start(bf16[2,128,512]{2,1,0:T(8,128)(2,1)S(1)} %pad_maximum_fusion.4), channel_id=1, source_target_pairs={{0,4},{1,5},{2,6},{3,7},{4,0},{5,1},{6,2},{7,3},{8,12},{9,13},{10,... | collective-permute-start | bytes 786440 | tf_op jit(solution)/shard_map/ppermute | solution.py:98
  188.1 13.3 %collective-permute-start.6 = (bf16[4,128,512]{2,1,0:T(8,128)(2,1)}, bf16[4,128,512]{2,1,0:T(8,128)(2,1)}, u32[]{:S(2)}, u32[]{:S(2)}) collective-permute-start(bf16[4,128,512]{2,1,0:T(8,128)(2,1)} %pad_maximum_fusion.3), channel_id=1, source_target_pairs={{0,2},{1,3},{2,0},{3,1},{4,6},{5,7},{6,4},{7,5},{8,10},{9,11},{10,... | collective-permute-start | bytes 1572872 | tf_op jit(solution)/shard_map/ppermute | solution.py:98
  190.7 12.8 %copy-start.30 = (f32[16,128]{1,0:T(8,128)}, f32[16,128]{1,0:T(8,128)S(1)}, u32[]{:S(2)}) copy-start(f32[16,128]{1,0:T(8,128)S(1)} %get-tuple-element.89) | copy-start | bytes 24580
  190.7 12.8 %copy-start.53 = (f32[32]{0:T(128)S(1)}, f32[32]{0:T(128)}, u32[]{:S(2)}) copy-start(f32[32]{0:T(128)} %multiply_reduce_fusion.9) | copy-start | bytes 388
  203.5 10.0 %collective-permute-start.7 = (bf16[8,128,512]{2,1,0:T(8,128)(2,1)}, bf16[8,128,512]{2,1,0:T(8,128)(2,1)}, u32[]{:S(2)}, u32[]{:S(2)}) collective-permute-start(bf16[8,128,512]{2,1,0:T(8,128)(2,1)} %pad_maximum_fusion.2), channel_id=1, source_target_pairs={{0,1},{1,0},{2,3},{3,2},{4,5},{5,4},{6,7},{7,6},{8,9},{9,8},{10,11... | collective-permute-start | bytes 3145736 | tf_op jit(solution)/shard_map/ppermute | solution.py:98
  232.7 13.6 %copy-start.8 = (f32[128,2048]{1,0:T(8,128)S(1)}, f32[128,2048]{1,0:T(8,128)}, u32[]{:S(2)}) copy-start(f32[128,2048]{1,0:T(8,128)} %copy-done.7) | copy-start | bytes 3145732
  232.7 13.6 %copy-start.33 = (f32[1,2048]{1,0:T(1,128)S(1)}, f32[1,2048]{1,0:T(1,128)}, u32[]{:S(2)}) copy-start(f32[1,2048]{1,0:T(1,128)} %copy-done.32) | copy-start | bytes 24580
  232.7 13.6 %copy-start.35 = (f32[1,2048]{1,0:T(1,128)S(1)}, f32[1,2048]{1,0:T(1,128)}, u32[]{:S(2)}) copy-start(f32[1,2048]{1,0:T(1,128)} %copy-done.34) | copy-start | bytes 24580
  258.9 3.5 %collective-permute-start.8 = (f32[2,2,2,168,256]{4,3,0,1,2:T(8,128)}, f32[2,2,2,168,256]{4,3,0,1,2:T(8,128)S(1)}, u32[]{:S(2)}, u32[]{:S(2)}) collective-permute-start(f32[2,2,2,168,256]{4,3,0,1,2:T(8,128)} %bitcast.202), channel_id=1, source_target_pairs={{0,1},{1,0},{2,3},{3,2},{4,5},{5,4},{6,7},{7,6},{8,9},{9,8},{10,11... | collective-permute-start | bytes 4128776 | tf_op jit(solution)/shard_map/ppermute | solution.py:84
  265.0 10.4 %collective-permute-start.9 = (bf16[2,2,168,256]{3,2,0,1:T(8,128)(2,1)S(1)}, bf16[2,2,168,256]{3,2,0,1:T(8,128)(2,1)S(1)}, u32[]{:S(2)}, u32[]{:S(2)}) collective-permute-start(bf16[2,2,168,256]{3,2,0,1:T(8,128)(2,1)S(1)} %fusion.30), channel_id=1, source_target_pairs={{0,2},{1,3},{2,0},{3,1},{4,6},{5,7},{6,4},{7,5},{8,10},{9,11},{10,... | collective-permute-start | bytes 1032200 | tf_op jit(solution)/shard_map/ppermute | solution.py:84
  265.4 30.5 %copy-start.3 = (bf16[1,128,2560]{2,1,0:T(8,128)(2,1)S(1)}, bf16[1,128,2560]{2,1,0:T(8,128)(2,1)}, u32[]{:S(2)}) copy-start(bf16[1,128,2560]{2,1,0:T(8,128)(2,1)} %param.20) | copy-start | bytes 1966084
  265.4 30.5 %copy-start.27 = (f32[2560]{0:T(1024)S(1)}, f32[2560]{0:T(1024)}, u32[]{:S(2)}) copy-start(f32[2560]{0:T(1024)} %copy-done.26) | copy-start | bytes 30724
  265.4 30.5 %copy-start.41 = (f32[128]{0:T(128)S(1)}, f32[128]{0:T(128)}, u32[]{:S(2)}) copy-start(f32[128]{0:T(128)} %copy-done.40) | copy-start | bytes 1540
  265.4 30.5 %copy-start.43 = (f32[128]{0:T(128)S(1)}, f32[128]{0:T(128)}, u32[]{:S(2)}) copy-start(f32[128]{0:T(128)} %copy-done.42) | copy-start | bytes 1540
  275.6 10.2 %collective-permute-start.10 = (bf16[2,168,256]{2,1,0:T(8,128)(2,1)S(1)}, bf16[2,168,256]{2,1,0:T(8,128)(2,1)S(1)}, u32[]{:S(2)}, u32[]{:S(2)}) collective-permute-start(bf16[2,168,256]{2,1,0:T(8,128)(2,1)S(1)} %fusion.35), channel_id=1, source_target_pairs={{0,4},{1,5},{2,6},{3,7},{4,0},{5,1},{6,2},{7,3},{8,12},{9,13},{10,... | collective-permute-start | bytes 516104 | tf_op jit(solution)/shard_map/ppermute | solution.py:84
  285.9 8.5 %collective-permute-start.11 = (bf16[168,256]{1,0:T(8,128)(2,1)S(1)}, bf16[168,256]{1,0:T(8,128)(2,1)S(1)}, u32[]{:S(2)}, u32[]{:S(2)}) collective-permute-start(bf16[168,256]{1,0:T(8,128)(2,1)S(1)} %fusion.36), channel_id=1, source_target_pairs={{0,8},{1,9},{2,10},{3,11},{4,12},{5,13},{6,14},{7,15},{8,0},{9,1},... | collective-permute-start | bytes 258056 | tf_op jit(solution)/shard_map/ppermute | solution.py:84
  294.4 5.5 %collective-permute-start.12 = (f32[168,256]{1,0:T(8,128)S(1)}, f32[168,256]{1,0:T(8,128)S(1)}, u32[]{:S(2)}, u32[]{:S(2)}) collective-permute-start(f32[168,256]{1,0:T(8,128)S(1)} %bitcast_add_fusion.3), channel_id=1, source_target_pairs={{0,128},{128,0},{1,129},{129,1},{2,130},{130,2},{3,131},{131,3},{4... | collective-permute-start | bytes 516104 | tf_op jit(solution)/shard_map/ppermute | solution.py:109
  299.2 14.8 %copy-start.5 = (f32[128,2560]{1,0:T(8,128)S(1)}, f32[128,2560]{1,0:T(8,128)}, u32[]{:S(2)}) copy-start(f32[128,2560]{1,0:T(8,128)} %copy-done.4) | copy-start | bytes 3932164
  299.9 7.0 %collective-permute-start.13 = (f32[168,256]{1,0:T(8,128)S(1)}, f32[168,256]{1,0:T(8,128)S(1)}, u32[]{:S(2)}, u32[]{:S(2)}) collective-permute-start(f32[168,256]{1,0:T(8,128)S(1)} %add.337), channel_id=1, source_target_pairs={{0,16},{16,0},{32,48},{48,32},{64,80},{80,64},{96,112},{112,96},{1... | collective-permute-start | bytes 516104 | tf_op jit(solution)/shard_map/ppermute | solution.py:109
  306.9 6.9 %collective-permute-start.14 = (f32[168,256]{1,0:T(8,128)S(1)}, f32[168,256]{1,0:T(8,128)S(1)}, u32[]{:S(2)}, u32[]{:S(2)}) collective-permute-start(f32[168,256]{1,0:T(8,128)S(1)} %add.338), channel_id=1, source_target_pairs={{0,32},{16,48},{32,0},{48,16},{64,96},{80,112},{96,64},{112,80},{1... | collective-permute-start | bytes 516104 | tf_op jit(solution)/shard_map/ppermute | solution.py:109
  313.9 8.3 %copy-start.1 = (bf16[3088,512]{1,0:T(8,128)(2,1)S(1)}, bf16[3088,512]{1,0:T(8,128)(2,1)}, u32[]{:S(2)}) copy-start(bf16[3088,512]{1,0:T(8,128)(2,1)} %param.30) | copy-start | bytes 9486340
  313.9 7.0 %collective-permute-start.15 = (f32[168,256]{1,0:T(8,128)S(1)}, f32[168,256]{1,0:T(8,128)S(1)}, u32[]{:S(2)}, u32[]{:S(2)}) collective-permute-start(f32[168,256]{1,0:T(8,128)S(1)} %add.339), channel_id=1, source_target_pairs={{0,64},{16,80},{32,96},{48,112},{64,0},{80,16},{96,32},{112,48},{1... | collective-permute-start | bytes 516104 | tf_op jit(solution)/shard_map/ppermute | solution.py:109
  (43 other events, 117.6 us)
Sparse Core Ops, SparseCore 0:
  9.9 141.4 all-gather.2

commit v9 on v7

--- a/solution.py
+++ b/solution.py
@@ -88,12 +88,17 @@
     return buf, ride
 
 
-def doubling_sum(value, axis):
+def doubling_sum(value, axis, wire_type=None):
     size = lax.axis_size(axis)
     bits = size.bit_length() - 1
     assert 1 << bits == size
     for k in range(bits):
-        value = value + lax.ppermute(value, axis, xor_pairs(size, 1 << k))
+        if wire_type is None:
+            value = value + lax.ppermute(value, axis, xor_pairs(size, 1 << k))
+        else:
+            sent = value.astype(wire_type)
+            got = lax.ppermute(sent, axis, xor_pairs(size, 1 << k))
+            value = sent.astype(value.dtype) + got.astype(value.dtype)
     return value
 
 
@@ -251,7 +256,7 @@
             - normed_h * jnp.mean(d_norm * normed_h, axis=-1, keepdims=True)
         )
     ).astype(jnp.bfloat16)
-    block = doubling_sum(doubling_sum(block, "sec"), "dp")
+    block = doubling_sum(doubling_sum(block, "sec", jnp.bfloat16), "dp", jnp.bfloat16)
     grad_w_out = block[:rows_dev]
     group_first = (lax.axis_index("sec") * n_dp + lax.axis_index("dp")) * ways * clips_dev
     all_rewards = block[rows_dev:].reshape(extra * cols)

time: 304 us -> 300 us (0.987)
  waiting for transfers between devices: 177 us -> 171 us
    ppermute x8 -> x4, waiting for transfers between devices: 27.1 us -> 11.7 us  [doubling_sum(): value = value + lax.ppermute(value, axis, xor_pairs(size, 1 << k))]
    ppermute x0 -> x4, waiting for transfers between devices: none -> 9.66 us  [doubling_sum(): got = lax.ppermute(sent, axis, xor_pairs(size, 1 << k))]
    ppermute x0 -> x4, starting transfers between devices: none -> 6.35 us  [doubling_sum(): got = lax.ppermute(sent, axis, xor_pairs(size, 1 << k))]
    ppermute x8 -> x4, starting transfers between devices: 18.7 us -> 13.2 us  [doubling_sum(): value = value + lax.ppermute(value, axis, xor_pairs(size, 1 << k))]
  transfers between devices with their start and end apart: 14 -> 14, of which waited for: 13 -> 12; matrix products, arithmetic and copies ran while one was open for 14% -> 14% of each run, Pallas kernels for 0% -> 0%
where the time goes in v9:
time: 300 us; the launch traced here: 299 us
  waiting for transfers between devices  171 us (57%)
  matrix products  45.8 us (15%)
  starting transfers between devices  25.4 us (8%)
  other arithmetic  21.5 us (7%)
  local copies, waits for them, and re-layouts  18 us (6%)
  between operations  17.2 us (6%)
    all_gather x1, waiting for transfers between devices, local(): w_all = lax.all_gather(w_qkv, 'seq', axis=0)  103 us
    ppermute x4, waiting for transfers between devices, halving_sum(): lax.ppermute(send.astype(wire_types[k]), axis, xor_pairs(size, 1 << k))  27.4 us
    all_gather x1, waiting for transfers between devices, local(): proj_b = lax.all_gather(proj_send, 'seq', axis=0, tiled=True)  18.2 us
    dot_general x1, matrix products, local(): jnp.einsum('cfd,hjdk->cfhjk', emb_b, w_all, preferred_element_type=jnp.fl...  14.6 us
    dot_general x1, matrix products, local(): jnp.einsum('cfhjk,hjdk->cfd', d_proj, w_all, preferred_element_type=jnp.f...  13.7 us
    ppermute x4, starting transfers between devices, doubling_sum(): value = value + lax.ppermute(value, axis, xor_pairs(size, 1 << k))  13.2 us
    ppermute x4, waiting for transfers between devices, doubling_sum(): value = value + lax.ppermute(value, axis, xor_pairs(size, 1 << k))  11.7 us
    ppermute x4, waiting for transfers between devices, doubling_sum(): got = lax.ppermute(sent, axis, xor_pairs(size, 1 << k))  9.66 us
  transfers between devices with their start and end apart: 14, of which 12 were waited for; matrix products, arithmetic and copies ran while one was open for 14% of the time, Pallas kernels for 0%

profile of v9, /device:TPU:6, one launch (start us, length us, event | category | flops | bytes accessed | tf_op | source)
XLA Modules:
  0.0 299.0 jit_solution(15822027975699652155)
XLA Ops:
  9.1 5.1 %gather_fusion = bf16[1024,512]{1,0:T(8,128)(2,1)} fusion(bf16[3088,512]{1,0:T(8,128)(2,1)S(1)} %copy-done, s32[1024]{0:T(1024)S(1)} %broadcast_clamp_fusion), kind=kCustom, calls=%fused_computation | custom fusion | bytes 2101248 | tf_op jit(solution)/shard_map/jit(_take)/gather | solution.py:131
  14.2 1.8 select_reduce_fusion
  20.8 2.0 collective-permute-start.1
  23.3 2.9 collective-permute-done.1
  26.3 3.4 %collective-permute-start.2 = (f32[32,512]{1,0:T(8,128)S(1)}, f32[32,512]{1,0:T(8,128)S(1)}, u32[]{:S(2)}, u32[]{:S(2)}) collective-permute-start(f32[32,512]{1,0:T(8,128)S(1)} %add.244), channel_id=1, source_target_pairs={{0,4},{1,5},{2,6},{3,7},{4,0},{5,1},{6,2},{7,3},{8,12},{9,13},{10,... | collective-permute-start | bytes 196616 | tf_op jit(solution)/shard_map/ppermute | solution.py:97
  29.7 5.2 %collective-permute-done.2 = f32[32,512]{1,0:T(8,128)S(1)} collective-permute-done((f32[32,512]{1,0:T(8,128)S(1)}, f32[32,512]{1,0:T(8,128)S(1)}, u32[]{:S(2)}, u32[]{:S(2)}) %collective-permute-start.2) | collective-permute-done | bytes 65568 | tf_op jit(solution)/shard_map/ppermute | solution.py:97
  34.9 7.6 %collective-permute-start.3 = (f32[32,512]{1,0:T(8,128)S(1)}, f32[32,512]{1,0:T(8,128)S(1)}, u32[]{:S(2)}, u32[]{:S(2)}) collective-permute-start(f32[32,512]{1,0:T(8,128)S(1)} %add.245), channel_id=1, source_target_pairs={{0,8},{1,9},{2,10},{3,11},{4,12},{5,13},{6,14},{7,15},{8,0},{9,1},... | collective-permute-start | bytes 196616 | tf_op jit(solution)/shard_map/ppermute | solution.py:97
  43.5 3.6 %collective-permute-done.3 = f32[32,512]{1,0:T(8,128)S(1)} collective-permute-done((f32[32,512]{1,0:T(8,128)S(1)}, f32[32,512]{1,0:T(8,128)S(1)}, u32[]{:S(2)}, u32[]{:S(2)}) %collective-permute-start.3) | collective-permute-done | bytes 65568 | tf_op jit(solution)/shard_map/ppermute | solution.py:97
  47.1 103.4 %all-gather.6.cloned.1.call-done = bf16[48,2048,128]{2,1,0:T(8,128)(2,1)} async-done(((bf16[3,2048,128]{2,1,0:T(8,128)(2,1)}), bf16[48,2048,128]{2,1,0:T(8,128)(2,1)}) %all-gather.6.cloned.1.call-update) | async-done | bytes 25165840 | tf_op jit(solution)/shard_map/all_gather | solution.py:136
  152.4 14.6 %convolution_bitcast_fusion.1 = f32[1,128,16,3,128]{1,4,3,2,0:T(8,128)S(1)} fusion(bf16[16,3,2048,128]{3,2,1,0:T(8,128)(2,1)} %bitcast.207, bf16[1,128,2048]{2,1,0:T(8,128)(2,1)} %convert_bitcast_fusion), kind=kOutput, calls=%fused_computation.8 | convolution fusion | flops 3221225472 | bytes 28835840 | tf_op jit(solution)/shard_map/cfd,hjdk->cfhjk/dot_general | solution.py:155
  168.5 2.6 convert_reduce_fusion.1
  172.1 2.2 copy.72
  175.3 18.2 %all-gather.4.cloned.1.call-done = bf16[2048,512]{1,0:T(8,128)(2,1)} async-done(((bf16[128,512]{1,0:T(8,128)(2,1)}), bf16[2048,512]{1,0:T(8,128)(2,1)}) %all-gather.4.cloned.1.call-update) | async-done | bytes 2097168 | tf_op jit(solution)/shard_map/all_gather | solution.py:153
  193.5 2.0 fusion.65
  197.5 3.4 %fusion.66 = f32[1,2048]{1,0:T(1,128)S(1)} fusion(f32[512,1]{0,1:T(1,128)S(1)} %bitcast.225, bf16[2048,512]{1,0:T(8,128)(2,1)} %all-gather.4.cloned.1.call-done), kind=kOutput, calls=%fused_computation.159 | convolution fusion | flops 12582912 | bytes 2107392 | tf_op jit(solution)/shard_map/dot_general | solution.py:191
  204.9 1.5 fusion.26
  206.4 13.7 %multiply_reduce_fusion = (f32[128]{0:T(128)S(1)}, f32[128,2048]{1,0:T(8,128)S(1)}) fusion(f32[128,2048]{1,0:T(8,128)} %copy-done.6, f32[128]{0:T(128)S(1)} %add_sqrt_fusion.3, bf16[16,3,2048,128]{3,2,1,0:T(8,128)(2,1)} %bitcast.208, bf16[128,16,1,128]{0,3,1,2:T(8,128)(2,1)} %multiply_convert_fusion, bf16[128,16,1,128]{0,3,1,2:T(8,128)(2,1)} %get-tuple-element.74, ...), kind=kOutput, calls=%fused_computation.47 | convolution fusion | flops 3223584768 | bytes 28836864 | tf_op jit(solution)/shard_map/cfhjk,hjdk->cfd/dot_general | solution.py:219
  222.1 1.9 fusion.55
  224.5 2.5 fusion.67
  232.8 3.1 %collective-permute-done.4 = f32[2,2,2,168,256]{4,3,0,1,2:T(8,128)S(1)} collective-permute-done((f32[2,2,2,168,256]{4,3,0,1,2:T(8,128)}, f32[2,2,2,168,256]{4,3,0,1,2:T(8,128)S(1)}, u32[]{:S(2)}, u32[]{:S(2)}) %collective-permute-start.4) | collective-permute-done | bytes 1376288 | tf_op jit(solution)/shard_map/ppermute | solution.py:84
  237.1 1.5 bitcast_add_fusion
  239.5 9.4 %collective-permute-done.5 = bf16[2,2,168,256]{3,2,0,1:T(8,128)(2,1)S(1)} collective-permute-done((bf16[2,2,168,256]{3,2,0,1:T(8,128)(2,1)S(1)}, bf16[2,2,168,256]{3,2,0,1:T(8,128)(2,1)S(1)}, u32[]{:S(2)}, u32[]{:S(2)}) %collective-permute-start.5) | collective-permute-done | bytes 344096 | tf_op jit(solution)/shard_map/ppermute | solution.py:84
  249.0 1.6 collective-permute-start.6
  250.6 8.8 %collective-permute-done.6 = bf16[2,168,256]{2,1,0:T(8,128)(2,1)S(1)} collective-permute-done((bf16[2,168,256]{2,1,0:T(8,128)(2,1)S(1)}, bf16[2,168,256]{2,1,0:T(8,128)(2,1)S(1)}, u32[]{:S(2)}, u32[]{:S(2)}) %collective-permute-start.6) | collective-permute-done | bytes 172064 | tf_op jit(solution)/shard_map/ppermute | solution.py:84
  259.5 3.1 %collective-permute-start.7 = (bf16[168,256]{1,0:T(8,128)(2,1)S(1)}, bf16[168,256]{1,0:T(8,128)(2,1)S(1)}, u32[]{:S(2)}, u32[]{:S(2)}) collective-permute-start(bf16[168,256]{1,0:T(8,128)(2,1)S(1)} %fusion.35), channel_id=1, source_target_pairs={{0,8},{1,9},{2,10},{3,11},{4,12},{5,13},{6,14},{7,15},{8,0},{9,1},... | collective-permute-start | bytes 258056 | tf_op jit(solution)/shard_map/ppermute | solution.py:84
  262.6 6.1 %collective-permute-done.7 = bf16[168,256]{1,0:T(8,128)(2,1)S(1)} collective-permute-done((bf16[168,256]{1,0:T(8,128)(2,1)S(1)}, bf16[168,256]{1,0:T(8,128)(2,1)S(1)}, u32[]{:S(2)}, u32[]{:S(2)}) %collective-permute-start.7) | collective-permute-done | bytes 86048 | tf_op jit(solution)/shard_map/ppermute | solution.py:84
  270.2 2.0 fusion.12
  273.4 2.9 collective-permute-start.9
  276.4 3.2 %collective-permute-done.9 = bf16[168,256]{1,0:T(8,128)(2,1)S(1)} collective-permute-done((bf16[168,256]{1,0:T(8,128)(2,1)S(1)}, bf16[168,256]{1,0:T(8,128)(2,1)S(1)}, u32[]{:S(2)}, u32[]{:S(2)}) %collective-permute-start.9) | collective-permute-done | bytes 86048 | tf_op jit(solution)/shard_map/ppermute | solution.py:100
  280.5 4.2 %collective-permute-done.10 = bf16[168,256]{1,0:T(8,128)(2,1)S(1)} collective-permute-done((bf16[168,256]{1,0:T(8,128)(2,1)S(1)}, bf16[168,256]{1,0:T(8,128)(2,1)S(1)}, u32[]{:S(2)}, u32[]{:S(2)}) %collective-permute-start.10) | collective-permute-done | bytes 86048 | tf_op jit(solution)/shard_map/ppermute | solution.py:100
  285.7 2.8 fusion.15
  288.6 2.3 collective-permute-done.11
  (140 shorter events, 33.1 us)
Async XLA Ops:
  7.2 1.9 copy-start
  7.2 143.4 %all-gather.6.cloned.1.call-start = ((), (), s32[]{:S(2)}) async-start(), calls=%async_computation.1 | async-start | bytes 26738688 | tf_op jit(solution)/shard_map/all_gather | solution.py:136
  7.9 185.6 %all-gather.4.cloned.1.call-start = ((), (), s32[]{:S(2)}) async-start(), calls=%async_computation | async-start | bytes 2228224 | tf_op jit(solution)/shard_map/all_gather | solution.py:153
  9.1 7.6 %copy-start.17 = (bf16[1,2560]{1,0:T(2,128)(2,1)S(1)}, bf16[1,2560]{1,0:T(2,128)(2,1)}, u32[]{:S(2)}) copy-start(bf16[1,2560]{1,0:T(2,128)(2,1)} %param.21) | copy-start | bytes 15364
  9.1 7.6 %copy-start.18 = (bf16[1,2560]{1,0:T(2,128)(2,1)S(1)}, bf16[1,2560]{1,0:T(2,128)(2,1)}, u32[]{:S(2)}) copy-start(bf16[1,2560]{1,0:T(2,128)(2,1)} %param.22) | copy-start | bytes 15364
  14.1 2.6 copy-start.2
  14.2 3.1 %copy-start.12 = (bf16[2560,256]{1,0:T(8,128)(2,1)S(1)}, bf16[2560,256]{1,0:T(8,128)(2,1)}, u32[]{:S(2)}) copy-start(bf16[2560,256]{1,0:T(8,128)(2,1)} %param.25) | copy-start | bytes 3932164
  14.2 3.1 %copy-start.19 = (bf16[1,128,256]{2,1,0:T(8,128)(2,1)S(1)}, bf16[1,128,256]{2,1,0:T(8,128)(2,1)}, u32[]{:S(2)}) copy-start(bf16[1,128,256]{2,1,0:T(8,128)(2,1)} %param.23) | copy-start | bytes 196612
  15.9 4.9 %collective-permute-start = (f32[32,512]{1,0:T(8,128)S(1)}, f32[32,512]{1,0:T(8,128)S(1)}, u32[]{:S(2)}, u32[]{:S(2)}) collective-permute-start(f32[32,512]{1,0:T(8,128)S(1)} %select_reduce_fusion), channel_id=1, source_target_pairs={{0,1},{1,0},{2,3},{3,2},{4,5},{5,4},{6,7},{7,6},{8,9},{9,8},{10,11... | collective-permute-start | bytes 196616 | tf_op jit(solution)/shard_map/ppermute | solution.py:97
  17.3 2.0 copy-start.15
  18.4 4.4 %copy-start.13 = (bf16[256,2048]{1,0:T(8,128)(2,1)S(1)}, bf16[256,2048]{1,0:T(8,128)(2,1)}, u32[]{:S(2)}) copy-start(bf16[256,2048]{1,0:T(8,128)(2,1)} %param.26) | copy-start | bytes 3145732
  20.8 5.4 %collective-permute-start.1 = (f32[32,512]{1,0:T(8,128)S(1)}, f32[32,512]{1,0:T(8,128)S(1)}, u32[]{:S(2)}, u32[]{:S(2)}) collective-permute-start(f32[32,512]{1,0:T(8,128)S(1)} %add.243), channel_id=1, source_target_pairs={{0,2},{1,3},{2,0},{3,1},{4,6},{5,7},{6,4},{7,5},{8,10},{9,11},{10,... | collective-permute-start | bytes 196616 | tf_op jit(solution)/shard_map/ppermute | solution.py:97
  23.3 129.1 %copy-start.6 = (f32[128,2048]{1,0:T(8,128)}, f32[128,2048]{1,0:T(8,128)S(1)}, u32[]{:S(2)}) copy-start(f32[128,2048]{1,0:T(8,128)S(1)} %get-tuple-element.88) | copy-start | bytes 3145732
  23.3 127.3 %copy-start.20 = (s32[16]{0:T(128)S(1)}, s32[16]{0:T(128)}, u32[]{:S(2)}) copy-start(s32[16]{0:T(128)} %param.32) | copy-start | bytes 196
  23.3 127.9 %copy-start.21 = (f32[16]{0:T(128)S(1)}, f32[16]{0:T(128)}, u32[]{:S(2)}) copy-start(f32[16]{0:T(128)} %param.33) | copy-start | bytes 196
  26.3 8.6 %collective-permute-start.2 = (f32[32,512]{1,0:T(8,128)S(1)}, f32[32,512]{1,0:T(8,128)S(1)}, u32[]{:S(2)}, u32[]{:S(2)}) collective-permute-start(f32[32,512]{1,0:T(8,128)S(1)} %add.244), channel_id=1, source_target_pairs={{0,4},{1,5},{2,6},{3,7},{4,0},{5,1},{6,2},{7,3},{8,12},{9,13},{10,... | collective-permute-start | bytes 196616 | tf_op jit(solution)/shard_map/ppermute | solution.py:97
  34.9 12.2 %collective-permute-start.3 = (f32[32,512]{1,0:T(8,128)S(1)}, f32[32,512]{1,0:T(8,128)S(1)}, u32[]{:S(2)}, u32[]{:S(2)}) collective-permute-start(f32[32,512]{1,0:T(8,128)S(1)} %add.245), channel_id=1, source_target_pairs={{0,8},{1,9},{2,10},{3,11},{4,12},{5,13},{6,14},{7,15},{8,0},{9,1},... | collective-permute-start | bytes 196616 | tf_op jit(solution)/shard_map/ppermute | solution.py:97
  197.4 3.9 %copy-start.8 = (f32[16,128,128]{1,2,0:T(8,128)S(1)}, f32[16,128,128]{1,2,0:T(8,128)}, u32[]{:S(2)}) copy-start(f32[16,128,128]{1,2,0:T(8,128)} %get-tuple-element.90) | copy-start | bytes 3145732
  206.4 13.7 %copy-start.7 = (f32[128,2048]{1,0:T(8,128)S(1)}, f32[128,2048]{1,0:T(8,128)}, u32[]{:S(2)}) copy-start(f32[128,2048]{1,0:T(8,128)} %copy-done.6) | copy-start | bytes 3145732
  224.5 4.7 %copy-start.9 = (bf16[1,2560,128]{2,1,0:T(8,128)(2,1)S(1)}, bf16[1,2560,128]{2,1,0:T(8,128)(2,1)}, u32[]{:S(2)}) copy-start(bf16[1,2560,128]{2,1,0:T(8,128)(2,1)} %copy.72) | copy-start | bytes 1966084
  231.4 5.7 %copy-start.5 = (f32[2,2,2,1,168,256]{5,4,3,2,1,0:T(8,128)S(1)}, f32[2,2,2,1,168,256]{5,4,3,2,1,0:T(8,128)}, u32[]{:S(2)}) copy-start(f32[2,2,2,1,168,256]{5,4,3,2,1,0:T(8,128)} %get-tuple-element.77) | copy-start | bytes 4128772
  232.6 3.3 %collective-permute-start.4 = (f32[2,2,2,168,256]{4,3,0,1,2:T(8,128)}, f32[2,2,2,168,256]{4,3,0,1,2:T(8,128)S(1)}, u32[]{:S(2)}, u32[]{:S(2)}) collective-permute-start(f32[2,2,2,168,256]{4,3,0,1,2:T(8,128)} %bitcast.205), channel_id=1, source_target_pairs={{0,1},{1,0},{2,3},{3,2},{4,5},{5,4},{6,7},{7,6},{8,9},{9,8},{10,11... | collective-permute-start | bytes 4128776 | tf_op jit(solution)/shard_map/ppermute | solution.py:84
  235.9 1.1 copy-start.11
  238.6 10.3 %collective-permute-start.5 = (bf16[2,2,168,256]{3,2,0,1:T(8,128)(2,1)S(1)}, bf16[2,2,168,256]{3,2,0,1:T(8,128)(2,1)S(1)}, u32[]{:S(2)}, u32[]{:S(2)}) collective-permute-start(bf16[2,2,168,256]{3,2,0,1:T(8,128)(2,1)S(1)} %fusion.28), channel_id=1, source_target_pairs={{0,2},{1,3},{2,0},{3,1},{4,6},{5,7},{6,4},{7,5},{8,10},{9,11},{10,... | collective-permute-start | bytes 1032200 | tf_op jit(solution)/shard_map/ppermute | solution.py:84
  239.5 30.7 %copy-start.3 = (bf16[1,128,2560]{2,1,0:T(8,128)(2,1)S(1)}, bf16[1,128,2560]{2,1,0:T(8,128)(2,1)}, u32[]{:S(2)}) copy-start(bf16[1,128,2560]{2,1,0:T(8,128)(2,1)} %param.20) | copy-start | bytes 1966084
  249.0 10.4 %collective-permute-start.6 = (bf16[2,168,256]{2,1,0:T(8,128)(2,1)S(1)}, bf16[2,168,256]{2,1,0:T(8,128)(2,1)S(1)}, u32[]{:S(2)}, u32[]{:S(2)}) collective-permute-start(bf16[2,168,256]{2,1,0:T(8,128)(2,1)S(1)} %fusion.33), channel_id=1, source_target_pairs={{0,4},{1,5},{2,6},{3,7},{4,0},{5,1},{6,2},{7,3},{8,12},{9,13},{10,... | collective-permute-start | bytes 516104 | tf_op jit(solution)/shard_map/ppermute | solution.py:84
  259.5 9.2 %collective-permute-start.7 = (bf16[168,256]{1,0:T(8,128)(2,1)S(1)}, bf16[168,256]{1,0:T(8,128)(2,1)S(1)}, u32[]{:S(2)}, u32[]{:S(2)}) collective-permute-start(bf16[168,256]{1,0:T(8,128)(2,1)S(1)} %fusion.35), channel_id=1, source_target_pairs={{0,8},{1,9},{2,10},{3,11},{4,12},{5,13},{6,14},{7,15},{8,0},{9,1},... | collective-permute-start | bytes 258056 | tf_op jit(solution)/shard_map/ppermute | solution.py:84
  268.7 4.7 %collective-permute-start.8 = (bf16[168,256]{1,0:T(8,128)(2,1)S(1)}, bf16[168,256]{1,0:T(8,128)(2,1)S(1)}, u32[]{:S(2)}, u32[]{:S(2)}) collective-permute-start(bf16[168,256]{1,0:T(8,128)(2,1)S(1)} %fusion.34), channel_id=1, source_target_pairs={{0,128},{128,0},{1,129},{129,1},{2,130},{130,2},{3,131},{131,3},{4... | collective-permute-start | bytes 258056 | tf_op jit(solution)/shard_map/ppermute | solution.py:100
  273.4 6.1 %collective-permute-start.9 = (bf16[168,256]{1,0:T(8,128)(2,1)S(1)}, bf16[168,256]{1,0:T(8,128)(2,1)S(1)}, u32[]{:S(2)}, u32[]{:S(2)}) collective-permute-start(bf16[168,256]{1,0:T(8,128)(2,1)S(1)} %add_convert_fusion.2), channel_id=1, source_target_pairs={{0,16},{16,0},{32,48},{48,32},{64,80},{80,64},{96,112},{112,96},{1... | collective-permute-start | bytes 258056 | tf_op jit(solution)/shard_map/ppermute | solution.py:100
  279.6 5.2 %collective-permute-start.10 = (bf16[168,256]{1,0:T(8,128)(2,1)S(1)}, bf16[168,256]{1,0:T(8,128)(2,1)S(1)}, u32[]{:S(2)}, u32[]{:S(2)}) collective-permute-start(bf16[168,256]{1,0:T(8,128)(2,1)S(1)} %add_convert_fusion.1), channel_id=1, source_target_pairs={{0,32},{16,48},{32,0},{48,16},{64,96},{80,112},{96,64},{112,80},{1... | collective-permute-start | bytes 258056 | tf_op jit(solution)/shard_map/ppermute | solution.py:100
  284.8 7.4 %copy-start.1 = (bf16[3088,512]{1,0:T(8,128)(2,1)S(1)}, bf16[3088,512]{1,0:T(8,128)(2,1)}, u32[]{:S(2)}) copy-start(bf16[3088,512]{1,0:T(8,128)(2,1)} %param.30) | copy-start | bytes 9486340
  284.8 6.1 %collective-permute-start.11 = (bf16[168,256]{1,0:T(8,128)(2,1)S(1)}, bf16[168,256]{1,0:T(8,128)(2,1)S(1)}, u32[]{:S(2)}, u32[]{:S(2)}) collective-permute-start(bf16[168,256]{1,0:T(8,128)(2,1)S(1)} %add_convert_fusion), channel_id=1, source_target_pairs={{0,64},{16,80},{32,96},{48,112},{64,0},{80,16},{96,32},{112,48},{1... | collective-permute-start | bytes 258056 | tf_op jit(solution)/shard_map/ppermute | solution.py:100
  (4 other events, 4.0 us)
Sparse Core Ops, SparseCore 0:
  9.9 140.6 all-gather.5
  152.4 41.0 all-gather.3

commit v10 on v9

--- a/solution.py
+++ b/solution.py
@@ -46,13 +46,23 @@
     return (vectors / length, length)
 
 
+def bf16_parts(values):
+    high = lax.reduce_precision(values, exponent_bits=8, mantissa_bits=7)
+    rest = values - high
+    middle = lax.reduce_precision(rest, exponent_bits=8, mantissa_bits=7)
+    return jnp.stack([high, middle, rest - middle]).astype(jnp.bfloat16)
+
+
 def norm_grad(grad, normed, scale_rms):
     return (grad - normed * jnp.mean(grad * normed, axis=-1, keepdims=True)) / scale_rms
 
 
-def motion_grad(d_emb, normed_e, scale_rms, motion, theta, embed_rows, root_rows):
+def motion_grad(d_emb, normed_e, scale_rms, motion, theta, w_embed, root_rows):
     d_unemb = norm_grad(d_emb, normed_e, scale_rms)
-    d_embedded = jnp.einsum("cfd,ed->cfe", d_unemb, embed_rows, precision=highest)
+    d_embedded = jnp.sum(
+        jnp.einsum("pcfd,ed->pcfe", bf16_parts(d_unemb), w_embed, preferred_element_type=jnp.float32),
+        axis=0,
+    )
     grad_east = suffix(jnp.sum(d_unemb * root_rows[0], axis=-1))
     grad_north = suffix(jnp.sum(d_unemb * root_rows[1], axis=-1))
     vel_east = motion[..., 1]
@@ -123,7 +133,6 @@
     me = lax.axis_index("seq")
     head_size = D_REW // HEADS
     root_rows = w_root.astype(jnp.float32)
-    embed_rows = w_embed.astype(jnp.float32)
 
     vocab_rows = text_table.shape[0]
     local_ids = text_ids - me * vocab_rows
@@ -151,7 +160,6 @@
     )
     text_unit, text_len = unit_rows(text_raw)
     proj_b = lax.all_gather(proj_send, "seq", axis=0, tiled=True)
-    proj_rows = proj_b.astype(jnp.float32)
     projected = jnp.einsum(
         "cfd,hjdk->cfhjk",
         emb_b,
@@ -188,9 +196,10 @@
         * (target - rewards[:, None] * motion_emb / emb_len[:, None])
         / emb_len[:, None]
     )
-    d_pooled = jnp.dot(d_memb, proj_rows.T, precision=highest).reshape(
-        clips_dev, HEADS, head_size
-    )
+    d_pooled = jnp.sum(
+        jnp.einsum("pcn,rn->pcr", bf16_parts(d_memb), proj_b, preferred_element_type=jnp.float32),
+        axis=0,
+    ).reshape(clips_dev, HEADS, head_size)
     reduction_dimension = jnp.einsum("chd,cghd->chg", d_pooled, value_f, precision=highest)
     d_value = jnp.transpose(column_mass, (0, 2, 1))[..., None] * d_pooled[:, None]
     pairwise_dot_similarity = jnp.sum(
@@ -217,7 +226,7 @@
     d_key = (d_ku - key_unit * jnp.sum(key_unit * d_ku, axis=-1, keepdims=True)) / key_len
     d_proj = jnp.stack([d_query, d_key, d_value], axis=3).astype(jnp.bfloat16)
     d_emb = jnp.einsum("cfhjk,hjdk->cfd", d_proj, w_all, preferred_element_type=jnp.float32)
-    d_motion = motion_grad(d_emb, normed_e, scale_rms, x_clean, theta, embed_rows, root_rows)
+    d_motion = motion_grad(d_emb, normed_e, scale_rms, x_clean, theta, w_embed, root_rows)
     d_eps_b = (-level * d_motion).astype(jnp.bfloat16)
     grad_term = jnp.einsum(
         "cdf,cfe->de", modulated_t, d_eps_b, preferred_element_type=jnp.float32

time: 300 us -> 298 us (level)
  no operation moved by 1% of the time
where the time goes in v10:
time: 298 us; the launch traced here: 297 us
  waiting for transfers between devices  170 us (57%)
  matrix products  44.2 us (15%)
  starting transfers between devices  25.3 us (8%)
  other arithmetic  21.8 us (7%)
  local copies, waits for them, and re-layouts  18.9 us (6%)
  between operations  17.3 us (6%)
    all_gather x1, waiting for transfers between devices, local(): w_all = lax.all_gather(w_qkv, 'seq', axis=0)  103 us
    ppermute x4, waiting for transfers between devices, halving_sum(): lax.ppermute(send.astype(wire_types[k]), axis, xor_pairs(size, 1 << k))  27.4 us
    all_gather x1, waiting for transfers between devices, local(): proj_b = lax.all_gather(proj_send, 'seq', axis=0, tiled=True)  18.2 us
    dot_general x1, matrix products, local(): jnp.einsum('cfd,hjdk->cfhjk', emb_b, w_all, preferred_element_type=jnp.fl...  14.6 us
    dot_general x1, matrix products, local(): jnp.einsum('cfhjk,hjdk->cfd', d_proj, w_all, preferred_element_type=jnp.f...  13.7 us
    ppermute x4, starting transfers between devices, doubling_sum(): value = value + lax.ppermute(value, axis, xor_pairs(size, 1 << k))  13.2 us
    ppermute x4, waiting for transfers between devices, doubling_sum(): value = value + lax.ppermute(value, axis, xor_pairs(size, 1 << k))  10.5 us
    ppermute x4, waiting for transfers between devices, doubling_sum(): got = lax.ppermute(sent, axis, xor_pairs(size, 1 << k))  9.76 us
  transfers between devices with their start and end apart: 14, of which 12 were waited for; matrix products, arithmetic and copies ran while one was open for 14% of the time, Pallas kernels for 0%

profile of v10, /device:TPU:6, one launch (start us, length us, event | category | flops | bytes accessed | tf_op | source)
XLA Modules:
  0.0 297.5 jit_solution(17791797564916144020)
XLA Ops:
  9.1 5.1 %gather_fusion = bf16[1024,512]{1,0:T(8,128)(2,1)} fusion(bf16[3088,512]{1,0:T(8,128)(2,1)S(1)} %copy-done, s32[1024]{0:T(1024)S(1)} %broadcast_clamp_fusion), kind=kCustom, calls=%fused_computation | custom fusion | bytes 2101248 | tf_op jit(solution)/shard_map/jit(_take)/gather | solution.py:140
  14.2 1.8 select_reduce_fusion
  20.8 2.0 collective-permute-start.1
  22.8 1.7 multiply_reduce_fusion.4
  24.5 1.7 collective-permute-done.1
  26.3 3.4 %collective-permute-start.2 = (f32[32,512]{1,0:T(8,128)S(1)}, f32[32,512]{1,0:T(8,128)S(1)}, u32[]{:S(2)}, u32[]{:S(2)}) collective-permute-start(f32[32,512]{1,0:T(8,128)S(1)} %add.242), channel_id=1, source_target_pairs={{0,4},{1,5},{2,6},{3,7},{4,0},{5,1},{6,2},{7,3},{8,12},{9,13},{10,... | collective-permute-start | bytes 196616 | tf_op jit(solution)/shard_map/ppermute | solution.py:107
  29.7 5.2 %collective-permute-done.2 = f32[32,512]{1,0:T(8,128)S(1)} collective-permute-done((f32[32,512]{1,0:T(8,128)S(1)}, f32[32,512]{1,0:T(8,128)S(1)}, u32[]{:S(2)}, u32[]{:S(2)}) %collective-permute-start.2) | collective-permute-done | bytes 65568 | tf_op jit(solution)/shard_map/ppermute | solution.py:107
  34.9 7.6 %collective-permute-start.3 = (f32[32,512]{1,0:T(8,128)S(1)}, f32[32,512]{1,0:T(8,128)S(1)}, u32[]{:S(2)}, u32[]{:S(2)}) collective-permute-start(f32[32,512]{1,0:T(8,128)S(1)} %add.243), channel_id=1, source_target_pairs={{0,8},{1,9},{2,10},{3,11},{4,12},{5,13},{6,14},{7,15},{8,0},{9,1},... | collective-permute-start | bytes 196616 | tf_op jit(solution)/shard_map/ppermute | solution.py:107
  43.5 3.6 %collective-permute-done.3 = f32[32,512]{1,0:T(8,128)S(1)} collective-permute-done((f32[32,512]{1,0:T(8,128)S(1)}, f32[32,512]{1,0:T(8,128)S(1)}, u32[]{:S(2)}, u32[]{:S(2)}) %collective-permute-start.3) | collective-permute-done | bytes 65568 | tf_op jit(solution)/shard_map/ppermute | solution.py:107
  47.1 103.4 %all-gather.6.cloned.1.call-done = bf16[48,2048,128]{2,1,0:T(8,128)(2,1)} async-done(((bf16[3,2048,128]{2,1,0:T(8,128)(2,1)}), bf16[48,2048,128]{2,1,0:T(8,128)(2,1)}) %all-gather.6.cloned.1.call-update) | async-done | bytes 25165840 | tf_op jit(solution)/shard_map/all_gather | solution.py:145
  152.4 14.6 %convolution_bitcast_fusion.1 = f32[1,128,16,3,128]{1,4,3,2,0:T(8,128)S(1)} fusion(bf16[16,3,2048,128]{3,2,1,0:T(8,128)(2,1)} %bitcast.209, bf16[1,128,2048]{2,1,0:T(8,128)(2,1)} %convert_bitcast_fusion), kind=kOutput, calls=%fused_computation.8 | convolution fusion | flops 3221225472 | bytes 28835840 | tf_op jit(solution)/shard_map/cfd,hjdk->cfhjk/dot_general | solution.py:163
  168.5 2.6 convert_reduce_fusion.1
  172.1 2.2 copy.72
  175.3 18.2 %all-gather.4.cloned.1.call-done = bf16[2048,512]{1,0:T(8,128)(2,1)} async-done(((bf16[128,512]{1,0:T(8,128)(2,1)}), bf16[2048,512]{1,0:T(8,128)(2,1)}) %all-gather.4.cloned.1.call-update) | async-done | bytes 2097168 | tf_op jit(solution)/shard_map/all_gather | solution.py:162
  193.5 2.0 fusion.86
  197.5 2.3 convolution_reduce_fusion
  203.9 1.5 fusion.40
  205.4 13.7 %multiply_reduce_fusion = (f32[128]{0:T(128)S(1)}, f32[128,2048]{1,0:T(8,128)S(1)}) fusion(f32[128,2048]{1,0:T(8,128)} %copy-done.6, f32[128]{0:T(128)S(1)} %add_sqrt_fusion.3, bf16[16,3,2048,128]{3,2,1,0:T(8,128)(2,1)} %bitcast.210, bf16[128,16,1,128]{0,3,1,2:T(8,128)(2,1)} %multiply_convert_fusion, bf16[128,16,1,128]{0,3,1,2:T(8,128)(2,1)} %get-tuple-element.76, ...), kind=kOutput, calls=%fused_computation.61 | convolution fusion | flops 3223584768 | bytes 28836864 | tf_op jit(solution)/shard_map/cfhjk,hjdk->cfd/dot_general | solution.py:228
  221.1 1.9 fusion.74
  231.3 3.1 %collective-permute-done.4 = f32[2,2,2,168,256]{4,3,0,1,2:T(8,128)S(1)} collective-permute-done((f32[2,2,2,168,256]{4,3,0,1,2:T(8,128)}, f32[2,2,2,168,256]{4,3,0,1,2:T(8,128)S(1)}, u32[]{:S(2)}, u32[]{:S(2)}) %collective-permute-start.4) | collective-permute-done | bytes 1376288 | tf_op jit(solution)/shard_map/ppermute | solution.py:94
  238.0 9.4 %collective-permute-done.5 = bf16[2,2,168,256]{3,2,0,1:T(8,128)(2,1)S(1)} collective-permute-done((bf16[2,2,168,256]{3,2,0,1:T(8,128)(2,1)S(1)}, bf16[2,2,168,256]{3,2,0,1:T(8,128)(2,1)S(1)}, u32[]{:S(2)}, u32[]{:S(2)}) %collective-permute-start.5) | collective-permute-done | bytes 344096 | tf_op jit(solution)/shard_map/ppermute | solution.py:94
  247.5 1.6 collective-permute-start.6
  249.1 8.8 %collective-permute-done.6 = bf16[2,168,256]{2,1,0:T(8,128)(2,1)S(1)} collective-permute-done((bf16[2,168,256]{2,1,0:T(8,128)(2,1)S(1)}, bf16[2,168,256]{2,1,0:T(8,128)(2,1)S(1)}, u32[]{:S(2)}, u32[]{:S(2)}) %collective-permute-start.6) | collective-permute-done | bytes 172064 | tf_op jit(solution)/shard_map/ppermute | solution.py:94
  258.0 3.1 %collective-permute-start.7 = (bf16[168,256]{1,0:T(8,128)(2,1)S(1)}, bf16[168,256]{1,0:T(8,128)(2,1)S(1)}, u32[]{:S(2)}, u32[]{:S(2)}) collective-permute-start(bf16[168,256]{1,0:T(8,128)(2,1)S(1)} %fusion.49), channel_id=1, source_target_pairs={{0,8},{1,9},{2,10},{3,11},{4,12},{5,13},{6,14},{7,15},{8,0},{9,1},... | collective-permute-start | bytes 258056 | tf_op jit(solution)/shard_map/ppermute | solution.py:94
  261.0 6.1 %collective-permute-done.7 = bf16[168,256]{1,0:T(8,128)(2,1)S(1)} collective-permute-done((bf16[168,256]{1,0:T(8,128)(2,1)S(1)}, bf16[168,256]{1,0:T(8,128)(2,1)S(1)}, u32[]{:S(2)}, u32[]{:S(2)}) %collective-permute-start.7) | collective-permute-done | bytes 86048 | tf_op jit(solution)/shard_map/ppermute | solution.py:94
  267.2 1.6 collective-permute-start.8
  268.8 2.0 fusion.18
  272.0 2.8 collective-permute-start.9
  274.8 3.2 %collective-permute-done.9 = bf16[168,256]{1,0:T(8,128)(2,1)S(1)} collective-permute-done((bf16[168,256]{1,0:T(8,128)(2,1)S(1)}, bf16[168,256]{1,0:T(8,128)(2,1)S(1)}, u32[]{:S(2)}, u32[]{:S(2)}) %collective-permute-start.9) | collective-permute-done | bytes 86048 | tf_op jit(solution)/shard_map/ppermute | solution.py:110
  279.0 4.2 %collective-permute-done.10 = bf16[168,256]{1,0:T(8,128)(2,1)S(1)} collective-permute-done((bf16[168,256]{1,0:T(8,128)(2,1)S(1)}, bf16[168,256]{1,0:T(8,128)(2,1)S(1)}, u32[]{:S(2)}, u32[]{:S(2)}) %collective-permute-start.10) | collective-permute-done | bytes 86048 | tf_op jit(solution)/shard_map/ppermute | solution.py:110
  284.2 2.8 fusion.21
  287.0 2.3 collective-permute-done.11
  (145 shorter events, 34.5 us)
Async XLA Ops:
  7.2 1.9 copy-start
  7.2 143.4 %all-gather.6.cloned.1.call-start = ((), (), s32[]{:S(2)}) async-start(), calls=%async_computation.1 | async-start | bytes 26738688 | tf_op jit(solution)/shard_map/all_gather | solution.py:145
  7.9 185.6 %all-gather.4.cloned.1.call-start = ((), (), s32[]{:S(2)}) async-start(), calls=%async_computation | async-start | bytes 2228224 | tf_op jit(solution)/shard_map/all_gather | solution.py:162
  9.1 7.6 %copy-start.16 = (bf16[1,2560]{1,0:T(2,128)(2,1)S(1)}, bf16[1,2560]{1,0:T(2,128)(2,1)}, u32[]{:S(2)}) copy-start(bf16[1,2560]{1,0:T(2,128)(2,1)} %param.21) | copy-start | bytes 15364
  9.1 7.6 %copy-start.17 = (bf16[1,2560]{1,0:T(2,128)(2,1)S(1)}, bf16[1,2560]{1,0:T(2,128)(2,1)}, u32[]{:S(2)}) copy-start(bf16[1,2560]{1,0:T(2,128)(2,1)} %param.22) | copy-start | bytes 15364
  14.1 2.6 copy-start.2
  14.2 3.1 %copy-start.12 = (bf16[2560,256]{1,0:T(8,128)(2,1)S(1)}, bf16[2560,256]{1,0:T(8,128)(2,1)}, u32[]{:S(2)}) copy-start(bf16[2560,256]{1,0:T(8,128)(2,1)} %param.25) | copy-start | bytes 3932164
  14.2 3.1 %copy-start.19 = (bf16[1,128,256]{2,1,0:T(8,128)(2,1)S(1)}, bf16[1,128,256]{2,1,0:T(8,128)(2,1)}, u32[]{:S(2)}) copy-start(bf16[1,128,256]{2,1,0:T(8,128)(2,1)} %param.23) | copy-start | bytes 196612
  15.9 4.9 %collective-permute-start = (f32[32,512]{1,0:T(8,128)S(1)}, f32[32,512]{1,0:T(8,128)S(1)}, u32[]{:S(2)}, u32[]{:S(2)}) collective-permute-start(f32[32,512]{1,0:T(8,128)S(1)} %select_reduce_fusion), channel_id=1, source_target_pairs={{0,1},{1,0},{2,3},{3,2},{4,5},{5,4},{6,7},{7,6},{8,9},{9,8},{10,11... | collective-permute-start | bytes 196616 | tf_op jit(solution)/shard_map/ppermute | solution.py:107
  17.3 2.0 copy-start.14
  20.8 5.4 %collective-permute-start.1 = (f32[32,512]{1,0:T(8,128)S(1)}, f32[32,512]{1,0:T(8,128)S(1)}, u32[]{:S(2)}, u32[]{:S(2)}) collective-permute-start(f32[32,512]{1,0:T(8,128)S(1)} %add.241), channel_id=1, source_target_pairs={{0,2},{1,3},{2,0},{3,1},{4,6},{5,7},{6,4},{7,5},{8,10},{9,11},{10,... | collective-permute-start | bytes 196616 | tf_op jit(solution)/shard_map/ppermute | solution.py:107
  24.5 127.9 %copy-start.6 = (f32[128,2048]{1,0:T(8,128)}, f32[128,2048]{1,0:T(8,128)S(1)}, u32[]{:S(2)}) copy-start(f32[128,2048]{1,0:T(8,128)S(1)} %get-tuple-element.95) | copy-start | bytes 3145732
  24.5 126.1 %copy-start.20 = (s32[16]{0:T(128)S(1)}, s32[16]{0:T(128)}, u32[]{:S(2)}) copy-start(s32[16]{0:T(128)} %param.32) | copy-start | bytes 196
  24.5 126.6 %copy-start.21 = (f32[16]{0:T(128)S(1)}, f32[16]{0:T(128)}, u32[]{:S(2)}) copy-start(f32[16]{0:T(128)} %param.33) | copy-start | bytes 196
  26.3 8.6 %collective-permute-start.2 = (f32[32,512]{1,0:T(8,128)S(1)}, f32[32,512]{1,0:T(8,128)S(1)}, u32[]{:S(2)}, u32[]{:S(2)}) collective-permute-start(f32[32,512]{1,0:T(8,128)S(1)} %add.242), channel_id=1, source_target_pairs={{0,4},{1,5},{2,6},{3,7},{4,0},{5,1},{6,2},{7,3},{8,12},{9,13},{10,... | collective-permute-start | bytes 196616 | tf_op jit(solution)/shard_map/ppermute | solution.py:107
  34.9 12.2 %collective-permute-start.3 = (f32[32,512]{1,0:T(8,128)S(1)}, f32[32,512]{1,0:T(8,128)S(1)}, u32[]{:S(2)}, u32[]{:S(2)}) collective-permute-start(f32[32,512]{1,0:T(8,128)S(1)} %add.243), channel_id=1, source_target_pairs={{0,8},{1,9},{2,10},{3,11},{4,12},{5,13},{6,14},{7,15},{8,0},{9,1},... | collective-permute-start | bytes 196616 | tf_op jit(solution)/shard_map/ppermute | solution.py:107
  197.5 2.9 copy-start.8
  205.4 13.7 %copy-start.7 = (f32[128,2048]{1,0:T(8,128)S(1)}, f32[128,2048]{1,0:T(8,128)}, u32[]{:S(2)}) copy-start(f32[128,2048]{1,0:T(8,128)} %copy-done.6) | copy-start | bytes 3145732
  223.4 1.2 copy-start.18
  225.3 2.3 copy-start.9
  229.8 5.7 %copy-start.5 = (f32[2,2,2,1,168,256]{5,4,3,2,1,0:T(8,128)S(1)}, f32[2,2,2,1,168,256]{5,4,3,2,1,0:T(8,128)}, u32[]{:S(2)}) copy-start(f32[2,2,2,1,168,256]{5,4,3,2,1,0:T(8,128)} %get-tuple-element.79) | copy-start | bytes 4128772
  231.0 3.3 %collective-permute-start.4 = (f32[2,2,2,168,256]{4,3,0,1,2:T(8,128)}, f32[2,2,2,168,256]{4,3,0,1,2:T(8,128)S(1)}, u32[]{:S(2)}, u32[]{:S(2)}) collective-permute-start(f32[2,2,2,168,256]{4,3,0,1,2:T(8,128)} %bitcast.207), channel_id=1, source_target_pairs={{0,1},{1,0},{2,3},{3,2},{4,5},{5,4},{6,7},{7,6},{8,9},{9,8},{10,11... | collective-permute-start | bytes 4128776 | tf_op jit(solution)/shard_map/ppermute | solution.py:94
  234.4 1.1 copy-start.11
  237.1 10.3 %collective-permute-start.5 = (bf16[2,2,168,256]{3,2,0,1:T(8,128)(2,1)S(1)}, bf16[2,2,168,256]{3,2,0,1:T(8,128)(2,1)S(1)}, u32[]{:S(2)}, u32[]{:S(2)}) collective-permute-start(bf16[2,2,168,256]{3,2,0,1:T(8,128)(2,1)S(1)} %fusion.42), channel_id=1, source_target_pairs={{0,2},{1,3},{2,0},{3,1},{4,6},{5,7},{6,4},{7,5},{8,10},{9,11},{10,... | collective-permute-start | bytes 1032200 | tf_op jit(solution)/shard_map/ppermute | solution.py:94
  238.0 30.8 %copy-start.3 = (bf16[1,128,2560]{2,1,0:T(8,128)(2,1)S(1)}, bf16[1,128,2560]{2,1,0:T(8,128)(2,1)}, u32[]{:S(2)}) copy-start(bf16[1,128,2560]{2,1,0:T(8,128)(2,1)} %param.20) | copy-start | bytes 1966084
  247.5 10.4 %collective-permute-start.6 = (bf16[2,168,256]{2,1,0:T(8,128)(2,1)S(1)}, bf16[2,168,256]{2,1,0:T(8,128)(2,1)S(1)}, u32[]{:S(2)}, u32[]{:S(2)}) collective-permute-start(bf16[2,168,256]{2,1,0:T(8,128)(2,1)S(1)} %fusion.47), channel_id=1, source_target_pairs={{0,4},{1,5},{2,6},{3,7},{4,0},{5,1},{6,2},{7,3},{8,12},{9,13},{10,... | collective-permute-start | bytes 516104 | tf_op jit(solution)/shard_map/ppermute | solution.py:94
  258.0 9.2 %collective-permute-start.7 = (bf16[168,256]{1,0:T(8,128)(2,1)S(1)}, bf16[168,256]{1,0:T(8,128)(2,1)S(1)}, u32[]{:S(2)}, u32[]{:S(2)}) collective-permute-start(bf16[168,256]{1,0:T(8,128)(2,1)S(1)} %fusion.49), channel_id=1, source_target_pairs={{0,8},{1,9},{2,10},{3,11},{4,12},{5,13},{6,14},{7,15},{8,0},{9,1},... | collective-permute-start | bytes 258056 | tf_op jit(solution)/shard_map/ppermute | solution.py:94
  267.2 4.8 %collective-permute-start.8 = (bf16[168,256]{1,0:T(8,128)(2,1)S(1)}, bf16[168,256]{1,0:T(8,128)(2,1)S(1)}, u32[]{:S(2)}, u32[]{:S(2)}) collective-permute-start(bf16[168,256]{1,0:T(8,128)(2,1)S(1)} %fusion.48), channel_id=1, source_target_pairs={{0,128},{128,0},{1,129},{129,1},{2,130},{130,2},{3,131},{131,3},{4... | collective-permute-start | bytes 258056 | tf_op jit(solution)/shard_map/ppermute | solution.py:110
  272.0 6.1 %collective-permute-start.9 = (bf16[168,256]{1,0:T(8,128)(2,1)S(1)}, bf16[168,256]{1,0:T(8,128)(2,1)S(1)}, u32[]{:S(2)}, u32[]{:S(2)}) collective-permute-start(bf16[168,256]{1,0:T(8,128)(2,1)S(1)} %add_convert_fusion.2), channel_id=1, source_target_pairs={{0,16},{16,0},{32,48},{48,32},{64,80},{80,64},{96,112},{112,96},{1... | collective-permute-start | bytes 258056 | tf_op jit(solution)/shard_map/ppermute | solution.py:110
  278.1 5.1 %collective-permute-start.10 = (bf16[168,256]{1,0:T(8,128)(2,1)S(1)}, bf16[168,256]{1,0:T(8,128)(2,1)S(1)}, u32[]{:S(2)}, u32[]{:S(2)}) collective-permute-start(bf16[168,256]{1,0:T(8,128)(2,1)S(1)} %add_convert_fusion.1), channel_id=1, source_target_pairs={{0,32},{16,48},{32,0},{48,16},{64,96},{80,112},{96,64},{112,80},{1... | collective-permute-start | bytes 258056 | tf_op jit(solution)/shard_map/ppermute | solution.py:110
  283.2 7.4 %copy-start.1 = (bf16[3088,512]{1,0:T(8,128)(2,1)S(1)}, bf16[3088,512]{1,0:T(8,128)(2,1)}, u32[]{:S(2)}) copy-start(bf16[3088,512]{1,0:T(8,128)(2,1)} %param.30) | copy-start | bytes 9486340
  283.2 6.1 %collective-permute-start.11 = (bf16[168,256]{1,0:T(8,128)(2,1)S(1)}, bf16[168,256]{1,0:T(8,128)(2,1)S(1)}, u32[]{:S(2)}, u32[]{:S(2)}) collective-permute-start(bf16[168,256]{1,0:T(8,128)(2,1)S(1)} %add_convert_fusion), channel_id=1, source_target_pairs={{0,64},{16,80},{32,96},{48,112},{64,0},{80,16},{96,32},{112,48},{1... | collective-permute-start | bytes 258056 | tf_op jit(solution)/shard_map/ppermute | solution.py:110
  (4 other events, 4.0 us)
Sparse Core Ops, SparseCore 0:
  9.9 140.6 all-gather.5
  152.4 41.0 all-gather.3

commit v11 on v10

--- a/solution.py
+++ b/solution.py
@@ -252,9 +252,7 @@
         axis=1,
     )
     seq_bits = ways.bit_length() - 1
-    block, d_eps_b = halving_sum(
-        stacked, "seq", [jnp.float32] + [jnp.bfloat16] * (seq_bits - 1), ride=d_eps_b
-    )
+    block, d_eps_b = halving_sum(stacked, "seq", [jnp.bfloat16] * seq_bits, ride=d_eps_b)
     d_mod = jnp.einsum("cfe,de->cfd", d_eps_b, w_out, preferred_element_type=jnp.float32)
     d_norm = d_mod * gain
     grad_hidden = (

time: 298 us -> 296 us (level)
  no operation moved by 1% of the time
where the time goes in v11:
time: 296 us; the launch traced here: 295 us
  waiting for transfers between devices  169 us (57%)
  matrix products  45.3 us (15%)
  starting transfers between devices  25.5 us (9%)
  other arithmetic  21.7 us (7%)
  between operations  17.2 us (6%)
  local copies, waits for them, and re-layouts  16.8 us (6%)
    all_gather x1, waiting for transfers between devices, local(): w_all = lax.all_gather(w_qkv, 'seq', axis=0)  103 us
    ppermute x4, waiting for transfers between devices, halving_sum(): lax.ppermute(send.astype(wire_types[k]), axis, xor_pairs(size, 1 << k))  26.2 us
    all_gather x1, waiting for transfers between devices, local(): proj_b = lax.all_gather(proj_send, 'seq', axis=0, tiled=True)  18.2 us
    dot_general x1, matrix products, local(): jnp.einsum('cfd,hjdk->cfhjk', emb_b, w_all, preferred_element_type=jnp.fl...  14.6 us
    dot_general x1, matrix products, local(): jnp.einsum('cfhjk,hjdk->cfd', d_proj, w_all, preferred_element_type=jnp.f...  13.7 us
    ppermute x4, starting transfers between devices, doubling_sum(): value = value + lax.ppermute(value, axis, xor_pairs(size, 1 << k))  13.2 us
    ppermute x4, waiting for transfers between devices, doubling_sum(): value = value + lax.ppermute(value, axis, xor_pairs(size, 1 << k))  10.5 us
    ppermute x4, waiting for transfers between devices, doubling_sum(): got = lax.ppermute(sent, axis, xor_pairs(size, 1 << k))  9.72 us
  transfers between devices with their start and end apart: 14, of which 12 were waited for; matrix products, arithmetic and copies ran while one was open for 14% of the time, Pallas kernels for 0%

profile of v11, /device:TPU:6, one launch (start us, length us, event | category | flops | bytes accessed | tf_op | source)
XLA Modules:
  0.0 295.2 jit_solution(3737927194466495248)
XLA Ops:
  9.1 5.1 %gather_fusion = bf16[1024,512]{1,0:T(8,128)(2,1)} fusion(bf16[3088,512]{1,0:T(8,128)(2,1)S(1)} %copy-done, s32[1024]{0:T(1024)S(1)} %broadcast_clamp_fusion), kind=kCustom, calls=%fused_computation | custom fusion | bytes 2101248 | tf_op jit(solution)/shard_map/jit(_take)/gather | solution.py:140
  14.2 1.8 select_reduce_fusion
  20.8 2.0 collective-permute-start.1
  22.8 1.7 multiply_reduce_fusion.4
  24.5 1.7 collective-permute-done.1
  26.3 3.4 %collective-permute-start.2 = (f32[32,512]{1,0:T(8,128)S(1)}, f32[32,512]{1,0:T(8,128)S(1)}, u32[]{:S(2)}, u32[]{:S(2)}) collective-permute-start(f32[32,512]{1,0:T(8,128)S(1)} %add.242), channel_id=1, source_target_pairs={{0,4},{1,5},{2,6},{3,7},{4,0},{5,1},{6,2},{7,3},{8,12},{9,13},{10,... | collective-permute-start | bytes 196616 | tf_op jit(solution)/shard_map/ppermute | solution.py:107
  29.7 5.2 %collective-permute-done.2 = f32[32,512]{1,0:T(8,128)S(1)} collective-permute-done((f32[32,512]{1,0:T(8,128)S(1)}, f32[32,512]{1,0:T(8,128)S(1)}, u32[]{:S(2)}, u32[]{:S(2)}) %collective-permute-start.2) | collective-permute-done | bytes 65568 | tf_op jit(solution)/shard_map/ppermute | solution.py:107
  34.9 7.6 %collective-permute-start.3 = (f32[32,512]{1,0:T(8,128)S(1)}, f32[32,512]{1,0:T(8,128)S(1)}, u32[]{:S(2)}, u32[]{:S(2)}) collective-permute-start(f32[32,512]{1,0:T(8,128)S(1)} %add.243), channel_id=1, source_target_pairs={{0,8},{1,9},{2,10},{3,11},{4,12},{5,13},{6,14},{7,15},{8,0},{9,1},... | collective-permute-start | bytes 196616 | tf_op jit(solution)/shard_map/ppermute | solution.py:107
  43.5 3.6 %collective-permute-done.3 = f32[32,512]{1,0:T(8,128)S(1)} collective-permute-done((f32[32,512]{1,0:T(8,128)S(1)}, f32[32,512]{1,0:T(8,128)S(1)}, u32[]{:S(2)}, u32[]{:S(2)}) %collective-permute-start.3) | collective-permute-done | bytes 65568 | tf_op jit(solution)/shard_map/ppermute | solution.py:107
  47.1 103.4 %all-gather.6.cloned.1.call-done = bf16[48,2048,128]{2,1,0:T(8,128)(2,1)} async-done(((bf16[3,2048,128]{2,1,0:T(8,128)(2,1)}), bf16[48,2048,128]{2,1,0:T(8,128)(2,1)}) %all-gather.6.cloned.1.call-update) | async-done | bytes 25165840 | tf_op jit(solution)/shard_map/all_gather | solution.py:145
  152.4 14.6 %convolution_bitcast_fusion.1 = f32[1,128,16,3,128]{1,4,3,2,0:T(8,128)S(1)} fusion(bf16[16,3,2048,128]{3,2,1,0:T(8,128)(2,1)} %bitcast.208, bf16[1,128,2048]{2,1,0:T(8,128)(2,1)} %convert_bitcast_fusion), kind=kOutput, calls=%fused_computation.8 | convolution fusion | flops 3221225472 | bytes 28835840 | tf_op jit(solution)/shard_map/cfd,hjdk->cfhjk/dot_general | solution.py:163
  168.5 2.6 convert_reduce_fusion.1
  172.1 2.2 copy.72
  175.3 18.2 %all-gather.4.cloned.1.call-done = bf16[2048,512]{1,0:T(8,128)(2,1)} async-done(((bf16[128,512]{1,0:T(8,128)(2,1)}), bf16[2048,512]{1,0:T(8,128)(2,1)}) %all-gather.4.cloned.1.call-update) | async-done | bytes 2097168 | tf_op jit(solution)/shard_map/all_gather | solution.py:162
  193.5 2.0 fusion.87
  197.5 2.3 convolution_reduce_fusion
  205.4 13.7 %multiply_reduce_fusion = (f32[128]{0:T(128)S(1)}, f32[128,2048]{1,0:T(8,128)S(1)}) fusion(f32[128,2048]{1,0:T(8,128)} %copy-done.6, f32[128]{0:T(128)S(1)} %add_sqrt_fusion.3, bf16[16,3,2048,128]{3,2,1,0:T(8,128)(2,1)} %bitcast.209, bf16[128,16,1,128]{0,3,1,2:T(8,128)(2,1)} %multiply_convert_fusion, bf16[128,16,1,128]{0,3,1,2:T(8,128)(2,1)} %get-tuple-element.76, ...), kind=kOutput, calls=%fused_computation.61 | convolution fusion | flops 3223584768 | bytes 28836864 | tf_op jit(solution)/shard_map/cfhjk,hjdk->cfd/dot_general | solution.py:228
  221.1 1.9 fusion.75
  227.6 1.6 fusion.53
  231.4 1.9 collective-permute-done.4
  235.7 9.4 %collective-permute-done.5 = bf16[2,2,168,256]{3,2,0,1:T(8,128)(2,1)S(1)} collective-permute-done((bf16[2,2,168,256]{3,2,0,1:T(8,128)(2,1)S(1)}, bf16[2,2,168,256]{3,2,0,1:T(8,128)(2,1)S(1)}, u32[]{:S(2)}, u32[]{:S(2)}) %collective-permute-start.5) | collective-permute-done | bytes 344096 | tf_op jit(solution)/shard_map/ppermute | solution.py:94
  245.3 1.6 collective-permute-start.6
  246.9 8.8 %collective-permute-done.6 = bf16[2,168,256]{2,1,0:T(8,128)(2,1)S(1)} collective-permute-done((bf16[2,168,256]{2,1,0:T(8,128)(2,1)S(1)}, bf16[2,168,256]{2,1,0:T(8,128)(2,1)S(1)}, u32[]{:S(2)}, u32[]{:S(2)}) %collective-permute-start.6) | collective-permute-done | bytes 172064 | tf_op jit(solution)/shard_map/ppermute | solution.py:94
  255.7 3.1 %collective-permute-start.7 = (bf16[168,256]{1,0:T(8,128)(2,1)S(1)}, bf16[168,256]{1,0:T(8,128)(2,1)S(1)}, u32[]{:S(2)}, u32[]{:S(2)}) collective-permute-start(bf16[168,256]{1,0:T(8,128)(2,1)S(1)} %fusion.50), channel_id=1, source_target_pairs={{0,8},{1,9},{2,10},{3,11},{4,12},{5,13},{6,14},{7,15},{8,0},{9,1},... | collective-permute-start | bytes 258056 | tf_op jit(solution)/shard_map/ppermute | solution.py:94
  258.8 6.1 %collective-permute-done.7 = bf16[168,256]{1,0:T(8,128)(2,1)S(1)} collective-permute-done((bf16[168,256]{1,0:T(8,128)(2,1)S(1)}, bf16[168,256]{1,0:T(8,128)(2,1)S(1)}, u32[]{:S(2)}, u32[]{:S(2)}) %collective-permute-start.7) | collective-permute-done | bytes 86048 | tf_op jit(solution)/shard_map/ppermute | solution.py:94
  264.9 1.6 collective-permute-start.8
  266.5 2.0 fusion.18
  269.7 2.9 collective-permute-start.9
  272.6 3.2 %collective-permute-done.9 = bf16[168,256]{1,0:T(8,128)(2,1)S(1)} collective-permute-done((bf16[168,256]{1,0:T(8,128)(2,1)S(1)}, bf16[168,256]{1,0:T(8,128)(2,1)S(1)}, u32[]{:S(2)}, u32[]{:S(2)}) %collective-permute-start.9) | collective-permute-done | bytes 86048 | tf_op jit(solution)/shard_map/ppermute | solution.py:110
  276.7 4.3 %collective-permute-done.10 = bf16[168,256]{1,0:T(8,128)(2,1)S(1)} collective-permute-done((bf16[168,256]{1,0:T(8,128)(2,1)S(1)}, bf16[168,256]{1,0:T(8,128)(2,1)S(1)}, u32[]{:S(2)}, u32[]{:S(2)}) %collective-permute-start.10) | collective-permute-done | bytes 86048 | tf_op jit(solution)/shard_map/ppermute | solution.py:110
  282.0 2.8 fusion.21
  284.8 2.3 collective-permute-done.11
  (140 shorter events, 33.4 us)
Async XLA Ops:
  7.2 1.9 copy-start
  7.2 143.4 %all-gather.6.cloned.1.call-start = ((), (), s32[]{:S(2)}) async-start(), calls=%async_computation.1 | async-start | bytes 26738688 | tf_op jit(solution)/shard_map/all_gather | solution.py:145
  7.9 185.6 %all-gather.4.cloned.1.call-start = ((), (), s32[]{:S(2)}) async-start(), calls=%async_computation | async-start | bytes 2228224 | tf_op jit(solution)/shard_map/all_gather | solution.py:162
  9.1 7.6 %copy-start.14 = (bf16[1,2560]{1,0:T(2,128)(2,1)S(1)}, bf16[1,2560]{1,0:T(2,128)(2,1)}, u32[]{:S(2)}) copy-start(bf16[1,2560]{1,0:T(2,128)(2,1)} %param.21) | copy-start | bytes 15364
  9.1 7.6 %copy-start.15 = (bf16[1,2560]{1,0:T(2,128)(2,1)S(1)}, bf16[1,2560]{1,0:T(2,128)(2,1)}, u32[]{:S(2)}) copy-start(bf16[1,2560]{1,0:T(2,128)(2,1)} %param.22) | copy-start | bytes 15364
  14.1 2.6 copy-start.2
  14.2 3.1 %copy-start.10 = (bf16[2560,256]{1,0:T(8,128)(2,1)S(1)}, bf16[2560,256]{1,0:T(8,128)(2,1)}, u32[]{:S(2)}) copy-start(bf16[2560,256]{1,0:T(8,128)(2,1)} %param.25) | copy-start | bytes 3932164
  14.2 3.1 %copy-start.17 = (bf16[1,128,256]{2,1,0:T(8,128)(2,1)S(1)}, bf16[1,128,256]{2,1,0:T(8,128)(2,1)}, u32[]{:S(2)}) copy-start(bf16[1,128,256]{2,1,0:T(8,128)(2,1)} %param.23) | copy-start | bytes 196612
  15.9 4.9 %collective-permute-start = (f32[32,512]{1,0:T(8,128)S(1)}, f32[32,512]{1,0:T(8,128)S(1)}, u32[]{:S(2)}, u32[]{:S(2)}) collective-permute-start(f32[32,512]{1,0:T(8,128)S(1)} %select_reduce_fusion), channel_id=1, source_target_pairs={{0,1},{1,0},{2,3},{3,2},{4,5},{5,4},{6,7},{7,6},{8,9},{9,8},{10,11... | collective-permute-start | bytes 196616 | tf_op jit(solution)/shard_map/ppermute | solution.py:107
  17.3 2.0 copy-start.12
  20.8 5.4 %collective-permute-start.1 = (f32[32,512]{1,0:T(8,128)S(1)}, f32[32,512]{1,0:T(8,128)S(1)}, u32[]{:S(2)}, u32[]{:S(2)}) collective-permute-start(f32[32,512]{1,0:T(8,128)S(1)} %add.241), channel_id=1, source_target_pairs={{0,2},{1,3},{2,0},{3,1},{4,6},{5,7},{6,4},{7,5},{8,10},{9,11},{10,... | collective-permute-start | bytes 196616 | tf_op jit(solution)/shard_map/ppermute | solution.py:107
  24.5 127.9 %copy-start.6 = (f32[128,2048]{1,0:T(8,128)}, f32[128,2048]{1,0:T(8,128)S(1)}, u32[]{:S(2)}) copy-start(f32[128,2048]{1,0:T(8,128)S(1)} %get-tuple-element.93) | copy-start | bytes 3145732
  24.5 126.1 %copy-start.18 = (s32[16]{0:T(128)S(1)}, s32[16]{0:T(128)}, u32[]{:S(2)}) copy-start(s32[16]{0:T(128)} %param.32) | copy-start | bytes 196
  24.5 126.6 %copy-start.19 = (f32[16]{0:T(128)S(1)}, f32[16]{0:T(128)}, u32[]{:S(2)}) copy-start(f32[16]{0:T(128)} %param.33) | copy-start | bytes 196
  26.3 8.6 %collective-permute-start.2 = (f32[32,512]{1,0:T(8,128)S(1)}, f32[32,512]{1,0:T(8,128)S(1)}, u32[]{:S(2)}, u32[]{:S(2)}) collective-permute-start(f32[32,512]{1,0:T(8,128)S(1)} %add.242), channel_id=1, source_target_pairs={{0,4},{1,5},{2,6},{3,7},{4,0},{5,1},{6,2},{7,3},{8,12},{9,13},{10,... | collective-permute-start | bytes 196616 | tf_op jit(solution)/shard_map/ppermute | solution.py:107
  34.9 12.2 %collective-permute-start.3 = (f32[32,512]{1,0:T(8,128)S(1)}, f32[32,512]{1,0:T(8,128)S(1)}, u32[]{:S(2)}, u32[]{:S(2)}) collective-permute-start(f32[32,512]{1,0:T(8,128)S(1)} %add.243), channel_id=1, source_target_pairs={{0,8},{1,9},{2,10},{3,11},{4,12},{5,13},{6,14},{7,15},{8,0},{9,1},... | collective-permute-start | bytes 196616 | tf_op jit(solution)/shard_map/ppermute | solution.py:107
  197.5 2.9 copy-start.8
  199.8 1.0 copy-start.9
  205.4 13.7 %copy-start.7 = (f32[128,2048]{1,0:T(8,128)S(1)}, f32[128,2048]{1,0:T(8,128)}, u32[]{:S(2)}) copy-start(f32[128,2048]{1,0:T(8,128)} %copy-done.6) | copy-start | bytes 3145732
  223.4 1.2 copy-start.16
  229.4 1.6 copy-start.5
  231.1 2.2 collective-permute-start.4
  234.8 10.3 %collective-permute-start.5 = (bf16[2,2,168,256]{3,2,0,1:T(8,128)(2,1)S(1)}, bf16[2,2,168,256]{3,2,0,1:T(8,128)(2,1)S(1)}, u32[]{:S(2)}, u32[]{:S(2)}) collective-permute-start(bf16[2,2,168,256]{3,2,0,1:T(8,128)(2,1)S(1)} %fusion.43), channel_id=1, source_target_pairs={{0,2},{1,3},{2,0},{3,1},{4,6},{5,7},{6,4},{7,5},{8,10},{9,11},{10,... | collective-permute-start | bytes 1032200 | tf_op jit(solution)/shard_map/ppermute | solution.py:94
  235.7 30.7 %copy-start.3 = (bf16[1,128,2560]{2,1,0:T(8,128)(2,1)S(1)}, bf16[1,128,2560]{2,1,0:T(8,128)(2,1)}, u32[]{:S(2)}) copy-start(bf16[1,128,2560]{2,1,0:T(8,128)(2,1)} %param.20) | copy-start | bytes 1966084
  245.3 10.4 %collective-permute-start.6 = (bf16[2,168,256]{2,1,0:T(8,128)(2,1)S(1)}, bf16[2,168,256]{2,1,0:T(8,128)(2,1)S(1)}, u32[]{:S(2)}, u32[]{:S(2)}) collective-permute-start(bf16[2,168,256]{2,1,0:T(8,128)(2,1)S(1)} %fusion.48), channel_id=1, source_target_pairs={{0,4},{1,5},{2,6},{3,7},{4,0},{5,1},{6,2},{7,3},{8,12},{9,13},{10,... | collective-permute-start | bytes 516104 | tf_op jit(solution)/shard_map/ppermute | solution.py:94
  255.7 9.2 %collective-permute-start.7 = (bf16[168,256]{1,0:T(8,128)(2,1)S(1)}, bf16[168,256]{1,0:T(8,128)(2,1)S(1)}, u32[]{:S(2)}, u32[]{:S(2)}) collective-permute-start(bf16[168,256]{1,0:T(8,128)(2,1)S(1)} %fusion.50), channel_id=1, source_target_pairs={{0,8},{1,9},{2,10},{3,11},{4,12},{5,13},{6,14},{7,15},{8,0},{9,1},... | collective-permute-start | bytes 258056 | tf_op jit(solution)/shard_map/ppermute | solution.py:94
  264.9 4.8 %collective-permute-start.8 = (bf16[168,256]{1,0:T(8,128)(2,1)S(1)}, bf16[168,256]{1,0:T(8,128)(2,1)S(1)}, u32[]{:S(2)}, u32[]{:S(2)}) collective-permute-start(bf16[168,256]{1,0:T(8,128)(2,1)S(1)} %fusion.49), channel_id=1, source_target_pairs={{0,128},{128,0},{1,129},{129,1},{2,130},{130,2},{3,131},{131,3},{4... | collective-permute-start | bytes 258056 | tf_op jit(solution)/shard_map/ppermute | solution.py:110
  268.5 1.1 copy-start.4
  269.7 6.1 %collective-permute-start.9 = (bf16[168,256]{1,0:T(8,128)(2,1)S(1)}, bf16[168,256]{1,0:T(8,128)(2,1)S(1)}, u32[]{:S(2)}, u32[]{:S(2)}) collective-permute-start(bf16[168,256]{1,0:T(8,128)(2,1)S(1)} %add_convert_fusion.2), channel_id=1, source_target_pairs={{0,16},{16,0},{32,48},{48,32},{64,80},{80,64},{96,112},{112,96},{1... | collective-permute-start | bytes 258056 | tf_op jit(solution)/shard_map/ppermute | solution.py:110
  275.8 5.2 %collective-permute-start.10 = (bf16[168,256]{1,0:T(8,128)(2,1)S(1)}, bf16[168,256]{1,0:T(8,128)(2,1)S(1)}, u32[]{:S(2)}, u32[]{:S(2)}) collective-permute-start(bf16[168,256]{1,0:T(8,128)(2,1)S(1)} %add_convert_fusion.1), channel_id=1, source_target_pairs={{0,32},{16,48},{32,0},{48,16},{64,96},{80,112},{96,64},{112,80},{1... | collective-permute-start | bytes 258056 | tf_op jit(solution)/shard_map/ppermute | solution.py:110
  281.0 7.4 %copy-start.1 = (bf16[3088,512]{1,0:T(8,128)(2,1)S(1)}, bf16[3088,512]{1,0:T(8,128)(2,1)}, u32[]{:S(2)}) copy-start(bf16[3088,512]{1,0:T(8,128)(2,1)} %param.30) | copy-start | bytes 9486340
  281.0 6.1 %collective-permute-start.11 = (bf16[168,256]{1,0:T(8,128)(2,1)S(1)}, bf16[168,256]{1,0:T(8,128)(2,1)S(1)}, u32[]{:S(2)}, u32[]{:S(2)}) collective-permute-start(bf16[168,256]{1,0:T(8,128)(2,1)S(1)} %add_convert_fusion), channel_id=1, source_target_pairs={{0,64},{16,80},{32,96},{48,112},{64,0},{80,16},{96,32},{112,48},{1... | collective-permute-start | bytes 258056 | tf_op jit(solution)/shard_map/ppermute | solution.py:110
  (2 other events, 1.9 us)
Sparse Core Ops, SparseCore 0:
  9.9 140.6 all-gather.5
  152.4 41.0 all-gather.3

commit v12 on v11

--- a/solution.py
+++ b/solution.py
@@ -182,7 +182,12 @@
     attention_b = focus_probabilities.astype(jnp.bfloat16)
     column_mass = jnp.sum(attention_b, axis=2, dtype=jnp.float32)
     value_f = value_b.astype(jnp.float32)
-    pooled = jnp.einsum("chg,cghd->chd", column_mass, value_f, precision=highest)
+    pooled = jnp.sum(
+        jnp.einsum(
+            "pchg,cghd->pchd", bf16_parts(column_mass), value_b, preferred_element_type=jnp.float32
+        ),
+        axis=0,
+    )
     pooled_b = pooled.astype(jnp.bfloat16).reshape(clips_dev, D_REW)
     motion_emb = jnp.dot(pooled_b, proj_b, preferred_element_type=jnp.float32)
     prompts = lax.dynamic_slice_in_dim(prompt_index, me * clips_dev, clips_dev)
@@ -200,7 +205,12 @@
         jnp.einsum("pcn,rn->pcr", bf16_parts(d_memb), proj_b, preferred_element_type=jnp.float32),
         axis=0,
     ).reshape(clips_dev, HEADS, head_size)
-    reduction_dimension = jnp.einsum("chd,cghd->chg", d_pooled, value_f, precision=highest)
+    reduction_dimension = jnp.sum(
+        jnp.einsum(
+            "pchd,cghd->pchg", bf16_parts(d_pooled), value_b, preferred_element_type=jnp.float32
+        ),
+        axis=0,
+    )
     d_value = jnp.transpose(column_mass, (0, 2, 1))[..., None] * d_pooled[:, None]
     pairwise_dot_similarity = jnp.sum(
         focus_probabilities * reduction_dimension[:, :, None, :], axis=-1, keepdims=True

time: 296 us -> 296 us (level)
  no operation moved by 1% of the time
where the time goes in v12:
time: 296 us; the launch traced here: 295 us
  waiting for transfers between devices  169 us (57%)
  matrix products  44.7 us (15%)
  starting transfers between devices  25.2 us (9%)
  other arithmetic  21.7 us (7%)
  between operations  17.3 us (6%)
  local copies, waits for them, and re-layouts  17.1 us (6%)
    all_gather x1, waiting for transfers between devices, local(): w_all = lax.all_gather(w_qkv, 'seq', axis=0)  104 us
    ppermute x4, waiting for transfers between devices, halving_sum(): lax.ppermute(send.astype(wire_types[k]), axis, xor_pairs(size, 1 << k))  26.3 us
    all_gather x1, waiting for transfers between devices, local(): proj_b = lax.all_gather(proj_send, 'seq', axis=0, tiled=True)  18.5 us
    dot_general x1, matrix products, local(): jnp.einsum('cfd,hjdk->cfhjk', emb_b, w_all, preferred_element_type=jnp.fl...  14.8 us
    dot_general x1, matrix products, local(): jnp.einsum('cfhjk,hjdk->cfd', d_proj, w_all, preferred_element_type=jnp.f...  13.8 us
    ppermute x4, starting transfers between devices, doubling_sum(): value = value + lax.ppermute(value, axis, xor_pairs(size, 1 << k))  13 us
    ppermute x4, waiting for transfers between devices, doubling_sum(): value = value + lax.ppermute(value, axis, xor_pairs(size, 1 << k))  10.5 us
    ppermute x4, waiting for transfers between devices, doubling_sum(): got = lax.ppermute(sent, axis, xor_pairs(size, 1 << k))  9.75 us
  transfers between devices with their start and end apart: 14, of which 12 were waited for; matrix products, arithmetic and copies ran while one was open for 14% of the time, Pallas kernels for 0%

profile of v12, /device:TPU:6, one launch (start us, length us, event | category | flops | bytes accessed | tf_op | source)
XLA Modules:
  0.0 295.4 jit_solution(5299318626511463626)
XLA Ops:
  9.1 5.1 %gather_fusion = bf16[1024,512]{1,0:T(8,128)(2,1)} fusion(bf16[3088,512]{1,0:T(8,128)(2,1)S(1)} %copy-done, s32[1024]{0:T(1024)S(1)} %broadcast_clamp_fusion), kind=kCustom, calls=%fused_computation | custom fusion | bytes 2101248 | tf_op jit(solution)/shard_map/jit(_take)/gather | solution.py:140
  14.2 1.8 select_reduce_fusion
  20.8 2.0 collective-permute-start.1
  22.8 1.7 multiply_reduce_fusion.4
  24.5 1.7 collective-permute-done.1
  26.3 3.4 %collective-permute-start.2 = (f32[32,512]{1,0:T(8,128)S(1)}, f32[32,512]{1,0:T(8,128)S(1)}, u32[]{:S(2)}, u32[]{:S(2)}) collective-permute-start(f32[32,512]{1,0:T(8,128)S(1)} %add.242), channel_id=1, source_target_pairs={{0,4},{1,5},{2,6},{3,7},{4,0},{5,1},{6,2},{7,3},{8,12},{9,13},{10,... | collective-permute-start | bytes 196616 | tf_op jit(solution)/shard_map/ppermute | solution.py:107
  29.7 5.2 %collective-permute-done.2 = f32[32,512]{1,0:T(8,128)S(1)} collective-permute-done((f32[32,512]{1,0:T(8,128)S(1)}, f32[32,512]{1,0:T(8,128)S(1)}, u32[]{:S(2)}, u32[]{:S(2)}) %collective-permute-start.2) | collective-permute-done | bytes 65568 | tf_op jit(solution)/shard_map/ppermute | solution.py:107
  34.9 7.5 %collective-permute-start.3 = (f32[32,512]{1,0:T(8,128)S(1)}, f32[32,512]{1,0:T(8,128)S(1)}, u32[]{:S(2)}, u32[]{:S(2)}) collective-permute-start(f32[32,512]{1,0:T(8,128)S(1)} %add.243), channel_id=1, source_target_pairs={{0,8},{1,9},{2,10},{3,11},{4,12},{5,13},{6,14},{7,15},{8,0},{9,1},... | collective-permute-start | bytes 196616 | tf_op jit(solution)/shard_map/ppermute | solution.py:107
  43.3 3.6 %collective-permute-done.3 = f32[32,512]{1,0:T(8,128)S(1)} collective-permute-done((f32[32,512]{1,0:T(8,128)S(1)}, f32[32,512]{1,0:T(8,128)S(1)}, u32[]{:S(2)}, u32[]{:S(2)}) %collective-permute-start.3) | collective-permute-done | bytes 65568 | tf_op jit(solution)/shard_map/ppermute | solution.py:107
  46.9 103.6 %all-gather.6.cloned.1.call-done = bf16[48,2048,128]{2,1,0:T(8,128)(2,1)} async-done(((bf16[3,2048,128]{2,1,0:T(8,128)(2,1)}), bf16[48,2048,128]{2,1,0:T(8,128)(2,1)}) %all-gather.6.cloned.1.call-update) | async-done | bytes 25165840 | tf_op jit(solution)/shard_map/all_gather | solution.py:145
  152.4 14.8 %convolution_bitcast_fusion.1 = f32[1,128,16,3,128]{1,4,3,2,0:T(8,128)S(1)} fusion(bf16[16,3,2048,128]{3,2,1,0:T(8,128)(2,1)} %bitcast.209, bf16[1,128,2048]{2,1,0:T(8,128)(2,1)} %convert_bitcast_fusion), kind=kOutput, calls=%fused_computation.8 | convolution fusion | flops 3221225472 | bytes 28835840 | tf_op jit(solution)/shard_map/cfd,hjdk->cfhjk/dot_general | solution.py:163
  168.7 2.6 convert_reduce_fusion.1
  171.8 2.2 copy.98
  175.0 18.5 %all-gather.4.cloned.1.call-done = bf16[2048,512]{1,0:T(8,128)(2,1)} async-done(((bf16[128,512]{1,0:T(8,128)(2,1)}), bf16[2048,512]{1,0:T(8,128)(2,1)}) %all-gather.4.cloned.1.call-update) | async-done | bytes 2097168 | tf_op jit(solution)/shard_map/all_gather | solution.py:162
  193.5 2.0 fusion.89
  197.5 2.3 convolution_reduce_fusion
  205.4 13.8 %multiply_reduce_fusion = (f32[128]{0:T(128)S(1)}, f32[128,2048]{1,0:T(8,128)S(1)}) fusion(f32[128,2048]{1,0:T(8,128)} %copy-done.6, f32[128]{0:T(128)S(1)} %add_sqrt_fusion.3, bf16[16,3,2048,128]{3,2,1,0:T(8,128)(2,1)} %bitcast.210, bf16[128,16,1,128]{0,3,1,2:T(8,128)(2,1)} %multiply_convert_fusion, bf16[128,16,1,128]{0,3,1,2:T(8,128)(2,1)} %get-tuple-element.76, ...), kind=kOutput, calls=%fused_computation.63 | convolution fusion | flops 3223584768 | bytes 28836864 | tf_op jit(solution)/shard_map/cfhjk,hjdk->cfd/dot_general | solution.py:238
  221.2 1.9 fusion.77
  227.7 1.6 fusion.51
  231.5 1.9 collective-permute-done.4
  235.8 9.4 %collective-permute-done.5 = bf16[2,2,168,256]{3,2,0,1:T(8,128)(2,1)S(1)} collective-permute-done((bf16[2,2,168,256]{3,2,0,1:T(8,128)(2,1)S(1)}, bf16[2,2,168,256]{3,2,0,1:T(8,128)(2,1)S(1)}, u32[]{:S(2)}, u32[]{:S(2)}) %collective-permute-start.5) | collective-permute-done | bytes 344096 | tf_op jit(solution)/shard_map/ppermute | solution.py:94
  245.4 1.6 collective-permute-start.6
  247.0 8.8 %collective-permute-done.6 = bf16[2,168,256]{2,1,0:T(8,128)(2,1)S(1)} collective-permute-done((bf16[2,168,256]{2,1,0:T(8,128)(2,1)S(1)}, bf16[2,168,256]{2,1,0:T(8,128)(2,1)S(1)}, u32[]{:S(2)}, u32[]{:S(2)}) %collective-permute-start.6) | collective-permute-done | bytes 172064 | tf_op jit(solution)/shard_map/ppermute | solution.py:94
  255.8 3.0 %collective-permute-start.7 = (bf16[168,256]{1,0:T(8,128)(2,1)S(1)}, bf16[168,256]{1,0:T(8,128)(2,1)S(1)}, u32[]{:S(2)}, u32[]{:S(2)}) collective-permute-start(bf16[168,256]{1,0:T(8,128)(2,1)S(1)} %fusion.48), channel_id=1, source_target_pairs={{0,8},{1,9},{2,10},{3,11},{4,12},{5,13},{6,14},{7,15},{8,0},{9,1},... | collective-permute-start | bytes 258056 | tf_op jit(solution)/shard_map/ppermute | solution.py:94
  258.8 6.2 %collective-permute-done.7 = bf16[168,256]{1,0:T(8,128)(2,1)S(1)} collective-permute-done((bf16[168,256]{1,0:T(8,128)(2,1)S(1)}, bf16[168,256]{1,0:T(8,128)(2,1)S(1)}, u32[]{:S(2)}, u32[]{:S(2)}) %collective-permute-start.7) | collective-permute-done | bytes 86048 | tf_op jit(solution)/shard_map/ppermute | solution.py:94
  265.0 1.6 collective-permute-start.8
  266.6 2.0 fusion.18
  269.8 2.9 collective-permute-start.9
  272.7 3.2 %collective-permute-done.9 = bf16[168,256]{1,0:T(8,128)(2,1)S(1)} collective-permute-done((bf16[168,256]{1,0:T(8,128)(2,1)S(1)}, bf16[168,256]{1,0:T(8,128)(2,1)S(1)}, u32[]{:S(2)}, u32[]{:S(2)}) %collective-permute-start.9) | collective-permute-done | bytes 86048 | tf_op jit(solution)/shard_map/ppermute | solution.py:110
  276.9 4.3 %collective-permute-done.10 = bf16[168,256]{1,0:T(8,128)(2,1)S(1)} collective-permute-done((bf16[168,256]{1,0:T(8,128)(2,1)S(1)}, bf16[168,256]{1,0:T(8,128)(2,1)S(1)}, u32[]{:S(2)}, u32[]{:S(2)}) %collective-permute-start.10) | collective-permute-done | bytes 86048 | tf_op jit(solution)/shard_map/ppermute | solution.py:110
  282.1 2.9 fusion.21
  284.9 2.3 collective-permute-done.11
  (143 shorter events, 32.8 us)
Async XLA Ops:
  7.2 1.9 copy-start
  7.2 143.4 %all-gather.6.cloned.1.call-start = ((), (), s32[]{:S(2)}) async-start(), calls=%async_computation.1 | async-start | bytes 26738688 | tf_op jit(solution)/shard_map/all_gather | solution.py:145
  7.9 185.6 %all-gather.4.cloned.1.call-start = ((), (), s32[]{:S(2)}) async-start(), calls=%async_computation | async-start | bytes 2228224 | tf_op jit(solution)/shard_map/all_gather | solution.py:162
  9.1 7.6 %copy-start.14 = (bf16[1,2560]{1,0:T(2,128)(2,1)S(1)}, bf16[1,2560]{1,0:T(2,128)(2,1)}, u32[]{:S(2)}) copy-start(bf16[1,2560]{1,0:T(2,128)(2,1)} %param.21) | copy-start | bytes 15364
  9.1 7.6 %copy-start.15 = (bf16[1,2560]{1,0:T(2,128)(2,1)S(1)}, bf16[1,2560]{1,0:T(2,128)(2,1)}, u32[]{:S(2)}) copy-start(bf16[1,2560]{1,0:T(2,128)(2,1)} %param.22) | copy-start | bytes 15364
  14.1 2.6 copy-start.2
  14.2 3.1 %copy-start.10 = (bf16[2560,256]{1,0:T(8,128)(2,1)S(1)}, bf16[2560,256]{1,0:T(8,128)(2,1)}, u32[]{:S(2)}) copy-start(bf16[2560,256]{1,0:T(8,128)(2,1)} %param.25) | copy-start | bytes 3932164
  14.2 3.1 %copy-start.17 = (bf16[1,128,256]{2,1,0:T(8,128)(2,1)S(1)}, bf16[1,128,256]{2,1,0:T(8,128)(2,1)}, u32[]{:S(2)}) copy-start(bf16[1,128,256]{2,1,0:T(8,128)(2,1)} %param.23) | copy-start | bytes 196612
  15.9 4.9 %collective-permute-start = (f32[32,512]{1,0:T(8,128)S(1)}, f32[32,512]{1,0:T(8,128)S(1)}, u32[]{:S(2)}, u32[]{:S(2)}) collective-permute-start(f32[32,512]{1,0:T(8,128)S(1)} %select_reduce_fusion), channel_id=1, source_target_pairs={{0,1},{1,0},{2,3},{3,2},{4,5},{5,4},{6,7},{7,6},{8,9},{9,8},{10,11... | collective-permute-start | bytes 196616 | tf_op jit(solution)/shard_map/ppermute | solution.py:107
  17.3 2.0 copy-start.12
  20.8 5.4 %collective-permute-start.1 = (f32[32,512]{1,0:T(8,128)S(1)}, f32[32,512]{1,0:T(8,128)S(1)}, u32[]{:S(2)}, u32[]{:S(2)}) collective-permute-start(f32[32,512]{1,0:T(8,128)S(1)} %add.241), channel_id=1, source_target_pairs={{0,2},{1,3},{2,0},{3,1},{4,6},{5,7},{6,4},{7,5},{8,10},{9,11},{10,... | collective-permute-start | bytes 196616 | tf_op jit(solution)/shard_map/ppermute | solution.py:107
  24.5 127.9 %copy-start.6 = (f32[128,2048]{1,0:T(8,128)}, f32[128,2048]{1,0:T(8,128)S(1)}, u32[]{:S(2)}) copy-start(f32[128,2048]{1,0:T(8,128)S(1)} %get-tuple-element.99) | copy-start | bytes 3145732
  24.5 126.1 %copy-start.18 = (s32[16]{0:T(128)S(1)}, s32[16]{0:T(128)}, u32[]{:S(2)}) copy-start(s32[16]{0:T(128)} %param.32) | copy-start | bytes 196
  24.5 126.6 %copy-start.19 = (f32[16]{0:T(128)S(1)}, f32[16]{0:T(128)}, u32[]{:S(2)}) copy-start(f32[16]{0:T(128)} %param.33) | copy-start | bytes 196
  26.3 8.6 %collective-permute-start.2 = (f32[32,512]{1,0:T(8,128)S(1)}, f32[32,512]{1,0:T(8,128)S(1)}, u32[]{:S(2)}, u32[]{:S(2)}) collective-permute-start(f32[32,512]{1,0:T(8,128)S(1)} %add.242), channel_id=1, source_target_pairs={{0,4},{1,5},{2,6},{3,7},{4,0},{5,1},{6,2},{7,3},{8,12},{9,13},{10,... | collective-permute-start | bytes 196616 | tf_op jit(solution)/shard_map/ppermute | solution.py:107
  34.9 12.0 %collective-permute-start.3 = (f32[32,512]{1,0:T(8,128)S(1)}, f32[32,512]{1,0:T(8,128)S(1)}, u32[]{:S(2)}, u32[]{:S(2)}) collective-permute-start(f32[32,512]{1,0:T(8,128)S(1)} %add.243), channel_id=1, source_target_pairs={{0,8},{1,9},{2,10},{3,11},{4,12},{5,13},{6,14},{7,15},{8,0},{9,1},... | collective-permute-start | bytes 196616 | tf_op jit(solution)/shard_map/ppermute | solution.py:107
  197.5 2.7 copy-start.8
  199.8 1.0 copy-start.9
  205.4 13.8 %copy-start.7 = (f32[128,2048]{1,0:T(8,128)S(1)}, f32[128,2048]{1,0:T(8,128)}, u32[]{:S(2)}) copy-start(f32[128,2048]{1,0:T(8,128)} %copy-done.6) | copy-start | bytes 3145732
  223.5 1.2 copy-start.16
  229.5 1.6 copy-start.5
  231.2 2.2 collective-permute-start.4
  234.9 10.3 %collective-permute-start.5 = (bf16[2,2,168,256]{3,2,0,1:T(8,128)(2,1)S(1)}, bf16[2,2,168,256]{3,2,0,1:T(8,128)(2,1)S(1)}, u32[]{:S(2)}, u32[]{:S(2)}) collective-permute-start(bf16[2,2,168,256]{3,2,0,1:T(8,128)(2,1)S(1)} %fusion.43), channel_id=1, source_target_pairs={{0,2},{1,3},{2,0},{3,1},{4,6},{5,7},{6,4},{7,5},{8,10},{9,11},{10,... | collective-permute-start | bytes 1032200 | tf_op jit(solution)/shard_map/ppermute | solution.py:94
  235.8 30.8 %copy-start.3 = (bf16[1,128,2560]{2,1,0:T(8,128)(2,1)S(1)}, bf16[1,128,2560]{2,1,0:T(8,128)(2,1)}, u32[]{:S(2)}) copy-start(bf16[1,128,2560]{2,1,0:T(8,128)(2,1)} %param.20) | copy-start | bytes 1966084
  245.4 10.4 %collective-permute-start.6 = (bf16[2,168,256]{2,1,0:T(8,128)(2,1)S(1)}, bf16[2,168,256]{2,1,0:T(8,128)(2,1)S(1)}, u32[]{:S(2)}, u32[]{:S(2)}) collective-permute-start(bf16[2,168,256]{2,1,0:T(8,128)(2,1)S(1)} %fusion.46), channel_id=1, source_target_pairs={{0,4},{1,5},{2,6},{3,7},{4,0},{5,1},{6,2},{7,3},{8,12},{9,13},{10,... | collective-permute-start | bytes 516104 | tf_op jit(solution)/shard_map/ppermute | solution.py:94
  255.8 9.2 %collective-permute-start.7 = (bf16[168,256]{1,0:T(8,128)(2,1)S(1)}, bf16[168,256]{1,0:T(8,128)(2,1)S(1)}, u32[]{:S(2)}, u32[]{:S(2)}) collective-permute-start(bf16[168,256]{1,0:T(8,128)(2,1)S(1)} %fusion.48), channel_id=1, source_target_pairs={{0,8},{1,9},{2,10},{3,11},{4,12},{5,13},{6,14},{7,15},{8,0},{9,1},... | collective-permute-start | bytes 258056 | tf_op jit(solution)/shard_map/ppermute | solution.py:94
  265.0 4.8 %collective-permute-start.8 = (bf16[168,256]{1,0:T(8,128)(2,1)S(1)}, bf16[168,256]{1,0:T(8,128)(2,1)S(1)}, u32[]{:S(2)}, u32[]{:S(2)}) collective-permute-start(bf16[168,256]{1,0:T(8,128)(2,1)S(1)} %fusion.47), channel_id=1, source_target_pairs={{0,128},{128,0},{1,129},{129,1},{2,130},{130,2},{3,131},{131,3},{4... | collective-permute-start | bytes 258056 | tf_op jit(solution)/shard_map/ppermute | solution.py:110
  268.6 1.1 copy-start.4
  269.8 6.1 %collective-permute-start.9 = (bf16[168,256]{1,0:T(8,128)(2,1)S(1)}, bf16[168,256]{1,0:T(8,128)(2,1)S(1)}, u32[]{:S(2)}, u32[]{:S(2)}) collective-permute-start(bf16[168,256]{1,0:T(8,128)(2,1)S(1)} %add_convert_fusion.2), channel_id=1, source_target_pairs={{0,16},{16,0},{32,48},{48,32},{64,80},{80,64},{96,112},{112,96},{1... | collective-permute-start | bytes 258056 | tf_op jit(solution)/shard_map/ppermute | solution.py:110
  275.9 5.2 %collective-permute-start.10 = (bf16[168,256]{1,0:T(8,128)(2,1)S(1)}, bf16[168,256]{1,0:T(8,128)(2,1)S(1)}, u32[]{:S(2)}, u32[]{:S(2)}) collective-permute-start(bf16[168,256]{1,0:T(8,128)(2,1)S(1)} %add_convert_fusion.1), channel_id=1, source_target_pairs={{0,32},{16,48},{32,0},{48,16},{64,96},{80,112},{96,64},{112,80},{1... | collective-permute-start | bytes 258056 | tf_op jit(solution)/shard_map/ppermute | solution.py:110
  281.1 7.4 %copy-start.1 = (bf16[3088,512]{1,0:T(8,128)(2,1)S(1)}, bf16[3088,512]{1,0:T(8,128)(2,1)}, u32[]{:S(2)}) copy-start(bf16[3088,512]{1,0:T(8,128)(2,1)} %param.30) | copy-start | bytes 9486340
  281.2 6.1 %collective-permute-start.11 = (bf16[168,256]{1,0:T(8,128)(2,1)S(1)}, bf16[168,256]{1,0:T(8,128)(2,1)S(1)}, u32[]{:S(2)}, u32[]{:S(2)}) collective-permute-start(bf16[168,256]{1,0:T(8,128)(2,1)S(1)} %add_convert_fusion), channel_id=1, source_target_pairs={{0,64},{16,80},{32,96},{48,112},{64,0},{80,16},{96,32},{112,48},{1... | collective-permute-start | bytes 258056 | tf_op jit(solution)/shard_map/ppermute | solution.py:110
  (2 other events, 1.9 us)
Sparse Core Ops, SparseCore 0:
  9.9 140.6 all-gather.5
  152.4 41.0 all-gather.3
